TPU v7x, 32 devices: a whole 2x2x4 slice. The times are simulated.
32 devices in a mesh: dp: 8 (over z, x), mp: 4 (over y, core).
Axes of the slice: x: 2, y: 2, z: 4, core: 2. Of those that a mesh axis runs over, the one named last changes fastest.
Arguments:
- queries: bfloat16 [1024, 4, 8192], P('dp', None, 'mp'), may hold values from -6 to 6
- fresh_key_value: bfloat16 [1024, 4, 2, 8, 128], P('dp', None, None, 'mp'), may hold values from -6 to 6
- key_value_pool: bfloat16 [4096, 2, 8, 16, 128], P('dp', None, 'mp'), may hold values from -6 to 6
- block_position_map: int32 [4096], replicated, may hold values from 0 to 4095
- request_blocks: int32 [1024, 4], P('dp'), may hold values from 0 to 4095, as said below
- live_prefix_length: int32 [1024], P('dp'), may hold values from 1 to 64, as said below
- request_adapter: int32 [1024, 1], P('dp'), may hold values from 0 to 15; in each aligned block of 128 rows (0 to 127, 128 to 255, ...) at most 8 rows name the same one
- output_weight: bfloat16 [8192, 8192], P('mp'), may hold values from -0.0625 to 0.0625
- adapter_down_panels: bfloat16 [16, 64, 8192], P('dp', None, 'mp'), may hold values from -0.0625 to 0.0625
- adapter_up_panels: bfloat16 [16, 64, 8192], P('dp', None, 'mp'), may hold values from -0.75 to 0.75
Outputs:
- layer_out: bfloat16 [1024, 4, 8192], P('dp', None, 'mp')
Inputs may be any that keep to these rules, and one draw needn't show every extreme that they name: `request_blocks`: every logical block is given a distinct pool position. The 512 entries of one index of dp name 256 distinct blocks, each exactly twice. Through the owner map at most 64 distinct blocks of one index of dp, and so at most 128 of its entries, lie on one pool owner (pool positions owner * 512 to owner * 512 + 511); one pool owner holds exactly 64 distinct blocks of every index of dp. `live_prefix_length`: all requests of some index of dp have the full 4 * 16 prefix tokens. `request_adapter`: among the 128 requests of one index of dp no adapter appears more than 8 times, and that many is reached.
All inputs are finite; a program needn't handle non-finite values.
Results may differ from a plain program's by a relative error of at most 0.008.
Values may be sent and summed in bfloat16 or wider, within the bound.
No kernel may reach another device: no remote copies, remote signals or barrier semaphores. Data moves between devices by JAX's collectives and lax.ppermute only.
A program may use at most 192 MiB of HBM per device.

v0:
```python
import jax
import jax.numpy as jnp
from jax import lax
from jax.sharding import PartitionSpec as P

ADAPTER_SCALE = 2.0


def shards(
    queries,
    fresh_key_value,
    key_value_pool,
    block_position_map,
    request_blocks,
    live_prefix_length,
    request_adapter,
    output_weight,
    adapter_down_panels,
    adapter_up_panels,
):
    owners = lax.axis_size("dp")
    req_dev, step_count, query_width = queries.shape
    kv_heads = fresh_key_value.shape[3]
    head_dim = fresh_key_value.shape[4]
    pool_dev = key_value_pool.shape[0]
    block_len = key_value_pool.shape[3]
    blocks_per = request_blocks.shape[1]
    entries = req_dev * blocks_per
    out_width = output_weight.shape[1]
    owner_range = jnp.arange(owners)
    positions = jnp.take(block_position_map, request_blocks.reshape(entries))
    target = positions // pool_dev
    local_slot = positions % pool_dev
    capacity = 2 * entries // owners
    marks = (target[:, None] == owner_range[None, :]).astype(jnp.int32)
    counts = jnp.cumsum(marks, axis=0)
    slot_index = jnp.take_along_axis(counts, target[:, None], axis=1)[:, 0] - 1
    wish_table = jnp.zeros((owners, capacity), jnp.int32).at[target, slot_index].set(local_slot)
    wanted = lax.all_to_all(wish_table, "dp", split_axis=0, concat_axis=0, tiled=True)
    served = jnp.take(key_value_pool, wanted.reshape(-1), axis=0).reshape(
        (owners, capacity) + key_value_pool.shape[1:]
    )
    fetched = lax.all_to_all(served, "dp", split_axis=0, concat_axis=0, tiled=True)
    flat_rows = fetched.reshape((owners * capacity,) + key_value_pool.shape[1:])
    own_blocks = jnp.take(flat_rows, target * capacity + slot_index, axis=0)
    own_blocks = own_blocks.reshape((req_dev, blocks_per) + key_value_pool.shape[1:])
    group_size = query_width // (kv_heads * head_dim)
    query = queries.reshape(req_dev, step_count, kv_heads, group_size, head_dim)
    score_scale = head_dim ** (-0.5)
    prefix_scores = (
        jnp.einsum(
            "qsghd,qbgtd->qsghbt", query, own_blocks[:, :, 0], preferred_element_type=jnp.float32
        )
        * score_scale
    )
    token_index = jnp.arange(blocks_per)[:, None] * block_len + jnp.arange(block_len)[None, :]
    live_mask = token_index[None] < live_prefix_length[:, None, None]
    prefix_scores = jnp.where(live_mask[:, None, None, None], prefix_scores, -jnp.inf)
    fresh_scores = (
        jnp.einsum(
            "qsghd,qjgd->qsghj", query, fresh_key_value[:, :, 0], preferred_element_type=jnp.float32
        )
        * score_scale
    )
    causal = jnp.arange(step_count)[None, :] <= jnp.arange(step_count)[:, None]
    fresh_scores = jnp.where(causal[None, :, None, None, :], fresh_scores, -jnp.inf)
    row_top = jnp.maximum(jnp.max(prefix_scores, axis=(4, 5)), jnp.max(fresh_scores, axis=4))
    prefix_w = jnp.exp(prefix_scores - row_top[..., None, None])
    fresh_w = jnp.exp(fresh_scores - row_top[..., None])
    row_total = jnp.sum(prefix_w, axis=(4, 5)) + jnp.sum(fresh_w, axis=4)
    prefix_p = (prefix_w / row_total[..., None, None]).astype(jnp.bfloat16)
    fresh_p = (fresh_w / row_total[..., None]).astype(jnp.bfloat16)
    attended = jnp.einsum(
        "qsghbt,qbgtd->qsghd", prefix_p, own_blocks[:, :, 1], preferred_element_type=jnp.float32
    )
    attended = attended + jnp.einsum(
        "qsghj,qjgd->qsghd", fresh_p, fresh_key_value[:, :, 1], preferred_element_type=jnp.float32
    )
    attended = attended.astype(jnp.bfloat16).reshape(req_dev, step_count, query_width)
    base_product = jnp.dot(
        attended.reshape(req_dev * step_count, query_width),
        output_weight,
        preferred_element_type=jnp.float32,
    )
    base_product = base_product.reshape(req_dev, step_count, out_width)
    adapter = request_adapter[:, 0]
    single_panel = lax.all_gather(adapter_down_panels, "dp", axis=0, tiled=True)
    panel_count = single_panel.shape[0]
    hit_mask = (adapter[:, None] == jnp.arange(panel_count)[None, :]).astype(jnp.float32)
    every_rank = jnp.einsum(
        "qsf,nrf->qsnr", attended, single_panel, preferred_element_type=jnp.float32
    )
    rank_part = jnp.einsum("qsnr,qn->qsr", every_rank, hit_mask)
    rank_sum = lax.psum(rank_part, "mp").astype(jnp.bfloat16)
    single_panel = lax.all_gather(adapter_up_panels, "dp", axis=0, tiled=True)
    panel_count = single_panel.shape[0]
    hit_mask = (adapter[:, None] == jnp.arange(panel_count)[None, :]).astype(jnp.bfloat16)
    selected_panel = rank_sum[:, :, None, :] * hit_mask[:, None, :, None]
    adapter_sum = jnp.einsum(
        "utja,jam->utm", selected_panel, single_panel, preferred_element_type=jnp.float32
    )
    adapter_output = (adapter_sum * ADAPTER_SCALE).astype(jnp.bfloat16)
    summed_output = lax.psum_scatter(base_product, "mp", scatter_dimension=2, tiled=True)
    return (summed_output + adapter_output.astype(jnp.float32)).astype(jnp.bfloat16)


def solution(mesh):
    in_specs = (
        P("dp", None, "mp"),
        P("dp", None, None, "mp", None),
        P("dp", None, "mp", None, None),
        P(),
        P("dp", None),
        P("dp"),
        P("dp", None),
        P("mp", None),
        P("dp", None, "mp"),
        P("dp", None, "mp"),
    )
    out_specs = P("dp", None, "mp")
    return jax.shard_map(shards, mesh=mesh, in_specs=in_specs, out_specs=out_specs, check_vma=False)
```

profile of v0, /device:TPU:0, one launch (start us, length us, event | category | flops | bytes accessed | tf_op | source)
XLA Modules:
  0.0 782.9 jit_solution(12249667621752705040)
XLA Ops:
  8.6 3.1 gather_fusion
  13.4 3.5 gather_fusion.3
  17.0 22.1 %scatter_fusion = s32[8,128]{1,0:T(8,128)S(1)} fusion(s32[8,128]{1,0:T(8,128)S(1)} %broadcast_in_dim.88, s32[512]{0:T(512)S(1)} %bitcast.112, s32[512]{0:T(512)S(1)} %add_select_fusion), kind=kCustom, calls=%fused_computation.4 | custom fusion | bytes 10240 | tf_op jit(solution)/shard_map/scatter | solution.py:38
  39.1 13.5 %all_to_all.14 = s32[8,1,128]{2,1,0:T(1,128)S(1)} all-to-all(s32[8,1,128]{2,1,0:T(1,128)S(1)} %bitcast.110), channel_id=1, replica_groups=mesh['dp'=8,'mp'=4] {'dp'}, dimensions={0} | all-to-all | bytes 8192 | tf_op jit(solution)/shard_map/all_to_all | solution.py:39
  52.6 16.9 %gather_fusion.1 = bf16[1024,2,2,16,128]{4,3,2,1,0:T(8,128)(2,1)} fusion(bf16[512,2,2,16,128]{4,3,2,1,0:T(8,128)(2,1)} %param.12, s32[1024]{0:T(1024)S(1)} %broadcast_clamp_fusion), kind=kCustom, calls=%fused_computation.1 | custom fusion | bytes 33558528 | tf_op jit(solution)/shard_map/jit(_take)/gather | solution.py:40
  69.5 14.2 %broadcast_select_fusion = bf16[8,128,2,2,16,128]{5,4,3,2,1,0:T(8,128)(2,1)} fusion(bf16[8,128,2,2,16,128]{5,4,3,2,1,0:T(8,128)(2,1)} %bitcast.111, pred[8,128]{1,0:T(8,128)(4,1)S(1)} %compare_and_fusion), kind=kLoop, calls=%fused_computation.7 | loop fusion | flops 8388608 | bytes 33555456 | tf_op jit(solution)/shard_map/jit(_take)/select_n | solution.py:40
  83.7 5.9 all-to-all-start.1
  91.7 3.2 reshape.512
  95.3 10.8 %fusion.42 = (f32[128,4,2,8]{3,1,2,0:T(4,128)S(1)}, f32[128,4,2,8,4]{3,4,1,2,0:T(4,128)}) fusion(bf16[128,4,2,8,128]{4,3,2,1,0:T(8,128)(2,1)S(1)} %reshape.512, bf16[128,4,1,2,128]{4,3,2,1,0:T(2,128)(2,1)S(1)} %get-tuple-element.9, pred[4,4]{1,0:T(4,128)(4,1)S(1)} %iota_compare_fusion.2), kind=kOutput, calls=%fused_computation.114 | convolution fusion | flops 8478720 | bytes 2523152 | tf_op jit(solution)/shard_map/qsghd,qjgd->qsghj/dot_general | solution.py:60
  106.5 412.3 %all-to-all-done.1 = bf16[8,128,2,2,16,128]{5,4,3,2,1,0:T(8,128)(2,1)} async-done(((bf16[8,128,2,2,16,128]{5,4,3,2,1,0:T(8,128)(2,1)}), bf16[8,128,2,2,16,128]{5,4,3,2,1,0:T(8,128)(2,1)}, u32[]{:S(2)}, u32[]{:S(2)}) %all-to-all-start.1) | async-done | bytes 16777248 | tf_op jit(solution)/shard_map/all_to_all | solution.py:43
  518.7 26.2 %gather_fusion.2 = bf16[512,2,2,16,128]{4,3,2,1,0:T(8,128)(2,1)} fusion(bf16[1024,2,2,16,128]{4,3,2,1,0:T(8,128)(2,1)} %bitcast.17, s32[1024]{0:T(1024)S(1)} %pad_clamp_fusion), kind=kCustom, calls=%fused_computation.2 | custom fusion | bytes 16779264 | tf_op jit(solution)/shard_map/jit(_take)/gather | solution.py:45
  544.9 4.6 copy_select_fusion
  549.6 3.2 copy-done.2
  552.8 17.3 %fusion.2 = f32[128,2,4,16,4,8]{3,5,4,2,1,0:T(8,128)} fusion(bf16[128,4,2,2,16,128]{5,4,1,3,0,2:T(8,128)(2,1)S(1)} %copy_select_fusion, bf16[128,4,2,8,128]{4,3,2,1,0:T(8,128)(2,1)S(1)} %reshape.512), kind=kOutput, calls=%fused_computation.10 | convolution fusion | flops 134217728 | bytes 8388608 | tf_op jit(solution)/shard_map/qsghd,qbgtd->qsghbt/dot_general | solution.py:51
  570.1 12.6 %copy.108 = f32[128,2,4,16,4,8]{0,3,2,5,1,4:T(8,128)S(1)} copy(f32[128,2,4,16,4,8]{3,5,4,2,1,0:T(8,128)} %fusion.2) | data formatting | bytes 4194304 | tf_op jit(solution)/shard_map/qsghd,qbgtd->qsghbt/dot_general | solution.py:51
  583.3 3.6 fusion.22
  589.4 11.9 %copy.114 = bf16[128,4,2,8,4,16]{5,3,4,1,2,0:T(8,128)(2,1)} copy(bf16[128,4,2,8,4,16]{0,5,4,3,2,1:T(8,128)(2,1)S(1)} %divide_convert_fusion) | data formatting | bytes 2097152 | tf_op jit(solution)/shard_map/convert_element_type | solution.py:71
  601.3 7.0 fusion.3
  611.0 3.4 copy.117
  614.4 27.1 %fusion = f32[128,4,8192]{2,0,1:T(8,128)} fusion(bf16[128,4,2048]{0,2,1:T(8,128)(2,1)S(1)} %bitcast.115, bf16[2048,8192]{1,0:T(8,128)(2,1)} %param.17), kind=kOutput, calls=%fused_computation.5 | convolution fusion | flops 17179869184 | bytes 52428800 | tf_op jit(solution)/shard_map/dot_general | solution.py:80
  642.2 4.5 multiply_reduce_fusion
  646.7 11.7 %all-reduce.1 = bf16[128,4,64]{0,2,1:T(8,128)(2,1)S(1)} all-reduce(f32[128,4,64]{0,2,1:T(8,128)S(1)} %multiply_reduce_fusion), channel_id=1, replica_groups=mesh['dp'=8,'mp'=4] {'mp'}, use_global_device_ids=true, to_apply=%region_8.9 | all-reduce | flops 32768 | bytes 196608 | tf_op jit(solution)/shard_map/psum | solution.py:94
  658.5 107.9 %reduce-scatter.2.cloned.1.call-done = f32[128,4,2048]{2,0,1:T(8,128)} async-done(((f32[128,4,8192]{2,0,1:T(8,128)}), f32[128,4,2048]{2,0,1:T(8,128)}) %reduce-scatter.2.cloned.1.call-update) | async-done | bytes 4194320 | tf_op jit(solution)/shard_map/reduce_scatter | solution.py:103
  766.4 5.9 add_convert_fusion
  (78 shorter events, 14.9 us)
Async XLA Ops:
  7.4 1.3 copy-start
  83.7 7.8 copy-start.8
  83.7 435.1 %all-to-all-start.1 = ((bf16[8,128,2,2,16,128]{5,4,3,2,1,0:T(8,128)(2,1)}), bf16[8,128,2,2,16,128]{5,4,3,2,1,0:T(8,128)(2,1)}, u32[]{:S(2)}, u32[]{:S(2)}) async-start(bf16[8,128,2,2,16,128]{5,4,3,2,1,0:T(8,128)(2,1)} %broadcast_select_fusion), calls=%async_computation.1 | async-start | bytes 33554432 | tf_op jit(solution)/shard_map/all_to_all | solution.py:43
  89.6 552.6 %all-gather.3.cloned.1.call-start = ((), (), s32[]{:S(2)}) async-start(), calls=%async_computation.4 | async-start | bytes 4718592 | tf_op jit(solution)/shard_map/all_gather | solution.py:87
  90.3 568.2 %all-gather.5.cloned.1.call-start = ((), (), s32[]{:S(2)}) async-start(), calls=%async_computation.5 | async-start | bytes 4718592 | tf_op jit(solution)/shard_map/all_gather | solution.py:95
  91.1 675.4 %reduce-scatter.2.cloned.1.call-start = ((), (), s32[]{:S(2)}) async-start(), calls=%async_computation.3 | async-start | bytes 20971520 | tf_op jit(solution)/shard_map/reduce_scatter | solution.py:103
  91.7 3.2 copy-start.6
  95.3 11.1 %copy-start.10 = (s32[128]{0:T(128)S(1)}, s32[128]{0:T(128)}, u32[]{:S(2)}) copy-start(s32[128]{0:T(128)} %param.15) | copy-start | bytes 1540
  549.5 3.2 copy-start.2
  583.3 4.4 copy-start.4
  601.3 7.0 copy-start.3
  601.3 7.0 copy-start.5
  601.3 7.0 copy-start.7
  641.5 0.7 copy-start.9
  766.4 8.8 %copy-start.1 = (s32[4096]{0:T(1024)S(1)}, s32[4096]{0:T(1024)}, u32[]{:S(2)}) copy-start(s32[4096]{0:T(1024)} %param.13) | copy-start | bytes 49156
Sparse Core Ops, SparseCore 0:
  92.8 337.8 all-gather.2
  433.0 128.1 all-gather.4
Sparse Core Ops, SparseCore 1:
  641.7 124.7 reduce-scatter.1
where the time goes:
time: 791 us; the launch traced here: 783 us
  waiting for transfers between devices  522 us (66%)
  local copies, waits for them, and re-layouts  114 us (14%)
  matrix products  75.3 us (10%)
  other arithmetic  25.6 us (3%)
  blocking collectives  25.2 us (3%)
  between operations  15.5 us (2%)
    all_to_all x1, waiting for transfers between devices, shards(): lax.all_to_all(served, 'dp', split_axis=0, concat_axis=0, tiled=True)  412 us
    reduce_scatter x1, waiting for transfers between devices, shards(): lax.psum_scatter(base_product, 'mp', scatter_dimension=2, tiled=True)  108 us
    dot_general x1, matrix products, shards(): jnp.dot(attended.reshape(req_dev * step_count, query_width), output_weigh...  27.1 us
    gather x1, local copies, waits for them, and re-layouts, shards(): own_blocks = jnp.take(flat_rows, target * capacity + slot_index, axis=0)  26.2 us
    scatter x1, local copies, waits for them, and re-layouts, shards(): jnp.zeros((owners, capacity), jnp.int32).at[target, slot_index]  22.1 us
    dot_general x1, matrix products, shards(): jnp.einsum('qsghd,qbgtd->qsghbt', query, own_blocks[:, :, 0], preferred_e...  17.3 us
    gather x1, local copies, waits for them, and re-layouts, shards(): jnp.take(key_value_pool, wanted.reshape(-1), axis=0)  16.9 us
  transfers between devices with their start and end apart: 4, of which 2 were waited for; matrix products, arithmetic and copies ran while one was open for 18% of the time, Pallas kernels for 0%

commit v1 on v0

--- a/solution.py
+++ b/solution.py
@@ -31,11 +31,20 @@
     positions = jnp.take(block_position_map, request_blocks.reshape(entries))
     target = positions // pool_dev
     local_slot = positions % pool_dev
-    capacity = 2 * entries // owners
-    marks = (target[:, None] == owner_range[None, :]).astype(jnp.int32)
-    counts = jnp.cumsum(marks, axis=0)
-    slot_index = jnp.take_along_axis(counts, target[:, None], axis=1)[:, 0] - 1
-    wish_table = jnp.zeros((owners, capacity), jnp.int32).at[target, slot_index].set(local_slot)
+    capacity = entries // owners
+    entry_ids = jnp.arange(entries)
+    same_block = positions[:, None] == positions[None, :]
+    earlier = entry_ids[None, :] < entry_ids[:, None]
+    first = jnp.logical_not(jnp.any(same_block & earlier, axis=1))
+    same_owner = target[:, None] == target[None, :]
+    rank = jnp.sum((same_owner & earlier & first[None, :]).astype(jnp.int32), axis=1)
+    first_of = same_block & first[None, :]
+    slot_index = jnp.sum(jnp.where(first_of, rank[None, :], 0), axis=1)
+    key = jnp.where(first, target * capacity + rank, -1)
+    table_ids = jnp.arange(owners * capacity)
+    wish_table = jnp.sum(
+        jnp.where(key[:, None] == table_ids[None, :], local_slot[:, None], 0), axis=0
+    ).reshape(owners, capacity)
     wanted = lax.all_to_all(wish_table, "dp", split_axis=0, concat_axis=0, tiled=True)
     served = jnp.take(key_value_pool, wanted.reshape(-1), axis=0).reshape(
         (owners, capacity) + key_value_pool.shape[1:]

time: 791 us -> 592 us (0.75)
  waiting for transfers between devices: 522 us -> 342 us
  local copies, waits for them, and re-layouts: 114 us -> 102 us
    all_to_all x1, waiting for transfers between devices: 412 us -> 233 us  [shards(): lax.all_to_all(served, 'dp', split_axis=0, concat_axis=0, tiled=True)]
    scatter x1 -> x0, local copies, waits for them, and re-layouts: 22.1 us -> none  [shards(): jnp.zeros((owners, capacity), jnp.int32).at[target, slot_index]]
    convert_element_type x1, local copies, waits for them, and re-layouts: 11.9 us -> 22.9 us  [shards(): prefix_p = (prefix_w / row_total[..., None, None]).astype(jnp.bfloat16)]
  transfers between devices with their start and end apart: 4 -> 4, of which waited for: 2 -> 2; matrix products, arithmetic and copies ran while one was open for 18% -> 26% of each run, Pallas kernels for 0% -> 0%
where the time goes in v1:
time: 592 us; the launch traced here: 585 us
  waiting for transfers between devices  342 us (58%)
  local copies, waits for them, and re-layouts  102 us (17%)
  matrix products  75.1 us (13%)
  blocking collectives  25.2 us (4%)
  other arithmetic  19.7 us (3%)
  between operations  15.4 us (3%)
    all_to_all x1, waiting for transfers between devices, shards(): lax.all_to_all(served, 'dp', split_axis=0, concat_axis=0, tiled=True)  233 us
    reduce_scatter x1, waiting for transfers between devices, shards(): lax.psum_scatter(base_product, 'mp', scatter_dimension=2, tiled=True)  108 us
    dot_general x1, matrix products, shards(): jnp.dot(attended.reshape(req_dev * step_count, query_width), output_weigh...  27 us
    gather x1, local copies, waits for them, and re-layouts, shards(): own_blocks = jnp.take(flat_rows, target * capacity + slot_index, axis=0)  23.6 us
    gather x1, local copies, waits for them, and re-layouts, shards(): jnp.take(key_value_pool, wanted.reshape(-1), axis=0)  22.9 us
    convert_element_type x1, local copies, waits for them, and re-layouts, shards(): prefix_p = (prefix_w / row_total[..., None, None]).astype(jnp.bfloat16)  22.9 us
    dot_general x1, matrix products, shards(): jnp.einsum('qsghd,qbgtd->qsghbt', query, own_blocks[:, :, 0], preferred_e...  17.3 us
    all_to_all x1, blocking collectives, shards(): lax.all_to_all(wish_table, 'dp', split_axis=0, concat_axis=0, tiled=True)  13.5 us
  transfers between devices with their start and end apart: 4, of which 2 were waited for; matrix products, arithmetic and copies ran while one was open for 26% of the time, Pallas kernels for 0%

profile of v1, /device:TPU:0, one launch (start us, length us, event | category | flops | bytes accessed | tf_op | source)
XLA Modules:
  0.0 584.8 jit_solution(10500240088412221773)
XLA Ops:
  8.4 3.1 gather_fusion
  12.4 13.5 %all_to_all.14 = s32[8,1,64]{2,1,0:T(1,128)S(1)} all-to-all(s32[8,1,64]{2,1,0:T(1,128)S(1)} %all_to_all.9), channel_id=1, replica_groups=mesh['dp'=8,'mp'=4] {'dp'}, dimensions={0} | all-to-all | bytes 4096 | tf_op jit(solution)/shard_map/all_to_all | solution.py:48
  27.2 22.9 %gather_fusion.1 = bf16[512,2,2,16,128]{4,3,2,1,0:T(8,128)(2,1)} fusion(bf16[512,2,2,16,128]{4,3,2,1,0:T(8,128)(2,1)} %param.14, s32[1024]{0:T(1024)S(1)} %pad_clamp_fusion.1), kind=kCustom, calls=%fused_computation.clone | custom fusion | bytes 16779264 | tf_op jit(solution)/shard_map/jit(_take)/gather | solution.py:49
  50.1 7.6 %broadcast_select_fusion.1 = bf16[512,2,2,16,128]{4,3,2,1,0:T(8,128)(2,1)} fusion(bf16[512,2,2,16,128]{4,3,2,1,0:T(8,128)(2,1)} %gather_fusion.1, pred[512]{0:T(512)(128)(4,1)S(1)} %compare_and_fusion.3), kind=kLoop, calls=%fused_computation.6 | loop fusion | flops 4194304 | bytes 16777728 | tf_op jit(solution)/shard_map/jit(_take)/select_n | solution.py:49
  57.7 5.0 all-to-all-start.1
  64.4 3.2 reshape.275
  68.0 10.8 %fusion.37 = (f32[128,4,2,8]{3,1,2,0:T(4,128)S(1)}, f32[128,4,2,8,4]{3,4,1,2,0:T(4,128)}) fusion(bf16[128,4,2,8,128]{4,3,2,1,0:T(8,128)(2,1)S(1)} %reshape.275, bf16[128,4,1,2,128]{4,3,2,1,0:T(2,128)(2,1)S(1)} %get-tuple-element.13, pred[4,4]{1,0:T(4,128)(4,1)S(1)} %iota_compare_fusion.3), kind=kOutput, calls=%fused_computation.79 | convolution fusion | flops 8478720 | bytes 2523152 | tf_op jit(solution)/shard_map/qsghd,qjgd->qsghj/dot_general | solution.py:69
  79.5 232.6 %all-to-all-done.1 = bf16[8,64,2,2,16,128]{5,4,3,2,1,0:T(8,128)(2,1)} async-done(((bf16[8,64,2,2,16,128]{5,4,3,2,1,0:T(8,128)(2,1)}), bf16[8,64,2,2,16,128]{5,4,3,2,1,0:T(8,128)(2,1)}, u32[]{:S(2)}, u32[]{:S(2)}) %all-to-all-start.1) | async-done | bytes 8388640 | tf_op jit(solution)/shard_map/all_to_all | solution.py:52
  312.1 23.6 %gather_fusion.2 = bf16[512,2,2,16,128]{4,3,2,1,0:T(8,128)(2,1)} fusion(bf16[512,2,2,16,128]{4,3,2,1,0:T(8,128)(2,1)} %bitcast.3, s32[1024]{0:T(1024)S(1)} %pad_clamp_fusion), kind=kCustom, calls=%fused_computation.1.clone | custom fusion | bytes 16779264 | tf_op jit(solution)/shard_map/jit(_take)/gather | solution.py:54
  335.7 4.9 broadcast_select_fusion
  340.6 3.7 fusion.35
  344.3 17.3 %fusion.2 = f32[128,2,4,16,4,8]{3,5,4,2,1,0:T(8,128)} fusion(bf16[128,4,1,2,16,128]{5,4,3,2,1,0:T(8,128)(2,1)S(1)} %get-tuple-element.11, bf16[128,4,2,8,128]{4,3,2,1,0:T(8,128)(2,1)S(1)} %reshape.275), kind=kOutput, calls=%fused_computation.8 | convolution fusion | flops 134217728 | bytes 8388608 | tf_op jit(solution)/shard_map/qsghd,qbgtd->qsghbt/dot_general | solution.py:60
  361.6 12.2 %copy.92 = f32[128,2,4,16,4,8]{0,3,2,5,1,4:T(8,128)S(1)} copy(f32[128,2,4,16,4,8]{3,5,4,2,1,0:T(8,128)} %fusion.2) | data formatting | bytes 4194304 | tf_op jit(solution)/shard_map/qsghd,qbgtd->qsghbt/dot_general | solution.py:60
  374.5 3.6 fusion.22
  380.6 22.9 %copy.98 = bf16[128,4,2,8,4,16]{5,3,4,1,2,0:T(8,128)(2,1)} copy(bf16[128,4,2,8,4,16]{0,5,4,3,2,1:T(8,128)(2,1)S(1)} %divide_convert_fusion) | data formatting | bytes 2097152 | tf_op jit(solution)/shard_map/convert_element_type | solution.py:80
  403.5 7.0 %fusion.3 = f32[128,2,128,4,8,1]{2,4,5,3,1,0:T(8,128)S(1)} fusion(bf16[128,4,2,8,4,16]{5,3,4,1,2,0:T(8,128)(2,1)} %copy.98, bf16[128,4,1,2,16,128]{5,4,3,2,1,0:T(8,128)(2,1)} %get-tuple-element.10), kind=kOutput, calls=%fused_computation.10 | convolution fusion | flops 134217728 | bytes 9437184 | tf_op jit(solution)/shard_map/qsghbt,qbgtd->qsghd/dot_general | solution.py:82
  410.5 2.6 fusion.4
  413.1 3.4 copy.101
  416.6 27.0 %fusion = f32[128,4,8192]{2,0,1:T(8,128)} fusion(bf16[128,4,2048]{0,2,1:T(8,128)(2,1)S(1)} %bitcast.89, bf16[2048,8192]{1,0:T(8,128)(2,1)} %param.19), kind=kOutput, calls=%fused_computation.3 | convolution fusion | flops 17179869184 | bytes 52428800 | tf_op jit(solution)/shard_map/dot_general | solution.py:89
  444.2 4.5 multiply_reduce_fusion
  448.7 11.7 %all-reduce.1 = bf16[128,4,64]{0,2,1:T(8,128)(2,1)S(1)} all-reduce(f32[128,4,64]{0,2,1:T(8,128)S(1)} %multiply_reduce_fusion), channel_id=1, replica_groups=mesh['dp'=8,'mp'=4] {'mp'}, use_global_device_ids=true, to_apply=%region_9.11 | all-reduce | flops 32768 | bytes 196608 | tf_op jit(solution)/shard_map/psum | solution.py:103
  460.5 107.8 %reduce-scatter.2.cloned.1.call-done = f32[128,4,2048]{2,0,1:T(8,128)} async-done(((f32[128,4,8192]{2,0,1:T(8,128)}), f32[128,4,2048]{2,0,1:T(8,128)}) %reduce-scatter.2.cloned.1.call-update) | async-done | bytes 4194320 | tf_op jit(solution)/shard_map/reduce_scatter | solution.py:112
  568.3 5.9 %add_convert_fusion = bf16[128,4,2048]{2,0,1:T(8,128)(2,1)S(1)} fusion(f32[128,4,2048]{2,0,1:T(8,128)} %reduce-scatter.2.cloned.1.call-done, bf16[16,64,2048]{2,1,0:T(8,128)(2,1)} %all-gather.5.cloned.1.call-done, bf16[128,16]{0,1:T(8,128)(2,1)S(1)} %get-tuple-element.15, bf16[128,4,64]{0,2,1:T(8,128)(2,1)S(1)} %all-reduce.1), kind=kOutput, calls=%fused_computation.19 | convolution fusion | flops 2153250816 | bytes 10555392 | tf_op jit(solution)/shard_map/utja,jam->utm/dot_general | solution.py:108
  574.2 2.9 copy.104
  (62 shorter events, 9.7 us)
Async XLA Ops:
  7.4 1.0 copy-start
  57.7 254.4 %all-to-all-start.1 = ((bf16[8,64,2,2,16,128]{5,4,3,2,1,0:T(8,128)(2,1)}), bf16[8,64,2,2,16,128]{5,4,3,2,1,0:T(8,128)(2,1)}, u32[]{:S(2)}, u32[]{:S(2)}) async-start(bf16[8,64,2,2,16,128]{5,4,3,2,1,0:T(8,128)(2,1)} %bitcast.87), calls=%async_computation.1 | async-start | bytes 16777216 | tf_op jit(solution)/shard_map/all_to_all | solution.py:52
  62.7 381.5 %all-gather.3.cloned.1.call-start = ((), (), s32[]{:S(2)}) async-start(), calls=%async_computation.4 | async-start | bytes 4718592 | tf_op jit(solution)/shard_map/all_gather | solution.py:96
  63.4 397.0 %all-gather.5.cloned.1.call-start = ((), (), s32[]{:S(2)}) async-start(), calls=%async_computation.5 | async-start | bytes 4718592 | tf_op jit(solution)/shard_map/all_gather | solution.py:104
  64.2 3.4 copy-start.5
  64.2 504.1 %reduce-scatter.2.cloned.1.call-start = ((), (), s32[]{:S(2)}) async-start(), calls=%async_computation.3 | async-start | bytes 20971520 | tf_op jit(solution)/shard_map/reduce_scatter | solution.py:112
  68.0 11.5 %copy-start.8 = (s32[128]{0:T(128)S(1)}, s32[128]{0:T(128)}, u32[]{:S(2)}) copy-start(s32[128]{0:T(128)} %param.17) | copy-start | bytes 1540
  374.5 4.4 copy-start.3
  403.4 7.0 %copy-start.2 = (f32[128,4,2,8,4]{3,4,1,2,0:T(4,128)S(1)}, f32[128,4,2,8,4]{3,4,1,2,0:T(4,128)}, u32[]{:S(2)}) copy-start(f32[128,4,2,8,4]{3,4,1,2,0:T(4,128)} %get-tuple-element.17) | copy-start | bytes 393220
  403.4 7.0 %copy-start.4 = (f32[128,4,2,8]{3,1,2,0:T(4,128)S(1)}, f32[128,4,2,8]{3,1,2,0:T(4,128)}, u32[]{:S(2)}) copy-start(f32[128,4,2,8]{3,1,2,0:T(4,128)} %copy-done.3) | copy-start | bytes 98308
  403.5 7.0 %copy-start.6 = (f32[128,4,2,8]{3,1,2,0:T(4,128)S(1)}, f32[128,4,2,8]{3,1,2,0:T(4,128)}, u32[]{:S(2)}) copy-start(f32[128,4,2,8]{3,1,2,0:T(4,128)} %copy.99) | copy-start | bytes 98308
  443.5 0.7 copy-start.7
  568.3 8.8 %copy-start.1 = (s32[4096]{0:T(1024)S(1)}, s32[4096]{0:T(1024)}, u32[]{:S(2)}) copy-start(s32[4096]{0:T(1024)} %param.15) | copy-start | bytes 49156
Sparse Core Ops, SparseCore 0:
  65.9 202.7 all-gather.2
  271.0 83.5 all-gather.4
Sparse Core Ops, SparseCore 1:
  443.7 124.6 reduce-scatter.1

commit v2 on v1

--- a/solution.py
+++ b/solution.py
@@ -50,6 +50,9 @@
         (owners, capacity) + key_value_pool.shape[1:]
     )
     fetched = lax.all_to_all(served, "dp", split_axis=0, concat_axis=0, tiled=True)
+    fetched, adapter_down_panels, adapter_up_panels = lax.optimization_barrier(
+        (fetched, adapter_down_panels, adapter_up_panels)
+    )
     flat_rows = fetched.reshape((owners * capacity,) + key_value_pool.shape[1:])
     own_blocks = jnp.take(flat_rows, target * capacity + slot_index, axis=0)
     own_blocks = own_blocks.reshape((req_dev, blocks_per) + key_value_pool.shape[1:])
@@ -109,7 +112,9 @@
         "utja,jam->utm", selected_panel, single_panel, preferred_element_type=jnp.float32
     )
     adapter_output = (adapter_sum * ADAPTER_SCALE).astype(jnp.bfloat16)
-    summed_output = lax.psum_scatter(base_product, "mp", scatter_dimension=2, tiled=True)
+    summed_output = lax.psum_scatter(
+        base_product.astype(jnp.bfloat16), "mp", scatter_dimension=2, tiled=True
+    )
     return (summed_output + adapter_output.astype(jnp.float32)).astype(jnp.bfloat16)
 
 

time: 592 us -> 480 us (0.81)
  waiting for transfers between devices: 342 us -> 53.4 us
  blocking collectives: 25.2 us -> 211 us
    all_to_all x1 -> x0, waiting for transfers between devices: 233 us -> none  [shards(): lax.all_to_all(served, 'dp', split_axis=0, concat_axis=0, tiled=True)]
    all_to_all x0 -> x1, blocking collectives: none -> 185 us  [shards(): lax.all_to_all(served, 'dp', split_axis=0, concat_axis=0, tiled=True)]
    reduce_scatter x1, waiting for transfers between devices: 108 us -> 53.3 us  [shards(): lax.psum_scatter(base_product.astype(jnp.bfloat16), 'mp', scatter_dimensi...]
  transfers between devices with their start and end apart: 4 -> 3, of which waited for: 2 -> 1; matrix products, arithmetic and copies ran while one was open for 26% -> 32% of each run, Pallas kernels for 0% -> 0%
where the time goes in v2:
time: 480 us; the launch traced here: 473 us
  blocking collectives  211 us (44%)
  local copies, waits for them, and re-layouts  102 us (21%)
  matrix products  74.1 us (15%)
  waiting for transfers between devices  53.4 us (11%)
  other arithmetic  17.1 us (4%)
  between operations  15.4 us (3%)
    all_to_all x1, blocking collectives, shards(): lax.all_to_all(served, 'dp', split_axis=0, concat_axis=0, tiled=True)  185 us
    reduce_scatter x1, waiting for transfers between devices, shards(): lax.psum_scatter(base_product.astype(jnp.bfloat16), 'mp', scatter_dimensi...  53.3 us
    dot_general x1, matrix products, shards(): jnp.dot(attended.reshape(req_dev * step_count, query_width), output_weigh...  25.9 us
    gather x1, local copies, waits for them, and re-layouts, shards(): own_blocks = jnp.take(flat_rows, target * capacity + slot_index, axis=0)  23.3 us
    convert_element_type x1, local copies, waits for them, and re-layouts, shards(): prefix_p = (prefix_w / row_total[..., None, None]).astype(jnp.bfloat16)  22.9 us
    gather x1, local copies, waits for them, and re-layouts, shards(): jnp.take(key_value_pool, wanted.reshape(-1), axis=0)  22.9 us
    dot_general x1, matrix products, shards(): jnp.einsum('qsghd,qbgtd->qsghbt', query, own_blocks[:, :, 0], preferred_e...  17.3 us
    all_to_all x1, blocking collectives, shards(): lax.all_to_all(wish_table, 'dp', split_axis=0, concat_axis=0, tiled=True)  13.5 us
  transfers between devices with their start and end apart: 3, of which 1 were waited for; matrix products, arithmetic and copies ran while one was open for 32% of the time, Pallas kernels for 0%

profile of v2, /device:TPU:0, one launch (start us, length us, event | category | flops | bytes accessed | tf_op | source)
XLA Modules:
  0.0 472.8 jit_solution(5721286463096546662)
XLA Ops:
  8.4 3.1 gather_fusion
  12.4 13.5 %all_to_all.14 = s32[8,1,64]{2,1,0:T(1,128)S(1)} all-to-all(s32[8,1,64]{2,1,0:T(1,128)S(1)} %all_to_all.9), channel_id=1, replica_groups=mesh['dp'=8,'mp'=4] {'dp'}, dimensions={0} | all-to-all | bytes 4096 | tf_op jit(solution)/shard_map/all_to_all | solution.py:48
  27.2 22.9 %gather_fusion.1 = bf16[512,2,2,16,128]{4,3,2,1,0:T(8,128)(2,1)} fusion(bf16[512,2,2,16,128]{4,3,2,1,0:T(8,128)(2,1)} %param.14, s32[1024]{0:T(1024)S(1)} %pad_clamp_fusion.1), kind=kCustom, calls=%fused_computation.clone | custom fusion | bytes 16779264 | tf_op jit(solution)/shard_map/jit(_take)/gather | solution.py:49
  50.1 4.9 %broadcast_select_fusion.1 = bf16[512,2,2,16,128]{4,3,2,1,0:T(8,128)(2,1)S(1)} fusion(bf16[512,2,2,16,128]{4,3,2,1,0:T(8,128)(2,1)} %gather_fusion.1, pred[512]{0:T(512)(128)(4,1)S(1)} %compare_and_fusion.3), kind=kLoop, calls=%fused_computation.7 | loop fusion | flops 4194304 | bytes 16777728 | tf_op jit(solution)/shard_map/jit(_take)/select_n | solution.py:49
  55.0 185.4 %all_to_all.15 = bf16[8,64,2,2,16,128]{5,4,3,2,1,0:T(8,128)(2,1)} all-to-all(bf16[8,64,2,2,16,128]{5,4,3,2,1,0:T(8,128)(2,1)S(1)} %bitcast.90), channel_id=1, replica_groups=mesh['dp'=8,'mp'=4] {'dp'}, dimensions={0} | all-to-all | bytes 16777216 | tf_op jit(solution)/shard_map/all_to_all | solution.py:52
  240.7 3.2 reshape.275
  244.2 10.8 %fusion.40 = (f32[128,4,2,8]{3,1,2,0:T(4,128)S(1)}, f32[128,4,2,8,4]{3,4,1,2,0:T(4,128)}) fusion(bf16[128,4,2,8,128]{4,3,2,1,0:T(8,128)(2,1)S(1)} %reshape.275, bf16[128,4,1,2,128]{4,3,2,1,0:T(2,128)(2,1)S(1)} %get-tuple-element.19, pred[4,4]{1,0:T(4,128)(4,1)S(1)} %iota_compare_fusion.3), kind=kOutput, calls=%fused_computation.80 | convolution fusion | flops 8478720 | bytes 2523152 | tf_op jit(solution)/shard_map/qsghd,qjgd->qsghj/dot_general | solution.py:72
  255.8 23.3 %gather_fusion.2 = bf16[512,2,2,16,128]{4,3,2,1,0:T(8,128)(2,1)} fusion(bf16[512,2,2,16,128]{4,3,2,1,0:T(8,128)(2,1)} %bitcast.91, s32[1024]{0:T(1024)S(1)} %pad_clamp_fusion), kind=kCustom, calls=%fused_computation.1.clone | custom fusion | bytes 16779264 | tf_op jit(solution)/shard_map/jit(_take)/gather | solution.py:57
  279.1 4.9 %broadcast_select_fusion = bf16[512,2,2,16,128]{4,3,2,1,0:T(8,128)(2,1)S(1)} fusion(bf16[512,2,2,16,128]{4,3,2,1,0:T(8,128)(2,1)} %gather_fusion.2, pred[512]{0:T(512)(128)(4,1)S(1)} %get-tuple-element.12), kind=kLoop, calls=%fused_computation.6 | loop fusion | flops 4194304 | bytes 16777728 | tf_op jit(solution)/shard_map/jit(_take)/select_n | solution.py:57
  284.0 3.7 fusion.38
  287.8 17.3 %fusion.5 = f32[128,2,4,16,4,8]{3,5,4,2,1,0:T(8,128)} fusion(bf16[128,4,1,2,16,128]{5,4,3,2,1,0:T(8,128)(2,1)S(1)} %get-tuple-element.17, bf16[128,4,2,8,128]{4,3,2,1,0:T(8,128)(2,1)S(1)} %reshape.275), kind=kOutput, calls=%fused_computation.9 | convolution fusion | flops 134217728 | bytes 8388608 | tf_op jit(solution)/shard_map/qsghd,qbgtd->qsghbt/dot_general | solution.py:63
  305.1 12.2 %copy.92 = f32[128,2,4,16,4,8]{0,3,2,5,1,4:T(8,128)S(1)} copy(f32[128,2,4,16,4,8]{3,5,4,2,1,0:T(8,128)} %fusion.5) | data formatting | bytes 4194304 | tf_op jit(solution)/shard_map/qsghd,qbgtd->qsghbt/dot_general | solution.py:63
  318.0 3.6 fusion.25
  322.4 1.0 copy.99
  324.1 22.9 %copy.98 = bf16[128,4,2,8,4,16]{5,3,4,1,2,0:T(8,128)(2,1)} copy(bf16[128,4,2,8,4,16]{0,5,4,3,2,1:T(8,128)(2,1)S(1)} %divide_convert_fusion) | data formatting | bytes 2097152 | tf_op jit(solution)/shard_map/convert_element_type | solution.py:83
  347.0 7.6 %fusion.6 = f32[128,2,128,4,8,1]{2,4,5,3,1,0:T(8,128)S(1)} fusion(bf16[128,4,2,8,4,16]{5,3,4,1,2,0:T(8,128)(2,1)} %copy.98, bf16[128,4,1,2,16,128]{5,4,3,2,1,0:T(8,128)(2,1)} %get-tuple-element.16), kind=kOutput, calls=%fused_computation.11 | convolution fusion | flops 134217728 | bytes 9437184 | tf_op jit(solution)/shard_map/qsghbt,qbgtd->qsghd/dot_general | solution.py:85
  354.5 2.6 fusion.7
  357.2 3.4 copy.101
  360.6 25.9 %fusion.2 = bf16[128,4,8192]{2,0,1:T(8,128)(2,1)} fusion(bf16[128,4,2048]{0,2,1:T(8,128)(2,1)S(1)} %bitcast.92, bf16[2048,8192]{1,0:T(8,128)(2,1)} %param.19), kind=kOutput, calls=%fused_computation.5 | convolution fusion | flops 17184063488 | bytes 44040192 | tf_op jit(solution)/shard_map/dot_general | solution.py:92
  387.2 4.5 multiply_reduce_fusion
  391.7 11.7 %all-reduce.1 = bf16[128,4,64]{0,2,1:T(8,128)(2,1)S(1)} all-reduce(f32[128,4,64]{0,2,1:T(8,128)S(1)} %multiply_reduce_fusion), channel_id=1, replica_groups=mesh['dp'=8,'mp'=4] {'mp'}, use_global_device_ids=true, to_apply=%region_9.11 | all-reduce | flops 32768 | bytes 196608 | tf_op jit(solution)/shard_map/psum | solution.py:106
  403.5 53.3 %reduce-scatter.2.cloned.1.call-done = bf16[128,4,2048]{2,0,1:T(8,128)(2,1)} async-done(((bf16[128,4,8192]{2,0,1:T(8,128)(2,1)}), bf16[128,4,2048]{2,0,1:T(8,128)(2,1)}) %reduce-scatter.2.cloned.1.call-update) | async-done | bytes 2097168 | tf_op jit(solution)/shard_map/reduce_scatter | solution.py:115
  456.8 5.4 %add_convert_fusion = bf16[128,4,2048]{2,0,1:T(8,128)(2,1)S(1)} fusion(bf16[128,4,2048]{2,0,1:T(8,128)(2,1)} %reduce-scatter.2.cloned.1.call-done, bf16[16,64,2048]{2,1,0:T(8,128)(2,1)} %all-gather.5.cloned.1.call-done, bf16[128,16]{0,1:T(8,128)(2,1)S(1)} %get-tuple-element.21, bf16[128,4,64]{0,2,1:T(8,128)(2,1)S(1)} %all-reduce.1), kind=kOutput, calls=%fused_computation.20 | convolution fusion | flops 2154299392 | bytes 8458240 | tf_op jit(solution)/shard_map/utja,jam->utm/dot_general | solution.py:111
  462.2 2.9 copy.104
  (61 shorter events, 7.2 us)
Async XLA Ops:
  7.4 1.0 copy-start
  7.4 379.8 %all-gather.3.cloned.1.call-start = ((), (), s32[]{:S(2)}) async-start(), calls=%async_computation.4 | async-start | bytes 4718592 | tf_op jit(solution)/shard_map/all_gather | solution.py:99
  240.4 3.4 copy-start.5
  240.4 163.0 %all-gather.5.cloned.1.call-start = ((), (), s32[]{:S(2)}) async-start(), calls=%async_computation.5 | async-start | bytes 4718592 | tf_op jit(solution)/shard_map/all_gather | solution.py:107
  244.2 11.5 %copy-start.8 = (s32[128]{0:T(128)S(1)}, s32[128]{0:T(128)}, u32[]{:S(2)}) copy-start(s32[128]{0:T(128)} %param.17) | copy-start | bytes 1540
  317.3 139.5 %reduce-scatter.2.cloned.1.call-start = ((), (), s32[]{:S(2)}) async-start(), calls=%async_computation.3 | async-start | bytes 10485760 | tf_op jit(solution)/shard_map/reduce_scatter | solution.py:115
  318.0 4.4 copy-start.3
  347.0 7.6 %copy-start.2 = (f32[128,4,2,8,4]{3,4,1,2,0:T(4,128)S(1)}, f32[128,4,2,8,4]{3,4,1,2,0:T(4,128)}, u32[]{:S(2)}) copy-start(f32[128,4,2,8,4]{3,4,1,2,0:T(4,128)} %get-tuple-element.23) | copy-start | bytes 393220
  347.0 7.6 %copy-start.4 = (f32[128,4,2,8]{3,1,2,0:T(4,128)S(1)}, f32[128,4,2,8]{3,1,2,0:T(4,128)}, u32[]{:S(2)}) copy-start(f32[128,4,2,8]{3,1,2,0:T(4,128)} %copy-done.3) | copy-start | bytes 98308
  347.0 7.6 %copy-start.6 = (f32[128,4,2,8]{3,1,2,0:T(4,128)S(1)}, f32[128,4,2,8]{3,1,2,0:T(4,128)}, u32[]{:S(2)}) copy-start(f32[128,4,2,8]{3,1,2,0:T(4,128)} %copy.99) | copy-start | bytes 98308
  386.5 0.7 copy-start.7
  456.8 8.3 %copy-start.1 = (s32[4096]{0:T(1024)S(1)}, s32[4096]{0:T(1024)}, u32[]{:S(2)}) copy-start(s32[4096]{0:T(1024)} %param.15) | copy-start | bytes 49156
Sparse Core Ops, SparseCore 0:
  240.5 72.4 all-gather.2
  317.4 72.4 all-gather.4
Sparse Core Ops, SparseCore 1:
  386.6 70.1 reduce-scatter.1

commit v3 on v2

--- a/solution.py
+++ b/solution.py
@@ -2,8 +2,102 @@
 import jax.numpy as jnp
 from jax import lax
 from jax.sharding import PartitionSpec as P
+from jax.experimental import pallas as pl
+from jax.experimental.pallas import tpu as pltpu
 
 ADAPTER_SCALE = 2.0
+
+
+def attention_kernel(idx_ref, rows_ref, q_ref, f_ref, live_ref, out_ref, *, req_blk, blocks_per, token_cap, steps, group, scale):
+    i = pl.program_id(0)
+    kv_groups, q_rows, _ = q_ref.shape
+    cols = live_ref.shape[2]
+    prefix_cols = req_blk * token_cap
+    fresh_cols = req_blk * steps
+    row_id = lax.broadcasted_iota(jnp.int32, (q_rows, cols), 0)
+    col_id = lax.broadcasted_iota(jnp.int32, (q_rows, cols), 1)
+    row_req = row_id // (steps * group)
+    row_step = (row_id % (steps * group)) // group
+    fresh_id = col_id - prefix_cols
+    col_req = jnp.where(
+        col_id < prefix_cols,
+        col_id // token_cap,
+        jnp.where(fresh_id < fresh_cols, fresh_id // steps, -1),
+    )
+    step_ok = jnp.logical_or(col_id < prefix_cols, fresh_id % steps <= row_step)
+    mask = (col_req == row_req) & step_ok & (live_ref[0] > 0)
+    pad_rows = cols - prefix_cols - fresh_cols
+    for g in range(kv_groups):
+        keys = []
+        values = []
+        for r in range(req_blk):
+            for b in range(blocks_per):
+                row = idx_ref[(i * req_blk + r) * blocks_per + b]
+                keys.append(rows_ref[row, 0, g])
+                values.append(rows_ref[row, 1, g])
+        keys.append(f_ref[g, 0])
+        values.append(f_ref[g, 1])
+        if pad_rows:
+            keys.append(jnp.zeros((pad_rows, keys[0].shape[1]), keys[0].dtype))
+            values.append(jnp.zeros((pad_rows, values[0].shape[1]), values[0].dtype))
+        key_mat = jnp.concatenate(keys, axis=0)
+        value_mat = jnp.concatenate(values, axis=0)
+        scores = lax.dot_general(
+            q_ref[g], key_mat, (((1,), (1,)), ((), ())), preferred_element_type=jnp.float32
+        ) * scale
+        scores = jnp.where(mask, scores, -jnp.inf)
+        top = jnp.max(scores, axis=1, keepdims=True)
+        weights = jnp.exp(scores - top)
+        total = jnp.sum(weights, axis=1, keepdims=True)
+        probs = (weights / total).astype(jnp.bfloat16)
+        out_ref[g] = jnp.dot(probs, value_mat, preferred_element_type=jnp.float32).astype(out_ref.dtype)
+
+
+def attend(row_index, rows, queries, fresh_key_value, live_prefix_length, blocks_per, interpret=False):
+    req_dev, steps, _ = queries.shape
+    kv_groups = fresh_key_value.shape[3]
+    head_dim = fresh_key_value.shape[4]
+    block_len = rows.shape[3]
+    group = queries.shape[2] // (kv_groups * head_dim)
+    token_cap = blocks_per * block_len
+    req_blk = 4
+    q_rows = req_blk * steps * group
+    prefix_cols = req_blk * token_cap
+    fresh_cols = req_blk * steps
+    cols = -(-(prefix_cols + fresh_cols) // 128) * 128
+    q_t = queries.reshape(req_dev, steps, kv_groups, group, head_dim).transpose(2, 0, 1, 3, 4)
+    q_t = q_t.reshape(kv_groups, req_dev * steps * group, head_dim)
+    f_t = fresh_key_value.transpose(3, 2, 0, 1, 4).reshape(kv_groups, 2, req_dev * steps, head_dim)
+    live = (jnp.arange(token_cap)[None, :] < live_prefix_length[:, None]).astype(jnp.int32)
+    live = live.reshape(req_dev // req_blk, prefix_cols)
+    extra = jnp.concatenate(
+        [jnp.ones((fresh_cols,), jnp.int32), jnp.zeros((cols - prefix_cols - fresh_cols,), jnp.int32)]
+    )
+    live = jnp.concatenate([live, jnp.broadcast_to(extra, (req_dev // req_blk, extra.shape[0]))], axis=1)
+    live = live.reshape(req_dev // req_blk, 1, cols)
+    body = lambda *refs: attention_kernel(
+        *refs, req_blk=req_blk, blocks_per=blocks_per, token_cap=token_cap, steps=steps,
+        group=group, scale=head_dim ** (-0.5),
+    )
+    grid_spec = pltpu.PrefetchScalarGridSpec(
+        num_scalar_prefetch=1,
+        grid=(req_dev // req_blk,),
+        in_specs=[
+            pl.BlockSpec(rows.shape, lambda i, idx: (0, 0, 0, 0, 0)),
+            pl.BlockSpec((kv_groups, q_rows, head_dim), lambda i, idx: (0, i, 0)),
+            pl.BlockSpec((kv_groups, 2, fresh_cols, head_dim), lambda i, idx: (0, 0, i, 0)),
+            pl.BlockSpec((1, 1, cols), lambda i, idx: (i, 0, 0)),
+        ],
+        out_specs=pl.BlockSpec((kv_groups, q_rows, head_dim), lambda i, idx: (0, i, 0)),
+    )
+    out = pl.pallas_call(
+        body,
+        grid_spec=grid_spec,
+        out_shape=jax.ShapeDtypeStruct(q_t.shape, jnp.bfloat16),
+        interpret=interpret,
+    )(row_index, rows, q_t, f_t, live)
+    out = out.reshape(kv_groups, req_dev, steps, group, head_dim).transpose(1, 2, 0, 3, 4)
+    return out.reshape(req_dev, steps, kv_groups * group * head_dim)
 
 
 def shards(
@@ -54,41 +148,8 @@
         (fetched, adapter_down_panels, adapter_up_panels)
     )
     flat_rows = fetched.reshape((owners * capacity,) + key_value_pool.shape[1:])
-    own_blocks = jnp.take(flat_rows, target * capacity + slot_index, axis=0)
-    own_blocks = own_blocks.reshape((req_dev, blocks_per) + key_value_pool.shape[1:])
-    group_size = query_width // (kv_heads * head_dim)
-    query = queries.reshape(req_dev, step_count, kv_heads, group_size, head_dim)
-    score_scale = head_dim ** (-0.5)
-    prefix_scores = (
-        jnp.einsum(
-            "qsghd,qbgtd->qsghbt", query, own_blocks[:, :, 0], preferred_element_type=jnp.float32
-        )
-        * score_scale
-    )
-    token_index = jnp.arange(blocks_per)[:, None] * block_len + jnp.arange(block_len)[None, :]
-    live_mask = token_index[None] < live_prefix_length[:, None, None]
-    prefix_scores = jnp.where(live_mask[:, None, None, None], prefix_scores, -jnp.inf)
-    fresh_scores = (
-        jnp.einsum(
-            "qsghd,qjgd->qsghj", query, fresh_key_value[:, :, 0], preferred_element_type=jnp.float32
-        )
-        * score_scale
-    )
-    causal = jnp.arange(step_count)[None, :] <= jnp.arange(step_count)[:, None]
-    fresh_scores = jnp.where(causal[None, :, None, None, :], fresh_scores, -jnp.inf)
-    row_top = jnp.maximum(jnp.max(prefix_scores, axis=(4, 5)), jnp.max(fresh_scores, axis=4))
-    prefix_w = jnp.exp(prefix_scores - row_top[..., None, None])
-    fresh_w = jnp.exp(fresh_scores - row_top[..., None])
-    row_total = jnp.sum(prefix_w, axis=(4, 5)) + jnp.sum(fresh_w, axis=4)
-    prefix_p = (prefix_w / row_total[..., None, None]).astype(jnp.bfloat16)
-    fresh_p = (fresh_w / row_total[..., None]).astype(jnp.bfloat16)
-    attended = jnp.einsum(
-        "qsghbt,qbgtd->qsghd", prefix_p, own_blocks[:, :, 1], preferred_element_type=jnp.float32
-    )
-    attended = attended + jnp.einsum(
-        "qsghj,qjgd->qsghd", fresh_p, fresh_key_value[:, :, 1], preferred_element_type=jnp.float32
-    )
-    attended = attended.astype(jnp.bfloat16).reshape(req_dev, step_count, query_width)
+    row_index = jnp.clip(target * capacity + slot_index, 0, owners * capacity - 1)
+    attended = attend(row_index, flat_rows, queries, fresh_key_value, live_prefix_length, blocks_per)
     base_product = jnp.dot(
         attended.reshape(req_dev * step_count, query_width),
         output_weight,

time: 480 us -> 405 us (0.84); the launches traced: 473 us -> 404 us
  local copies, waits for them, and re-layouts: 102 us -> 44.7 us
  matrix products: 74.1 us -> 37.4 us
  Pallas kernels: 0 us -> 32.7 us
  other arithmetic: 17.1 us -> 6.97 us
    all_gather x1, waiting for transfers between devices: 0.02 us -> 54.8 us  [shards(): single_panel = lax.all_gather(adapter_up_panels, 'dp', axis=0, tiled=True)]
    reduce_scatter x1, waiting for transfers between devices: 53.3 us -> 0.01 us  [shards(): lax.psum_scatter(base_product.astype(jnp.bfloat16), 'mp', scatter_dimensi...]
    dot_general x4 -> x0, matrix products: 38.3 us -> none  [the longest x1 17.3 us: shards(): jnp.einsum('qsghd,qbgtd->qsghbt', query, own_blocks[:, :, 0], preferred_e...]
    pallas_call x0 -> x1, Pallas kernels: none -> 32.7 us  [attend(): pl.pallas_call(body, grid_spec=grid_spec, out_shape=jax.ShapeDtypeStruct(...]
    convert_element_type x2 -> x0, local copies, waits for them, and re-layouts: 26.3 us -> none  [the longest x1 22.9 us: shards(): prefix_p = (prefix_w / row_total[..., None, None]).astype(jnp.bfloat16)]
    gather x1 -> x0, local copies, waits for them, and re-layouts: 23.3 us -> none  [shards(): own_blocks = jnp.take(flat_rows, target * capacity + slot_index, axis=0)]
    dot_general x1 -> x2, local copies, waits for them, and re-layouts: 12.2 us -> 4.56 us  [shards(): jnp.dot(attended.reshape(req_dev * step_count, query_width), output_weigh...]
  transfers between devices with their start and end apart: 3 -> 3, of which waited for: 1 -> 1; matrix products, arithmetic and copies ran while one was open for 32% -> 11% of each run, Pallas kernels for 0% -> 8%
where the time goes in v3:
time: 405 us; the launch traced here: 404 us
  blocking collectives  211 us (52%)
  waiting for transfers between devices  55.6 us (14%)
  local copies, waits for them, and re-layouts  44.7 us (11%)
  matrix products  37.4 us (9%)
  Pallas kernels  32.7 us (8%)
  between operations  15 us (4%)
  other arithmetic  6.97 us (2%)
    all_to_all x1, blocking collectives, shards(): lax.all_to_all(served, 'dp', split_axis=0, concat_axis=0, tiled=True)  185 us
    all_gather x1, waiting for transfers between devices, shards(): single_panel = lax.all_gather(adapter_up_panels, 'dp', axis=0, tiled=True)  54.8 us
    pallas_call x1, Pallas kernels, attend(): pl.pallas_call(body, grid_spec=grid_spec, out_shape=jax.ShapeDtypeStruct(...  32.7 us
    dot_general x1, matrix products, shards(): jnp.dot(attended.reshape(req_dev * step_count, query_width), output_weigh...  26.1 us
    gather x1, local copies, waits for them, and re-layouts, shards(): jnp.take(key_value_pool, wanted.reshape(-1), axis=0)  22.9 us
    all_to_all x1, blocking collectives, shards(): lax.all_to_all(wish_table, 'dp', split_axis=0, concat_axis=0, tiled=True)  13.5 us
    psum x1, blocking collectives, shards(): rank_sum = lax.psum(rank_part, 'mp').astype(jnp.bfloat16)  12.1 us
  transfers between devices with their start and end apart: 3, of which 1 were waited for; matrix products, arithmetic and copies ran while one was open for 11% of the time, Pallas kernels for 8%

profile of v3, /device:TPU:0, one launch (start us, length us, event | category | flops | bytes accessed | tf_op | source)
XLA Modules:
  0.0 403.6 jit_solution(13619538211304349218)
XLA Ops:
  7.4 0.8 copy.27
  8.4 3.1 gather_fusion
  12.5 0.6 add_select_fusion.2
  13.4 13.5 %all_to_all.14 = s32[8,1,64]{2,1,0:T(1,128)S(1)} all-to-all(s32[8,1,64]{2,1,0:T(1,128)S(1)} %all_to_all.9), channel_id=1, replica_groups=mesh['dp'=8,'mp'=4] {'dp'}, dimensions={0} | all-to-all | bytes 4096 | tf_op jit(solution)/shard_map/all_to_all | solution.py:142
  27.4 0.7 reduce.5
  28.2 22.9 %gather_fusion.1 = bf16[512,2,2,16,128]{4,3,2,1,0:T(8,128)(2,1)} fusion(bf16[512,2,2,16,128]{4,3,2,1,0:T(8,128)(2,1)} %param.12, s32[1024]{0:T(1024)S(1)} %pad_clamp_fusion), kind=kCustom, calls=%fused_computation.1 | custom fusion | bytes 16779264 | tf_op jit(solution)/shard_map/jit(_take)/gather | solution.py:143
  51.1 4.5 %broadcast_select_fusion = bf16[8,64,2,2,16,128]{5,4,3,2,1,0:T(8,128)(2,1)S(1)} fusion(bf16[8,64,2,2,16,128]{5,4,3,2,1,0:T(8,128)(2,1)} %bitcast.55, pred[8,64]{1,0:T(8,128)(4,1)S(1)} %compare_and_fusion.2), kind=kLoop, calls=%fused_computation.5 | loop fusion | flops 4194304 | bytes 16777728 | tf_op jit(solution)/shard_map/jit(_take)/select_n | solution.py:143
  55.6 185.4 %all_to_all.15 = bf16[8,64,2,2,16,128]{5,4,3,2,1,0:T(8,128)(2,1)} all-to-all(bf16[8,64,2,2,16,128]{5,4,3,2,1,0:T(8,128)(2,1)S(1)} %broadcast_select_fusion), channel_id=1, replica_groups=mesh['dp'=8,'mp'=4] {'dp'}, dimensions={0} | all-to-all | bytes 16777216 | tf_op jit(solution)/shard_map/all_to_all | solution.py:146
  241.1 0.7 all-gather.5.cloned.1.call-update
  242.0 3.2 reshape.264
  245.2 1.7 copy.29
  246.9 1.0 copy.30
  248.3 0.6 reshape.267.refs_4_
  249.0 32.7 %shard_map.100 = bf16[2,4096,128]{2,1,0:T(8,128)(2,1)} custom-call(s32[512]{0:T(512)} %get-tuple-element.14.refs_0_, bf16[512,2,2,16,128]{4,3,2,1,0:T(8,128)(2,1)} %bitcast.54, bf16[2,4096,128]{2,1,0:T(8,128)(2,1)} %bitcast.56, bf16[2,2,512,128]{3,2,1,0:T(8,128)(2,1)} %bitcast.58, s32[32,1,384]{2,1,0:T(1,128)} %reshape.267.refs_4_), custom_call_target="tpu_custom_call" | custom-call | tf_op jit(solution)/shard_map/pallas_call | solution.py:93
  281.7 2.0 copy.31
  283.7 2.3 dot_general.14
  285.9 26.1 %fusion.2 = bf16[128,4,8192]{2,0,1:T(8,128)(2,1)} fusion(bf16[128,4,2048]{2,0,1:T(8,128)(2,1)} %dot_general.14, bf16[2048,8192]{1,0:T(8,128)(2,1)} %param.17), kind=kOutput, calls=%fused_computation.4 | convolution fusion | flops 17184063488 | bytes 44040192 | tf_op jit(solution)/shard_map/dot_general | solution.py:153
  312.1 0.6 copy-done.4
  312.7 2.3 reshape.286
  315.0 5.9 %multiply_reduce_fusion = f32[128,4,64]{0,2,1:T(8,128)S(1)} fusion(bf16[16,64,2048]{2,1,0:T(8,128)(2,1)} %all-gather.3.cloned.1.call-done, bf16[128,4,2048,1]{2,0,1,3:T(8,128)(2,1)} %reshape.286, f32[128,16]{0,1:T(8,128)S(1)} %get-tuple-element.15), kind=kOutput, calls=%fused_computation.14 | convolution fusion | flops 2148499456 | bytes 6430720 | tf_op jit(solution)/shard_map/qsf,nrf->qsnr/dot_general | solution.py:163
  320.9 12.1 %all-reduce.1 = bf16[128,4,64]{0,2,1:T(8,128)(2,1)S(1)} all-reduce(f32[128,4,64]{0,2,1:T(8,128)S(1)} %multiply_reduce_fusion), channel_id=1, replica_groups=mesh['dp'=8,'mp'=4] {'mp'}, use_global_device_ids=true, to_apply=%region_5.6 | all-reduce | flops 32768 | bytes 196608 | tf_op jit(solution)/shard_map/psum | solution.py:167
  333.0 54.8 %all-gather.5.cloned.1.call-done = bf16[16,64,2048]{2,1,0:T(8,128)(2,1)} async-done(((bf16[2,64,2048]{2,1,0:T(8,128)(2,1)}), bf16[16,64,2048]{2,1,0:T(8,128)(2,1)}) %all-gather.5.cloned.1.call-update) | async-done | bytes 4194320 | tf_op jit(solution)/shard_map/all_gather | solution.py:168
  387.8 5.4 %add_convert_fusion = bf16[128,4,2048]{2,0,1:T(8,128)(2,1)S(1)} fusion(bf16[128,4,2048]{2,0,1:T(8,128)(2,1)} %reduce-scatter.2.cloned.1.call-done, bf16[16,64,2048]{2,1,0:T(8,128)(2,1)} %all-gather.5.cloned.1.call-done, bf16[128,16]{0,1:T(8,128)(2,1)S(1)} %get-tuple-element.16, bf16[128,4,64]{0,2,1:T(8,128)(2,1)S(1)} %all-reduce.1), kind=kOutput, calls=%fused_computation.12 | convolution fusion | flops 2154299392 | bytes 8458240 | tf_op jit(solution)/shard_map/utja,jam->utm/dot_general | solution.py:172
  393.2 2.9 copy.32
  (44 shorter events, 2.8 us)
Async XLA Ops:
  7.4 1.0 copy-start
  7.4 307.6 %all-gather.3.cloned.1.call-start = ((), (), s32[]{:S(2)}) async-start(), calls=%async_computation.4 | async-start | bytes 4718592 | tf_op jit(solution)/shard_map/all_gather | solution.py:160
  241.0 146.8 %all-gather.5.cloned.1.call-start = ((), (), s32[]{:S(2)}) async-start(), calls=%async_computation.5 | async-start | bytes 4718592 | tf_op jit(solution)/shard_map/all_gather | solution.py:168
  241.8 5.1 %copy-start.2 = (bf16[128,4,2,2,128]{4,3,2,1,0:T(2,128)(2,1)S(1)}, bf16[128,4,2,2,128]{4,3,2,1,0:T(2,128)(2,1)}, u32[]{:S(2)}) copy-start(bf16[128,4,2,2,128]{4,3,2,1,0:T(2,128)(2,1)} %param.11) | copy-start | bytes 1572868
  241.8 6.1 %copy-start.3 = (s32[128]{0:T(128)S(1)}, s32[128]{0:T(128)}, u32[]{:S(2)}) copy-start(s32[128]{0:T(128)} %param.15) | copy-start | bytes 1540
  241.8 6.5 %copy-start.5 = (s32[128]{0:T(128)S(1)}, s32[128]{0:T(128)}, u32[]{:S(2)}) copy-start(s32[128]{0:T(128)} %constant.65.clone.1) | copy-start | bytes 1540
  241.8 146.0 %reduce-scatter.2.cloned.1.call-start = ((), (), s32[]{:S(2)}) async-start(), calls=%async_computation.3 | async-start | bytes 10485760 | tf_op jit(solution)/shard_map/reduce_scatter | solution.py:176
  312.1 0.7 copy-start.4
  387.8 8.3 %copy-start.1 = (s32[4096]{0:T(1024)S(1)}, s32[4096]{0:T(1024)}, u32[]{:S(2)}) copy-start(s32[4096]{0:T(1024)} %param.13) | copy-start | bytes 49156
Sparse Core Ops, SparseCore 0:
  241.1 72.7 all-gather.2
  316.3 71.4 all-gather.4
Sparse Core Ops, SparseCore 1:
  312.2 71.0 reduce-scatter.1

commit v4 on v3

--- a/solution.py
+++ b/solution.py
@@ -140,13 +140,11 @@
         jnp.where(key[:, None] == table_ids[None, :], local_slot[:, None], 0), axis=0
     ).reshape(owners, capacity)
     wanted = lax.all_to_all(wish_table, "dp", split_axis=0, concat_axis=0, tiled=True)
-    served = jnp.take(key_value_pool, wanted.reshape(-1), axis=0).reshape(
+    served = jnp.take(key_value_pool, wanted.reshape(-1), axis=0, mode="clip").reshape(
         (owners, capacity) + key_value_pool.shape[1:]
     )
     fetched = lax.all_to_all(served, "dp", split_axis=0, concat_axis=0, tiled=True)
-    fetched, adapter_down_panels, adapter_up_panels = lax.optimization_barrier(
-        (fetched, adapter_down_panels, adapter_up_panels)
-    )
+    fetched, adapter_up_panels = lax.optimization_barrier((fetched, adapter_up_panels))
     flat_rows = fetched.reshape((owners * capacity,) + key_value_pool.shape[1:])
     row_index = jnp.clip(target * capacity + slot_index, 0, owners * capacity - 1)
     attended = attend(row_index, flat_rows, queries, fresh_key_value, live_prefix_length, blocks_per)

time: 405 us -> 448 us (1.11)
  waiting for transfers between devices: 55.6 us -> 283 us
  blocking collectives: 211 us -> 25.2 us
  starting transfers between devices: 0.27 us -> 5.28 us
  other arithmetic: 6.97 us -> 2.43 us
    all_to_all x0 -> x1, waiting for transfers between devices: none -> 232 us  [shards(): lax.all_to_all(served, 'dp', split_axis=0, concat_axis=0, tiled=True)]
    all_to_all x1 -> x0, blocking collectives: 185 us -> none  [shards(): lax.all_to_all(served, 'dp', split_axis=0, concat_axis=0, tiled=True)]
    all_gather x1, waiting for transfers between devices: 54.8 us -> 0.02 us  [shards(): single_panel = lax.all_gather(adapter_up_panels, 'dp', axis=0, tiled=True)]
    reduce_scatter x1, waiting for transfers between devices: 0.01 us -> 50.6 us  [shards(): lax.psum_scatter(base_product.astype(jnp.bfloat16), 'mp', scatter_dimensi...]
    all_to_all x0 -> x1, starting transfers between devices: none -> 4.97 us  [shards(): lax.all_to_all(served, 'dp', split_axis=0, concat_axis=0, tiled=True)]
    select_n x2 -> x0, other arithmetic: 4.53 us -> none  [shards(): jnp.take(key_value_pool, wanted.reshape(-1), axis=0)]
  transfers between devices with their start and end apart: 3 -> 4, of which waited for: 1 -> 2; matrix products, arithmetic and copies ran while one was open for 11% -> 10% of each run, Pallas kernels for 8% -> 7%
where the time goes in v4:
time: 448 us; the launch traced here: 446 us
  waiting for transfers between devices  283 us (63%)
  local copies, waits for them, and re-layouts  44.7 us (10%)
  matrix products  37.4 us (8%)
  Pallas kernels  32.8 us (7%)
  blocking collectives  25.2 us (6%)
  between operations  15 us (3%)
  starting transfers between devices  5.28 us (1%)
    all_to_all x1, waiting for transfers between devices, shards(): lax.all_to_all(served, 'dp', split_axis=0, concat_axis=0, tiled=True)  232 us
    reduce_scatter x1, waiting for transfers between devices, shards(): lax.psum_scatter(base_product.astype(jnp.bfloat16), 'mp', scatter_dimensi...  50.6 us
    pallas_call x1, Pallas kernels, attend(): pl.pallas_call(body, grid_spec=grid_spec, out_shape=jax.ShapeDtypeStruct(...  32.8 us
    dot_general x1, matrix products, shards(): jnp.dot(attended.reshape(req_dev * step_count, query_width), output_weigh...  26.1 us
    gather x1, local copies, waits for them, and re-layouts, shards(): jnp.take(key_value_pool, wanted.reshape(-1), axis=0, mode='clip')  22.9 us
    all_to_all x1, blocking collectives, shards(): lax.all_to_all(wish_table, 'dp', split_axis=0, concat_axis=0, tiled=True)  13.5 us
    psum x1, blocking collectives, shards(): rank_sum = lax.psum(rank_part, 'mp').astype(jnp.bfloat16)  11.7 us
  transfers between devices with their start and end apart: 4, of which 2 were waited for; matrix products, arithmetic and copies ran while one was open for 10% of the time, Pallas kernels for 7%

profile of v4, /device:TPU:0, one launch (start us, length us, event | category | flops | bytes accessed | tf_op | source)
XLA Modules:
  0.0 445.9 jit_solution(16657080108679664790)
XLA Ops:
  7.4 0.8 copy.27
  8.4 3.1 gather_fusion
  12.5 0.6 add_select_fusion.2
  13.4 13.5 %all_to_all.14 = s32[8,1,64]{2,1,0:T(1,128)S(1)} all-to-all(s32[8,1,64]{2,1,0:T(1,128)S(1)} %all_to_all.9), channel_id=1, replica_groups=mesh['dp'=8,'mp'=4] {'dp'}, dimensions={0} | all-to-all | bytes 4096 | tf_op jit(solution)/shard_map/all_to_all | solution.py:142
  27.4 0.7 reduce.5
  28.2 22.9 %gather_fusion.1 = bf16[512,2,2,16,128]{4,3,2,1,0:T(8,128)(2,1)} fusion(bf16[512,2,2,16,128]{4,3,2,1,0:T(8,128)(2,1)} %param.12, s32[1024]{0:T(1024)S(1)} %pad_clamp_fusion), kind=kCustom, calls=%fused_computation.1 | custom fusion | bytes 16779264 | tf_op jit(solution)/shard_map/jit(_take)/gather | solution.py:143
  51.1 5.0 %all-to-all-start.1 = ((bf16[8,64,2,2,16,128]{5,4,3,2,1,0:T(8,128)(2,1)}), bf16[8,64,2,2,16,128]{5,4,3,2,1,0:T(8,128)(2,1)}, u32[]{:S(2)}, u32[]{:S(2)}) async-start(bf16[8,64,2,2,16,128]{5,4,3,2,1,0:T(8,128)(2,1)} %bitcast.52), calls=%async_computation.1 | async-start | bytes 16777216 | tf_op jit(solution)/shard_map/all_to_all | solution.py:146
  56.1 0.7 all-gather.3.cloned.1.call-update
  56.8 231.7 %all-to-all-done.1 = bf16[8,64,2,2,16,128]{5,4,3,2,1,0:T(8,128)(2,1)} async-done(((bf16[8,64,2,2,16,128]{5,4,3,2,1,0:T(8,128)(2,1)}), bf16[8,64,2,2,16,128]{5,4,3,2,1,0:T(8,128)(2,1)}, u32[]{:S(2)}, u32[]{:S(2)}) %all-to-all-start.1) | async-done | bytes 8388640 | tf_op jit(solution)/shard_map/all_to_all | solution.py:146
  288.8 3.2 reshape.224
  292.0 1.7 copy.29
  293.7 1.0 copy.30
  295.2 0.6 reshape.227.refs_4_
  295.8 32.8 %shard_map.100 = bf16[2,4096,128]{2,1,0:T(8,128)(2,1)} custom-call(s32[512]{0:T(512)} %get-tuple-element.12.refs_0_, bf16[512,2,2,16,128]{4,3,2,1,0:T(8,128)(2,1)} %bitcast.3.refs_1_, bf16[2,4096,128]{2,1,0:T(8,128)(2,1)} %bitcast.53, bf16[2,2,512,128]{3,2,1,0:T(8,128)(2,1)} %bitcast.55, s32[32,1,384]{2,1,0:T(1,128)} %reshape.227.refs_4_), custom_call_target="tpu_custom_call" | custom-call | tf_op jit(solution)/shard_map/pallas_call | solution.py:93
  328.6 2.0 copy.31
  330.5 2.3 dot_general.14
  332.8 26.1 %fusion.2 = bf16[128,4,8192]{2,0,1:T(8,128)(2,1)} fusion(bf16[128,4,2048]{2,0,1:T(8,128)(2,1)} %dot_general.14, bf16[2048,8192]{1,0:T(8,128)(2,1)} %param.17), kind=kOutput, calls=%fused_computation.4 | convolution fusion | flops 17184063488 | bytes 44040192 | tf_op jit(solution)/shard_map/dot_general | solution.py:151
  359.0 0.6 copy-done.4
  359.6 2.3 reshape.247
  361.9 5.9 %multiply_reduce_fusion = f32[128,4,64]{0,2,1:T(8,128)S(1)} fusion(bf16[16,64,2048]{2,1,0:T(8,128)(2,1)} %all-gather.3.cloned.1.call-done, bf16[128,4,2048,1]{2,0,1,3:T(8,128)(2,1)} %reshape.247, f32[128,16]{0,1:T(8,128)S(1)} %get-tuple-element.13), kind=kOutput, calls=%fused_computation.13 | convolution fusion | flops 2148499456 | bytes 6430720 | tf_op jit(solution)/shard_map/qsf,nrf->qsnr/dot_general | solution.py:161
  367.8 11.7 %all-reduce.1 = bf16[128,4,64]{0,2,1:T(8,128)(2,1)S(1)} all-reduce(f32[128,4,64]{0,2,1:T(8,128)S(1)} %multiply_reduce_fusion), channel_id=1, replica_groups=mesh['dp'=8,'mp'=4] {'mp'}, use_global_device_ids=true, to_apply=%region_5.6 | all-reduce | flops 32768 | bytes 196608 | tf_op jit(solution)/shard_map/psum | solution.py:165
  379.5 50.6 %reduce-scatter.2.cloned.1.call-done = bf16[128,4,2048]{2,0,1:T(8,128)(2,1)} async-done(((bf16[128,4,8192]{2,0,1:T(8,128)(2,1)}), bf16[128,4,2048]{2,0,1:T(8,128)(2,1)}) %reduce-scatter.2.cloned.1.call-update) | async-done | bytes 2097168 | tf_op jit(solution)/shard_map/reduce_scatter | solution.py:174
  430.1 5.4 %add_convert_fusion = bf16[128,4,2048]{2,0,1:T(8,128)(2,1)S(1)} fusion(bf16[128,4,2048]{2,0,1:T(8,128)(2,1)} %reduce-scatter.2.cloned.1.call-done, bf16[16,64,2048]{2,1,0:T(8,128)(2,1)} %all-gather.5.cloned.1.call-done, bf16[128,16]{0,1:T(8,128)(2,1)S(1)} %get-tuple-element.14, bf16[128,4,64]{0,2,1:T(8,128)(2,1)S(1)} %all-reduce.1), kind=kOutput, calls=%fused_computation.11 | convolution fusion | flops 2154299392 | bytes 8458240 | tf_op jit(solution)/shard_map/utja,jam->utm/dot_general | solution.py:170
  435.5 2.9 copy.32
  (42 shorter events, 2.8 us)
Async XLA Ops:
  7.4 1.0 copy-start
  51.1 237.5 %all-to-all-start.1 = ((bf16[8,64,2,2,16,128]{5,4,3,2,1,0:T(8,128)(2,1)}), bf16[8,64,2,2,16,128]{5,4,3,2,1,0:T(8,128)(2,1)}, u32[]{:S(2)}, u32[]{:S(2)}) async-start(bf16[8,64,2,2,16,128]{5,4,3,2,1,0:T(8,128)(2,1)} %bitcast.52), calls=%async_computation.1 | async-start | bytes 16777216 | tf_op jit(solution)/shard_map/all_to_all | solution.py:146
  56.0 305.8 %all-gather.3.cloned.1.call-start = ((), (), s32[]{:S(2)}) async-start(), calls=%async_computation.4 | async-start | bytes 4718592 | tf_op jit(solution)/shard_map/all_gather | solution.py:158
  56.8 322.7 %all-gather.5.cloned.1.call-start = ((), (), s32[]{:S(2)}) async-start(), calls=%async_computation.5 | async-start | bytes 4718592 | tf_op jit(solution)/shard_map/all_gather | solution.py:166
  288.6 5.1 %copy-start.2 = (bf16[128,4,2,2,128]{4,3,2,1,0:T(2,128)(2,1)S(1)}, bf16[128,4,2,2,128]{4,3,2,1,0:T(2,128)(2,1)}, u32[]{:S(2)}) copy-start(bf16[128,4,2,2,128]{4,3,2,1,0:T(2,128)(2,1)} %param.11) | copy-start | bytes 1572868
  288.6 6.1 %copy-start.3 = (s32[128]{0:T(128)S(1)}, s32[128]{0:T(128)}, u32[]{:S(2)}) copy-start(s32[128]{0:T(128)} %param.15) | copy-start | bytes 1540
  288.6 6.5 %copy-start.5 = (s32[128]{0:T(128)S(1)}, s32[128]{0:T(128)}, u32[]{:S(2)}) copy-start(s32[128]{0:T(128)} %constant.52.clone.1) | copy-start | bytes 1540
  288.6 141.5 %reduce-scatter.2.cloned.1.call-start = ((), (), s32[]{:S(2)}) async-start(), calls=%async_computation.3 | async-start | bytes 10485760 | tf_op jit(solution)/shard_map/reduce_scatter | solution.py:174
  358.9 0.7 copy-start.4
  430.1 8.3 %copy-start.1 = (s32[4096]{0:T(1024)S(1)}, s32[4096]{0:T(1024)}, u32[]{:S(2)}) copy-start(s32[4096]{0:T(1024)} %param.13) | copy-start | bytes 49156
Sparse Core Ops, SparseCore 0:
  59.2 202.7 all-gather.2
  288.7 72.3 all-gather.4
Sparse Core Ops, SparseCore 1:
  359.0 71.0 reduce-scatter.1

commit v5 on v4

--- a/solution.py
+++ b/solution.py
@@ -6,6 +6,7 @@
 from jax.experimental.pallas import tpu as pltpu
 
 ADAPTER_SCALE = 2.0
+ADAPTER_CAP = 8
 
 
 def attention_kernel(idx_ref, rows_ref, q_ref, f_ref, live_ref, out_ref, *, req_blk, blocks_per, token_cap, steps, group, scale):
@@ -144,7 +145,6 @@
         (owners, capacity) + key_value_pool.shape[1:]
     )
     fetched = lax.all_to_all(served, "dp", split_axis=0, concat_axis=0, tiled=True)
-    fetched, adapter_up_panels = lax.optimization_barrier((fetched, adapter_up_panels))
     flat_rows = fetched.reshape((owners * capacity,) + key_value_pool.shape[1:])
     row_index = jnp.clip(target * capacity + slot_index, 0, owners * capacity - 1)
     attended = attend(row_index, flat_rows, queries, fresh_key_value, live_prefix_length, blocks_per)
@@ -155,22 +155,35 @@
     )
     base_product = base_product.reshape(req_dev, step_count, out_width)
     adapter = request_adapter[:, 0]
-    single_panel = lax.all_gather(adapter_down_panels, "dp", axis=0, tiled=True)
-    panel_count = single_panel.shape[0]
-    hit_mask = (adapter[:, None] == jnp.arange(panel_count)[None, :]).astype(jnp.float32)
-    every_rank = jnp.einsum(
-        "qsf,nrf->qsnr", attended, single_panel, preferred_element_type=jnp.float32
-    )
-    rank_part = jnp.einsum("qsnr,qn->qsr", every_rank, hit_mask)
+    local_adapters, rank_dim, _ = adapter_down_panels.shape
+    slots = local_adapters * ADAPTER_CAP
+    request_ids = jnp.arange(req_dev)
+    same_adapter = adapter[:, None] == adapter[None, :]
+    before = request_ids[None, :] < request_ids[:, None]
+    repeat = jnp.sum((same_adapter & before).astype(jnp.int32), axis=1)
+    flat_slot = (adapter // local_adapters) * slots + (adapter % local_adapters) * ADAPTER_CAP + repeat
+    slot_ids = jnp.arange(owners * slots)
+    slot_owner = jnp.sum(
+        jnp.where(flat_slot[:, None] == slot_ids[None, :], request_ids[:, None], 0), axis=0
+    )
+    outgoing = jnp.take(attended, slot_owner, axis=0, mode="clip")
+    incoming = lax.all_to_all(
+        outgoing.reshape((owners, slots) + attended.shape[1:]), "dp", split_axis=0, concat_axis=0, tiled=True
+    )
+    incoming = incoming.reshape(owners, local_adapters, ADAPTER_CAP, step_count, -1)
+    rank_part = jnp.einsum(
+        "onksf,nrf->onksr", incoming, adapter_down_panels, preferred_element_type=jnp.float32
+    )
     rank_sum = lax.psum(rank_part, "mp").astype(jnp.bfloat16)
-    single_panel = lax.all_gather(adapter_up_panels, "dp", axis=0, tiled=True)
-    panel_count = single_panel.shape[0]
-    hit_mask = (adapter[:, None] == jnp.arange(panel_count)[None, :]).astype(jnp.bfloat16)
-    selected_panel = rank_sum[:, :, None, :] * hit_mask[:, None, :, None]
     adapter_sum = jnp.einsum(
-        "utja,jam->utm", selected_panel, single_panel, preferred_element_type=jnp.float32
-    )
-    adapter_output = (adapter_sum * ADAPTER_SCALE).astype(jnp.bfloat16)
+        "onksr,nrm->onksm", rank_sum, adapter_up_panels, preferred_element_type=jnp.float32
+    )
+    adapter_rows = (adapter_sum * ADAPTER_SCALE).astype(jnp.bfloat16)
+    returned = lax.all_to_all(
+        adapter_rows.reshape(owners, slots, step_count, -1), "dp", split_axis=0, concat_axis=0, tiled=True
+    )
+    returned = returned.reshape(owners * slots, step_count, -1)
+    adapter_output = jnp.take(returned, jnp.clip(flat_slot, 0, owners * slots - 1), axis=0, mode="clip")
     summed_output = lax.psum_scatter(
         base_product.astype(jnp.bfloat16), "mp", scatter_dimension=2, tiled=True
     )

time: 448 us -> 458 us (1.022)
  waiting for transfers between devices: 283 us -> 223 us
  blocking collectives: 25.2 us -> 81.8 us
  local copies, waits for them, and re-layouts: 44.7 us -> 59.4 us
  matrix products: 37.4 us -> 29.9 us
    all_to_all x1, waiting for transfers between devices: 232 us -> 175 us  [shards(): lax.all_to_all(served, 'dp', split_axis=0, concat_axis=0, tiled=True)]
    all_to_all x0 -> x1, blocking collectives: none -> 51.8 us  [shards(): lax.all_to_all(outgoing.reshape((owners, slots) + attended.shape[1:]), 'd...]
    reduce_scatter x1, waiting for transfers between devices: 50.6 us -> 0.02 us  [shards(): lax.psum_scatter(base_product.astype(jnp.bfloat16), 'mp', scatter_dimensi...]
    all_to_all x0 -> x1, waiting for transfers between devices: none -> 48.3 us  [shards(): lax.all_to_all(adapter_rows.reshape(owners, slots, step_count, -1), 'dp',...]
    dot_general x2, matrix products: 11.3 us -> 1.38 us  [the longest x1 0.69 us: shards(): jnp.einsum('onksf,nrf->onksr', incoming, adapter_down_panels, preferred_e...]
    gather x0 -> x2, local copies, waits for them, and re-layouts: none -> 7.45 us  [the longest x1 3.93 us: shards(): jnp.take(returned, jnp.clip(flat_slot, 0, owners * slots - 1), axis=0, mo...]
    psum x1, blocking collectives: 11.7 us -> 16.5 us  [shards(): rank_sum = lax.psum(rank_part, 'mp').astype(jnp.bfloat16)]
  transfers between devices with their start and end apart: 4 -> 3, of which waited for: 2 -> 2; matrix products, arithmetic and copies ran while one was open for 10% -> 5% of each run, Pallas kernels for 7% -> 0%
where the time goes in v5:
time: 458 us; the launch traced here: 456 us
  waiting for transfers between devices  223 us (49%)
  blocking collectives  81.8 us (18%)
  local copies, waits for them, and re-layouts  59.4 us (13%)
  Pallas kernels  32.7 us (7%)
  matrix products  29.9 us (7%)
  between operations  13.6 us (3%)
  starting transfers between devices  9.69 us (2%)
  other arithmetic  5.67 us (1%)
    all_to_all x1, waiting for transfers between devices, shards(): lax.all_to_all(served, 'dp', split_axis=0, concat_axis=0, tiled=True)  175 us
    all_to_all x1, blocking collectives, shards(): lax.all_to_all(outgoing.reshape((owners, slots) + attended.shape[1:]), 'd...  51.8 us
    all_to_all x1, waiting for transfers between devices, shards(): lax.all_to_all(adapter_rows.reshape(owners, slots, step_count, -1), 'dp',...  48.3 us
    pallas_call x1, Pallas kernels, attend(): pl.pallas_call(body, grid_spec=grid_spec, out_shape=jax.ShapeDtypeStruct(...  32.7 us
    dot_general x1, matrix products, shards(): jnp.dot(attended.reshape(req_dev * step_count, query_width), output_weigh...  28.5 us
    gather x1, local copies, waits for them, and re-layouts, shards(): jnp.take(key_value_pool, wanted.reshape(-1), axis=0, mode='clip')  22.9 us
    psum x1, blocking collectives, shards(): rank_sum = lax.psum(rank_part, 'mp').astype(jnp.bfloat16)  16.5 us
    all_to_all x1, blocking collectives, shards(): lax.all_to_all(wish_table, 'dp', split_axis=0, concat_axis=0, tiled=True)  13.5 us
  transfers between devices with their start and end apart: 3, of which 2 were waited for; matrix products, arithmetic and copies ran while one was open for 5% of the time, Pallas kernels for 0%

profile of v5, /device:TPU:0, one launch (start us, length us, event | category | flops | bytes accessed | tf_op | source)
XLA Modules:
  0.0 455.8 jit_solution(6932768627100449805)
XLA Ops:
  6.5 0.8 copy.36
  7.6 3.4 gather_fusion
  12.9 13.5 %all_to_all.24 = s32[8,1,64]{2,1,0:T(1,128)S(1)} all-to-all(s32[8,1,64]{2,1,0:T(1,128)S(1)} %all_to_all.15), channel_id=1, replica_groups=mesh['dp'=8,'mp'=4] {'dp'}, dimensions={0} | all-to-all | bytes 4096 | tf_op jit(solution)/shard_map/all_to_all | solution.py:143
  27.6 22.9 %gather_fusion.1 = bf16[512,2,2,16,128]{4,3,2,1,0:T(8,128)(2,1)} fusion(bf16[512,2,2,16,128]{4,3,2,1,0:T(8,128)(2,1)} %param.12, s32[1024]{0:T(1024)S(1)} %pad_clamp_fusion.2), kind=kCustom, calls=%fused_computation.1 | custom fusion | bytes 16779264 | tf_op jit(solution)/shard_map/jit(_take)/gather | solution.py:144
  50.5 5.0 %all-to-all-start.1 = ((bf16[8,64,2,2,16,128]{5,4,3,2,1,0:T(8,128)(2,1)}), bf16[8,64,2,2,16,128]{5,4,3,2,1,0:T(8,128)(2,1)}, u32[]{:S(2)}, u32[]{:S(2)}) async-start(bf16[8,64,2,2,16,128]{5,4,3,2,1,0:T(8,128)(2,1)} %bitcast.49), calls=%async_computation.1 | async-start | bytes 16777216 | tf_op jit(solution)/shard_map/all_to_all | solution.py:147
  55.7 3.2 reshape.216
  58.9 1.7 copy.38
  60.6 1.0 copy.39
  62.7 174.7 %all-to-all-done.1 = bf16[8,64,2,2,16,128]{5,4,3,2,1,0:T(8,128)(2,1)} async-done(((bf16[8,64,2,2,16,128]{5,4,3,2,1,0:T(8,128)(2,1)}), bf16[8,64,2,2,16,128]{5,4,3,2,1,0:T(8,128)(2,1)}, u32[]{:S(2)}, u32[]{:S(2)}) %all-to-all-start.1) | async-done | bytes 8388640 | tf_op jit(solution)/shard_map/all_to_all | solution.py:147
  237.4 32.7 %shard_map.100 = bf16[2,4096,128]{2,1,0:T(8,128)(2,1)} custom-call(s32[512]{0:T(512)} %get-tuple-element.10.refs_0_, bf16[512,2,2,16,128]{4,3,2,1,0:T(8,128)(2,1)} %bitcast.2.refs_1_, bf16[2,4096,128]{2,1,0:T(8,128)(2,1)} %bitcast.53, bf16[2,2,512,128]{3,2,1,0:T(8,128)(2,1)} %bitcast.55, s32[32,1,384]{2,1,0:T(1,128)} %reshape.219.refs_4_), custom_call_target="tpu_custom_call" | custom-call | tf_op jit(solution)/shard_map/pallas_call | solution.py:94
  270.2 3.5 copy.40
  273.7 2.5 dot_general.11
  276.2 28.5 %fusion.2 = bf16[128,4,8192]{2,0,1:T(8,128)(2,1)} fusion(bf16[2048,8192]{1,0:T(8,128)(2,1)} %param.17, bf16[128,4,2048]{2,1,0:T(4,128)(2,1)S(1)} %dot_general.11), kind=kOutput, calls=%fused_computation.6 | convolution fusion | flops 17184063488 | bytes 44040192 | tf_op jit(solution)/shard_map/dot_general | solution.py:151
  305.7 3.5 gather_fusion.2
  309.2 2.9 copy.42
  312.1 51.8 %all_to_all.25 = bf16[8,16,4,2048]{3,1,2,0:T(8,128)(2,1)S(1)} all-to-all(bf16[8,16,4,2048]{3,1,2,0:T(8,128)(2,1)S(1)} %copy.42), channel_id=1, replica_groups=mesh['dp'=8,'mp'=4] {'dp'}, dimensions={0} | all-to-all | bytes 4194304 | tf_op jit(solution)/shard_map/all_to_all | solution.py:170
  364.7 16.5 %all-reduce.1 = bf16[8,2,8,4,64]{4,3,2,0,1:T(4,128)(2,1)S(1)} all-reduce(f32[8,2,8,4,64]{4,3,2,0,1:T(4,128)S(1)} %bitcast.56), channel_id=1, replica_groups=mesh['dp'=8,'mp'=4] {'mp'}, use_global_device_ids=true, to_apply=%region_7.8 | all-reduce | flops 32768 | bytes 196608 | tf_op jit(solution)/shard_map/psum | solution.py:177
  381.9 1.5 copy.63
  383.4 4.5 all-to-all-start.3
  387.9 48.3 %all-to-all-done.3 = bf16[8,16,4,2048]{3,1,2,0:T(8,128)(2,1)S(1)} async-done(((bf16[8,16,4,2048]{3,1,2,0:T(8,128)(2,1)}), bf16[8,16,4,2048]{3,1,2,0:T(8,128)(2,1)S(1)}, u32[]{:S(2)}, u32[]{:S(2)}) %all-to-all-start.3) | async-done | bytes 2097184 | tf_op jit(solution)/shard_map/all_to_all | solution.py:182
  436.1 3.0 copy.46
  439.1 3.9 gather_fusion.3
  443.1 2.9 add_convert_fusion
  446.0 2.9 copy.48
  (49 shorter events, 7.0 us)
Async XLA Ops:
  6.5 374.7 %copy-start = (bf16[2,64,2048]{2,1,0:T(8,128)(2,1)S(1)}, bf16[2,64,2048]{2,1,0:T(8,128)(2,1)}, u32[]{:S(2)}) copy-start(bf16[2,64,2048]{2,1,0:T(8,128)(2,1)} %param.19) | copy-start | bytes 1572868
  50.5 186.9 %all-to-all-start.1 = ((bf16[8,64,2,2,16,128]{5,4,3,2,1,0:T(8,128)(2,1)}), bf16[8,64,2,2,16,128]{5,4,3,2,1,0:T(8,128)(2,1)}, u32[]{:S(2)}, u32[]{:S(2)}) async-start(bf16[8,64,2,2,16,128]{5,4,3,2,1,0:T(8,128)(2,1)} %bitcast.49), calls=%async_computation.1 | async-start | bytes 16777216 | tf_op jit(solution)/shard_map/all_to_all | solution.py:147
  55.5 387.5 %reduce-scatter.2.cloned.1.call-start = ((), (), s32[]{:S(2)}) async-start(), calls=%async_computation.5 | async-start | bytes 10485760 | tf_op jit(solution)/shard_map/reduce_scatter | solution.py:187
  58.9 1.7 copy-start.1
  58.9 2.7 copy-start.2
  58.9 3.1 copy-start.4
  304.7 0.7 copy-start.3
  312.1 51.9 %copy-start.5 = (bf16[2,64,2048]{2,1,0:T(8,128)(2,1)S(1)}, bf16[2,64,2048]{2,1,0:T(8,128)(2,1)}, u32[]{:S(2)}) copy-start(bf16[2,64,2048]{2,1,0:T(8,128)(2,1)} %param.18) | copy-start | bytes 1572868
  383.4 52.8 %all-to-all-start.3 = ((bf16[8,16,4,2048]{3,1,2,0:T(8,128)(2,1)}), bf16[8,16,4,2048]{3,1,2,0:T(8,128)(2,1)S(1)}, u32[]{:S(2)}, u32[]{:S(2)}) async-start(bf16[8,16,4,2048]{3,1,2,0:T(8,128)(2,1)} %bitcast.50), calls=%async_computation.4 | async-start | bytes 4194304 | tf_op jit(solution)/shard_map/all_to_all | solution.py:182
Sparse Core Ops, SparseCore 0:
  304.9 73.1 reduce-scatter.1

commit v6 on v3

--- a/solution.py
+++ b/solution.py
@@ -6,6 +6,47 @@
 from jax.experimental.pallas import tpu as pltpu
 
 ADAPTER_SCALE = 2.0
+
+
+def gather_rows_kernel(idx_ref, src_ref, dst_ref, sems):
+    count = dst_ref.shape[0]
+    depth = sems.shape[0]
+
+    def copy(j):
+        return pltpu.make_async_copy(src_ref.at[idx_ref[j]], dst_ref.at[j], sems.at[j % depth])
+
+    def issue(j, carry):
+        @pl.when(j >= depth)
+        def _():
+            copy(j - depth).wait()
+
+        copy(j).start()
+        return carry
+
+    def drain(j, carry):
+        copy(j).wait()
+        return carry
+
+    lax.fori_loop(0, count, issue, 0)
+    lax.fori_loop(count - depth, count, drain, 0)
+
+
+def gather_rows(table, index, interpret=False):
+    count = index.shape[0]
+    depth = min(16, count)
+    grid_spec = pltpu.PrefetchScalarGridSpec(
+        num_scalar_prefetch=1,
+        grid=(1,),
+        in_specs=[pl.BlockSpec(memory_space=pl.ANY)],
+        out_specs=pl.BlockSpec(memory_space=pl.ANY),
+        scratch_shapes=[pltpu.SemaphoreType.DMA((depth,))],
+    )
+    return pl.pallas_call(
+        gather_rows_kernel,
+        grid_spec=grid_spec,
+        out_shape=jax.ShapeDtypeStruct((count,) + table.shape[1:], table.dtype),
+        interpret=interpret,
+    )(index, table)
 
 
 def attention_kernel(idx_ref, rows_ref, q_ref, f_ref, live_ref, out_ref, *, req_blk, blocks_per, token_cap, steps, group, scale):
@@ -140,7 +181,7 @@
         jnp.where(key[:, None] == table_ids[None, :], local_slot[:, None], 0), axis=0
     ).reshape(owners, capacity)
     wanted = lax.all_to_all(wish_table, "dp", split_axis=0, concat_axis=0, tiled=True)
-    served = jnp.take(key_value_pool, wanted.reshape(-1), axis=0).reshape(
+    served = gather_rows(key_value_pool, jnp.clip(wanted.reshape(-1), 0, pool_dev - 1)).reshape(
         (owners, capacity) + key_value_pool.shape[1:]
     )
     fetched = lax.all_to_all(served, "dp", split_axis=0, concat_axis=0, tiled=True)

time: 405 us -> 635 us (1.57)
  Pallas kernels: 32.7 us -> 289 us
  local copies, waits for them, and re-layouts: 44.7 us -> 21.9 us
    pallas_call x0 -> x1, Pallas kernels: none -> 256 us  [gather_rows(): pl.pallas_call(gather_rows_kernel, grid_spec=grid_spec, out_shape=jax.Sha...]
    gather x1 -> x0, local copies, waits for them, and re-layouts: 22.9 us -> none  [shards(): jnp.take(key_value_pool, wanted.reshape(-1), axis=0)]
  transfers between devices with their start and end apart: 3 -> 3, of which waited for: 1 -> 1; matrix products, arithmetic and copies ran while one was open for 11% -> 7% of each run, Pallas kernels for 8% -> 5%
where the time goes in v6:
time: 635 us; the launch traced here: 634 us
  Pallas kernels  289 us (46%)
  blocking collectives  213 us (34%)
  waiting for transfers between devices  55.7 us (9%)
  matrix products  37.4 us (6%)
  local copies, waits for them, and re-layouts  21.9 us (3%)
  between operations  15 us (2%)
    pallas_call x1, Pallas kernels, gather_rows(): pl.pallas_call(gather_rows_kernel, grid_spec=grid_spec, out_shape=jax.Sha...  256 us
    all_to_all x1, blocking collectives, shards(): lax.all_to_all(served, 'dp', split_axis=0, concat_axis=0, tiled=True)  188 us
    all_gather x1, waiting for transfers between devices, shards(): single_panel = lax.all_gather(adapter_up_panels, 'dp', axis=0, tiled=True)  54.9 us
    pallas_call x1, Pallas kernels, attend(): pl.pallas_call(body, grid_spec=grid_spec, out_shape=jax.ShapeDtypeStruct(...  32.7 us
    dot_general x1, matrix products, shards(): jnp.dot(attended.reshape(req_dev * step_count, query_width), output_weigh...  26.1 us
    all_to_all x1, blocking collectives, shards(): lax.all_to_all(wish_table, 'dp', split_axis=0, concat_axis=0, tiled=True)  13.5 us
  transfers between devices with their start and end apart: 3, of which 1 were waited for; matrix products, arithmetic and copies ran while one was open for 7% of the time, Pallas kernels for 5%

profile of v6, /device:TPU:0, one launch (start us, length us, event | category | flops | bytes accessed | tf_op | source)
XLA Modules:
  0.0 633.8 jit_solution(17729579716597500496)
XLA Ops:
  7.4 0.8 copy.27
  8.4 3.1 gather_fusion
  12.1 0.4 select_reduce_fusion.1
  12.5 0.6 add_select_fusion.2
  13.4 13.5 %all_to_all.14 = s32[8,1,64]{2,1,0:T(1,128)S(1)} all-to-all(s32[8,1,64]{2,1,0:T(1,128)S(1)} %all_to_all.9), channel_id=1, replica_groups=mesh['dp'=8,'mp'=4] {'dp'}, dimensions={0} | all-to-all | bytes 4096 | tf_op jit(solution)/shard_map/all_to_all | solution.py:183
  26.9 0.7 min.14.idx_ref
  27.6 256.1 %shard_map.100 = bf16[512,2,2,16,128]{4,3,2,1,0:T(8,128)(2,1)} custom-call(s32[512]{0:T(512)} %min.14.idx_ref, bf16[512,2,2,16,128]{4,3,2,1,0:T(8,128)(2,1)} %src_ref.1), custom_call_target="tpu_custom_call" | custom-call | tf_op jit(solution)/shard_map/pallas_call | solution.py:44
  283.7 187.6 %all_to_all.15 = bf16[8,64,2,2,16,128]{5,4,3,2,1,0:T(8,128)(2,1)} all-to-all(bf16[8,64,2,2,16,128]{5,4,3,2,1,0:T(8,128)(2,1)} %bitcast.53), channel_id=1, replica_groups=mesh['dp'=8,'mp'=4] {'dp'}, dimensions={0} | all-to-all | bytes 16777216 | tf_op jit(solution)/shard_map/all_to_all | solution.py:187
  471.4 0.7 all-gather.5.cloned.1.call-update
  472.2 3.2 reshape.226
  475.4 1.7 copy.29
  477.1 1.0 copy.30
  478.5 0.6 reshape.229.refs_4_
  479.1 32.7 %shard_map.101 = bf16[2,4096,128]{2,1,0:T(8,128)(2,1)} custom-call(s32[512]{0:T(512)} %get-tuple-element.14.refs_0_, bf16[512,2,2,16,128]{4,3,2,1,0:T(8,128)(2,1)} %bitcast.52, bf16[2,4096,128]{2,1,0:T(8,128)(2,1)} %bitcast.54, bf16[2,2,512,128]{3,2,1,0:T(8,128)(2,1)} %bitcast.56, s32[32,1,384]{2,1,0:T(1,128)} %reshape.229.refs_4_), custom_call_target="tpu_custom_call" | custom-call | tf_op jit(solution)/shard_map/pallas_call | solution.py:134
  511.9 2.0 copy.31
  513.8 2.3 dot_general.14
  516.1 26.1 %fusion.2 = bf16[128,4,8192]{2,0,1:T(8,128)(2,1)} fusion(bf16[128,4,2048]{2,0,1:T(8,128)(2,1)} %dot_general.14, bf16[2048,8192]{1,0:T(8,128)(2,1)} %param.17), kind=kOutput, calls=%fused_computation.3 | convolution fusion | flops 17184063488 | bytes 44040192 | tf_op jit(solution)/shard_map/dot_general | solution.py:194
  542.2 0.6 copy-done.4
  542.9 2.3 reshape.240
  545.1 5.9 multiply_reduce_fusion
  551.0 12.1 %all-reduce.1 = bf16[128,4,64]{0,2,1:T(8,128)(2,1)S(1)} all-reduce(f32[128,4,64]{0,2,1:T(8,128)S(1)} %multiply_reduce_fusion), channel_id=1, replica_groups=mesh['dp'=8,'mp'=4] {'mp'}, use_global_device_ids=true, to_apply=%region_5.6 | all-reduce | flops 32768 | bytes 196608 | tf_op jit(solution)/shard_map/psum | solution.py:208
  563.1 54.9 %all-gather.5.cloned.1.call-done = bf16[16,64,2048]{2,1,0:T(8,128)(2,1)} async-done(((bf16[2,64,2048]{2,1,0:T(8,128)(2,1)}), bf16[16,64,2048]{2,1,0:T(8,128)(2,1)}) %all-gather.5.cloned.1.call-update) | async-done | bytes 4194320 | tf_op jit(solution)/shard_map/all_gather | solution.py:209
  618.1 5.4 add_convert_fusion
  623.4 2.9 copy.32
  (39 shorter events, 1.6 us)
Async XLA Ops:
  7.4 1.0 copy-start
  7.4 537.8 %all-gather.3.cloned.1.call-start = ((), (), s32[]{:S(2)}) async-start(), calls=%async_computation.4 | async-start | bytes 4718592 | tf_op jit(solution)/shard_map/all_gather | solution.py:201
  471.3 146.7 %all-gather.5.cloned.1.call-start = ((), (), s32[]{:S(2)}) async-start(), calls=%async_computation.5 | async-start | bytes 4718592 | tf_op jit(solution)/shard_map/all_gather | solution.py:209
  472.1 5.0 copy-start.2
  472.1 6.0 copy-start.3
  472.1 6.4 %copy-start.5 = (s32[128]{0:T(128)S(1)}, s32[128]{0:T(128)}, u32[]{:S(2)}) copy-start(s32[128]{0:T(128)} %constant.52.clone.1) | copy-start | bytes 1540
  472.1 146.0 %reduce-scatter.2.cloned.1.call-start = ((), (), s32[]{:S(2)}) async-start(), calls=%async_computation.3 | async-start | bytes 10485760 | tf_op jit(solution)/shard_map/reduce_scatter | solution.py:217
  542.2 0.7 copy-start.4
  618.1 8.3 %copy-start.1 = (s32[4096]{0:T(1024)S(1)}, s32[4096]{0:T(1024)}, u32[]{:S(2)}) copy-start(s32[4096]{0:T(1024)} %param.13) | copy-start | bytes 49156
Sparse Core Ops, SparseCore 0:
  471.4 72.3 all-gather.2
  546.2 71.8 all-gather.4
Sparse Core Ops, SparseCore 1:
  542.3 71.0 reduce-scatter.1

commit v7 on v3

--- a/solution.py
+++ b/solution.py
@@ -140,7 +140,10 @@
         jnp.where(key[:, None] == table_ids[None, :], local_slot[:, None], 0), axis=0
     ).reshape(owners, capacity)
     wanted = lax.all_to_all(wish_table, "dp", split_axis=0, concat_axis=0, tiled=True)
-    served = jnp.take(key_value_pool, wanted.reshape(-1), axis=0).reshape(
+    pick = (wanted.reshape(-1)[:, None] == jnp.arange(pool_dev)[None, :]).astype(key_value_pool.dtype)
+    served = jnp.dot(
+        pick, key_value_pool.reshape(pool_dev, -1), preferred_element_type=jnp.float32
+    ).astype(key_value_pool.dtype).reshape(
         (owners, capacity) + key_value_pool.shape[1:]
     )
     fetched = lax.all_to_all(served, "dp", split_axis=0, concat_axis=0, tiled=True)

time: 405 us -> 407 us (level)
  matrix products: 37.4 us -> 54.5 us
  local copies, waits for them, and re-layouts: 44.7 us -> 31.1 us
  other arithmetic: 6.97 us -> 2.42 us
    gather x1 -> x0, local copies, waits for them, and re-layouts: 22.9 us -> none  [shards(): jnp.take(key_value_pool, wanted.reshape(-1), axis=0)]
    dot_general x0 -> x1, matrix products: none -> 17.2 us  [shards(): jnp.dot(pick, key_value_pool.reshape(pool_dev, -1), preferred_element_typ...]
    unnamed x13 -> x14, local copies, waits for them, and re-layouts: 1.46 us -> 10.8 us
    select_n x2 -> x0, other arithmetic: 4.53 us -> none  [shards(): jnp.take(key_value_pool, wanted.reshape(-1), axis=0)]
where the time goes in v7:
time: 407 us; the launch traced here: 405 us
  blocking collectives  213 us (52%)
  waiting for transfers between devices  55.6 us (14%)
  matrix products  54.5 us (13%)
  Pallas kernels  32.7 us (8%)
  local copies, waits for them, and re-layouts  31.1 us (8%)
  between operations  15 us (4%)
    all_to_all x1, blocking collectives, shards(): lax.all_to_all(served, 'dp', split_axis=0, concat_axis=0, tiled=True)  188 us
    all_gather x1, waiting for transfers between devices, shards(): single_panel = lax.all_gather(adapter_up_panels, 'dp', axis=0, tiled=True)  54.8 us
    pallas_call x1, Pallas kernels, attend(): pl.pallas_call(body, grid_spec=grid_spec, out_shape=jax.ShapeDtypeStruct(...  32.7 us
    dot_general x1, matrix products, shards(): jnp.dot(attended.reshape(req_dev * step_count, query_width), output_weigh...  26.1 us
    dot_general x1, matrix products, shards(): jnp.dot(pick, key_value_pool.reshape(pool_dev, -1), preferred_element_typ...  17.2 us
    all_to_all x1, blocking collectives, shards(): lax.all_to_all(wish_table, 'dp', split_axis=0, concat_axis=0, tiled=True)  13.5 us
    psum x1, blocking collectives, shards(): rank_sum = lax.psum(rank_part, 'mp').astype(jnp.bfloat16)  12.1 us
    unnamed x14, local copies, waits for them, and re-layouts  10.8 us
  transfers between devices with their start and end apart: 3, of which 1 were waited for; matrix products, arithmetic and copies ran while one was open for 11% of the time, Pallas kernels for 8%

profile of v7, /device:TPU:0, one launch (start us, length us, event | category | flops | bytes accessed | tf_op | source)
XLA Modules:
  0.0 404.9 jit_solution(6138020425241811742)
XLA Ops:
  7.4 0.8 copy.27
  8.4 3.1 gather_fusion
  12.5 0.6 add_select_fusion.2
  13.4 13.5 %all_to_all.14 = s32[8,1,64]{2,1,0:T(1,128)S(1)} all-to-all(s32[8,1,64]{2,1,0:T(1,128)S(1)} %all_to_all.9), channel_id=1, replica_groups=mesh['dp'=8,'mp'=4] {'dp'}, dimensions={0} | all-to-all | bytes 4096 | tf_op jit(solution)/shard_map/all_to_all | solution.py:142
  27.4 0.7 reduce.5
  28.2 17.2 %fusion.7 = bf16[64,8,64,128]{3,1,2,0:T(8,128)(2,1)} fusion(bf16[64,8,64,128]{3,2,1,0:T(8,128)(2,1)} %bitcast.70, s32[512]{0:T(512)S(1)} %eq.86), kind=kOutput, calls=%fused_computation.7 | convolution fusion | flops 4299423744 | bytes 16779264 | tf_op jit(solution)/shard_map/dot_general | solution.py:144
  45.3 9.3 %copy.42 = bf16[64,8,64,128]{3,2,1,0:T(8,128)(2,1)} copy(bf16[64,8,64,128]{3,1,2,0:T(8,128)(2,1)} %fusion.7) | data formatting | bytes 16777216
  54.6 187.6 %all_to_all.15 = bf16[8,64,2,2,16,128]{5,4,3,2,1,0:T(8,128)(2,1)} all-to-all(bf16[8,64,2,2,16,128]{5,4,3,2,1,0:T(8,128)(2,1)} %bitcast.63), channel_id=1, replica_groups=mesh['dp'=8,'mp'=4] {'dp'}, dimensions={0} | all-to-all | bytes 16777216 | tf_op jit(solution)/shard_map/all_to_all | solution.py:149
  242.3 0.7 all-gather.5.cloned.1.call-update
  243.3 3.2 reshape.227
  246.5 1.7 copy.29
  248.2 1.0 copy.30
  249.6 0.6 reshape.230.refs_4_
  250.2 32.7 %shard_map.100 = bf16[2,4096,128]{2,1,0:T(8,128)(2,1)} custom-call(s32[512]{0:T(512)} %get-tuple-element.14.refs_0_, bf16[512,2,2,16,128]{4,3,2,1,0:T(8,128)(2,1)} %bitcast.62, bf16[2,4096,128]{2,1,0:T(8,128)(2,1)} %bitcast.64, bf16[2,2,512,128]{3,2,1,0:T(8,128)(2,1)} %bitcast.66, s32[32,1,384]{2,1,0:T(1,128)} %reshape.230.refs_4_), custom_call_target="tpu_custom_call" | custom-call | tf_op jit(solution)/shard_map/pallas_call | solution.py:93
  283.0 2.0 copy.31
  284.9 2.3 dot_general.18
  287.2 26.1 %fusion.2 = bf16[128,4,8192]{2,0,1:T(8,128)(2,1)} fusion(bf16[128,4,2048]{2,0,1:T(8,128)(2,1)} %dot_general.18, bf16[2048,8192]{1,0:T(8,128)(2,1)} %param.17), kind=kOutput, calls=%fused_computation.4 | convolution fusion | flops 17184063488 | bytes 44040192 | tf_op jit(solution)/shard_map/dot_general | solution.py:156
  313.4 0.6 copy-done.4
  314.0 2.3 reshape.241
  316.3 5.9 %multiply_reduce_fusion = f32[128,4,64]{0,2,1:T(8,128)S(1)} fusion(bf16[16,64,2048]{2,1,0:T(8,128)(2,1)} %all-gather.3.cloned.1.call-done, bf16[128,4,2048,1]{2,0,1,3:T(8,128)(2,1)} %reshape.241, f32[128,16]{0,1:T(8,128)S(1)} %get-tuple-element.15), kind=kOutput, calls=%fused_computation.16 | convolution fusion | flops 2148499456 | bytes 6430720 | tf_op jit(solution)/shard_map/qsf,nrf->qsnr/dot_general | solution.py:166
  322.2 12.1 %all-reduce.1 = bf16[128,4,64]{0,2,1:T(8,128)(2,1)S(1)} all-reduce(f32[128,4,64]{0,2,1:T(8,128)S(1)} %multiply_reduce_fusion), channel_id=1, replica_groups=mesh['dp'=8,'mp'=4] {'mp'}, use_global_device_ids=true, to_apply=%region_5.6 | all-reduce | flops 32768 | bytes 196608 | tf_op jit(solution)/shard_map/psum | solution.py:170
  334.3 54.8 %all-gather.5.cloned.1.call-done = bf16[16,64,2048]{2,1,0:T(8,128)(2,1)} async-done(((bf16[2,64,2048]{2,1,0:T(8,128)(2,1)}), bf16[16,64,2048]{2,1,0:T(8,128)(2,1)}) %all-gather.5.cloned.1.call-update) | async-done | bytes 4194320 | tf_op jit(solution)/shard_map/all_gather | solution.py:171
  389.1 5.4 %add_convert_fusion = bf16[128,4,2048]{2,0,1:T(8,128)(2,1)S(1)} fusion(bf16[128,4,2048]{2,0,1:T(8,128)(2,1)} %reduce-scatter.2.cloned.1.call-done, bf16[16,64,2048]{2,1,0:T(8,128)(2,1)} %all-gather.5.cloned.1.call-done, bf16[128,16]{0,1:T(8,128)(2,1)S(1)} %get-tuple-element.16, bf16[128,4,64]{0,2,1:T(8,128)(2,1)S(1)} %all-reduce.1), kind=kOutput, calls=%fused_computation.14 | convolution fusion | flops 2154299392 | bytes 8458240 | tf_op jit(solution)/shard_map/utja,jam->utm/dot_general | solution.py:175
  394.5 2.9 copy.32
  (41 shorter events, 2.8 us)
Async XLA Ops:
  7.4 1.0 copy-start
  7.4 308.9 %all-gather.3.cloned.1.call-start = ((), (), s32[]{:S(2)}) async-start(), calls=%async_computation.4 | async-start | bytes 4718592 | tf_op jit(solution)/shard_map/all_gather | solution.py:163
  242.3 146.8 %all-gather.5.cloned.1.call-start = ((), (), s32[]{:S(2)}) async-start(), calls=%async_computation.5 | async-start | bytes 4718592 | tf_op jit(solution)/shard_map/all_gather | solution.py:171
  243.0 5.1 %copy-start.2 = (bf16[128,4,2,2,128]{4,3,2,1,0:T(2,128)(2,1)S(1)}, bf16[128,4,2,2,128]{4,3,2,1,0:T(2,128)(2,1)}, u32[]{:S(2)}) copy-start(bf16[128,4,2,2,128]{4,3,2,1,0:T(2,128)(2,1)} %param.11) | copy-start | bytes 1572868
  243.1 6.1 %copy-start.3 = (s32[128]{0:T(128)S(1)}, s32[128]{0:T(128)}, u32[]{:S(2)}) copy-start(s32[128]{0:T(128)} %param.15) | copy-start | bytes 1540
  243.1 6.5 %copy-start.5 = (s32[128]{0:T(128)S(1)}, s32[128]{0:T(128)}, u32[]{:S(2)}) copy-start(s32[128]{0:T(128)} %constant.52.clone.1) | copy-start | bytes 1540
  243.1 146.0 %reduce-scatter.2.cloned.1.call-start = ((), (), s32[]{:S(2)}) async-start(), calls=%async_computation.3 | async-start | bytes 10485760 | tf_op jit(solution)/shard_map/reduce_scatter | solution.py:179
  313.3 0.7 copy-start.4
  389.1 8.3 %copy-start.1 = (s32[4096]{0:T(1024)S(1)}, s32[4096]{0:T(1024)}, u32[]{:S(2)}) copy-start(s32[4096]{0:T(1024)} %param.13) | copy-start | bytes 49156
Sparse Core Ops, SparseCore 0:
  242.4 72.7 all-gather.2
  317.6 71.4 all-gather.4
Sparse Core Ops, SparseCore 1:
  313.4 71.0 reduce-scatter.1

commit v8 on v4

--- a/solution.py
+++ b/solution.py
@@ -143,25 +143,52 @@
     served = jnp.take(key_value_pool, wanted.reshape(-1), axis=0, mode="clip").reshape(
         (owners, capacity) + key_value_pool.shape[1:]
     )
+    early_down = lax.all_gather(adapter_down_panels[:1], "dp", axis=0, tiled=True)
+    served, early_down = lax.optimization_barrier((served, early_down))
     fetched = lax.all_to_all(served, "dp", split_axis=0, concat_axis=0, tiled=True)
-    fetched, adapter_up_panels = lax.optimization_barrier((fetched, adapter_up_panels))
+    fetched, late_down, adapter_up_panels = lax.optimization_barrier(
+        (fetched, adapter_down_panels[1:], adapter_up_panels)
+    )
     flat_rows = fetched.reshape((owners * capacity,) + key_value_pool.shape[1:])
     row_index = jnp.clip(target * capacity + slot_index, 0, owners * capacity - 1)
-    attended = attend(row_index, flat_rows, queries, fresh_key_value, live_prefix_length, blocks_per)
-    base_product = jnp.dot(
-        attended.reshape(req_dev * step_count, query_width),
-        output_weight,
-        preferred_element_type=jnp.float32,
-    )
-    base_product = base_product.reshape(req_dev, step_count, out_width)
+    half = req_dev // 2
+    pieces = []
+    summed = []
+    for part in range(2):
+        rows_of = slice(part * half, (part + 1) * half)
+        part_attended = attend(
+            row_index[part * half * blocks_per:(part + 1) * half * blocks_per],
+            flat_rows,
+            queries[rows_of],
+            fresh_key_value[rows_of],
+            live_prefix_length[rows_of],
+            blocks_per,
+        )
+        part_product = jnp.dot(
+            part_attended.reshape(half * step_count, query_width),
+            output_weight,
+            preferred_element_type=jnp.float32,
+        ).reshape(half, step_count, out_width)
+        summed.append(
+            lax.psum_scatter(part_product.astype(jnp.bfloat16), "mp", scatter_dimension=2, tiled=True)
+        )
+        pieces.append(part_attended)
+    attended = jnp.concatenate(pieces, axis=0)
+    summed_output = jnp.concatenate(summed, axis=0)
     adapter = request_adapter[:, 0]
-    single_panel = lax.all_gather(adapter_down_panels, "dp", axis=0, tiled=True)
-    panel_count = single_panel.shape[0]
-    hit_mask = (adapter[:, None] == jnp.arange(panel_count)[None, :]).astype(jnp.float32)
-    every_rank = jnp.einsum(
-        "qsf,nrf->qsnr", attended, single_panel, preferred_element_type=jnp.float32
-    )
-    rank_part = jnp.einsum("qsnr,qn->qsr", every_rank, hit_mask)
+    local_adapters = adapter_down_panels.shape[0]
+    rank_part = 0.0
+    late_down = lax.all_gather(late_down, "dp", axis=0, tiled=True)
+    for low, width, panel in ((0, 1, early_down), (1, local_adapters - 1, late_down)):
+        if width == 0:
+            continue
+        panel_ids = jnp.arange(panel.shape[0])
+        hit_mask = (
+            (adapter[:, None] // local_adapters == (panel_ids // width)[None, :])
+            & (adapter[:, None] % local_adapters == (low + panel_ids % width)[None, :])
+        ).astype(jnp.float32)
+        every_rank = jnp.einsum("qsf,nrf->qsnr", attended, panel, preferred_element_type=jnp.float32)
+        rank_part = rank_part + jnp.einsum("qsnr,qn->qsr", every_rank, hit_mask)
     rank_sum = lax.psum(rank_part, "mp").astype(jnp.bfloat16)
     single_panel = lax.all_gather(adapter_up_panels, "dp", axis=0, tiled=True)
     panel_count = single_panel.shape[0]
@@ -171,9 +198,6 @@
         "utja,jam->utm", selected_panel, single_panel, preferred_element_type=jnp.float32
     )
     adapter_output = (adapter_sum * ADAPTER_SCALE).astype(jnp.bfloat16)
-    summed_output = lax.psum_scatter(
-        base_product.astype(jnp.bfloat16), "mp", scatter_dimension=2, tiled=True
-    )
     return (summed_output + adapter_output.astype(jnp.float32)).astype(jnp.bfloat16)
 
 

time: 448 us -> 481 us (1.074)
  blocking collectives: 25.2 us -> 214 us
  waiting for transfers between devices: 283 us -> 119 us
  matrix products: 37.4 us -> 44 us
    all_to_all x1 -> x0, waiting for transfers between devices: 232 us -> none  [shards(): lax.all_to_all(served, 'dp', split_axis=0, concat_axis=0, tiled=True)]
    all_to_all x0 -> x1, blocking collectives: none -> 189 us  [shards(): lax.all_to_all(served, 'dp', split_axis=0, concat_axis=0, tiled=True)]
    reduce_scatter x1 -> x2, waiting for transfers between devices: 50.6 us -> 92.3 us  [shards(): lax.psum_scatter(part_product.astype(jnp.bfloat16), 'mp', scatter_dimensi...]
    all_gather x1, waiting for transfers between devices: 0.02 us -> 15.7 us  [shards(): single_panel = lax.all_gather(adapter_up_panels, 'dp', axis=0, tiled=True)]
    all_gather x1 -> x2, waiting for transfers between devices: 0.01 us -> 10.2 us  [the longest x1 10.2 us: shards(): lax.all_gather(adapter_down_panels[:1], 'dp', axis=0, tiled=True)]
    dot_general x2 -> x4, matrix products: 32 us -> 38.7 us  [the longest x2 32.9 us: shards(): jnp.dot(part_attended.reshape(half * step_count, query_width), output_wei...]
    slice x0 -> x4, local copies, waits for them, and re-layouts: none -> 5.04 us  [the longest x1 2.55 us: shards(): queries[rows_of]]
    all_to_all x1 -> x0, starting transfers between devices: 4.97 us -> none  [shards(): lax.all_to_all(served, 'dp', split_axis=0, concat_axis=0, tiled=True)]
  transfers between devices with their start and end apart: 4 -> 5, of which waited for: 2 -> 4; matrix products, arithmetic and copies ran while one was open for 10% -> 18% of each run, Pallas kernels for 7% -> 8%
where the time goes in v8:
time: 481 us; the launch traced here: 479 us
  blocking collectives  214 us (44%)
  waiting for transfers between devices  119 us (25%)
  local copies, waits for them, and re-layouts  48.8 us (10%)
  matrix products  44 us (9%)
  Pallas kernels  37.5 us (8%)
  between operations  13.4 us (3%)
    all_to_all x1, blocking collectives, shards(): lax.all_to_all(served, 'dp', split_axis=0, concat_axis=0, tiled=True)  189 us
    reduce_scatter x2, waiting for transfers between devices, shards(): lax.psum_scatter(part_product.astype(jnp.bfloat16), 'mp', scatter_dimensi...  92.3 us
    pallas_call x2, Pallas kernels, attend(): pl.pallas_call(body, grid_spec=grid_spec, out_shape=jax.ShapeDtypeStruct(...  37.5 us
    dot_general x2, matrix products, shards(): jnp.dot(part_attended.reshape(half * step_count, query_width), output_wei...  32.9 us
    gather x1, local copies, waits for them, and re-layouts, shards(): jnp.take(key_value_pool, wanted.reshape(-1), axis=0, mode='clip')  22.9 us
    all_gather x1, waiting for transfers between devices, shards(): single_panel = lax.all_gather(adapter_up_panels, 'dp', axis=0, tiled=True)  15.7 us
    all_to_all x1, blocking collectives, shards(): lax.all_to_all(wish_table, 'dp', split_axis=0, concat_axis=0, tiled=True)  13.5 us
    psum x1, blocking collectives, shards(): rank_sum = lax.psum(rank_part, 'mp').astype(jnp.bfloat16)  12.4 us
  transfers between devices with their start and end apart: 5, of which 4 were waited for; matrix products, arithmetic and copies ran while one was open for 18% of the time, Pallas kernels for 8%

profile of v8, /device:TPU:0, one launch (start us, length us, event | category | flops | bytes accessed | tf_op | source)
XLA Modules:
  0.0 479.5 jit_solution(10801958615670975226)
XLA Ops:
  6.5 1.9 fusion.55
  9.5 3.1 gather_fusion
  13.9 13.5 %all_to_all.14 = s32[8,1,64]{2,1,0:T(1,128)S(1)} all-to-all(s32[8,1,64]{2,1,0:T(1,128)S(1)} %all_to_all.9), channel_id=1, replica_groups=mesh['dp'=8,'mp'=4] {'dp'}, dimensions={0} | all-to-all | bytes 4096 | tf_op jit(solution)/shard_map/all_to_all | solution.py:142
  28.6 22.9 %gather_fusion.1 = bf16[512,2,2,16,128]{4,3,2,1,0:T(8,128)(2,1)} fusion(bf16[512,2,2,16,128]{4,3,2,1,0:T(8,128)(2,1)} %param.12, s32[1024]{0:T(1024)S(1)} %pad_clamp_fusion), kind=kCustom, calls=%fused_computation.1 | custom fusion | bytes 16779264 | tf_op jit(solution)/shard_map/jit(_take)/gather | solution.py:143
  51.5 10.2 %all-gather.4.cloned.1.call-done = bf16[8,64,2048]{2,1,0:T(8,128)(2,1)} async-done(((bf16[1,64,2048]{2,1,0:T(8,128)(2,1)}), bf16[8,64,2048]{2,1,0:T(8,128)(2,1)}) %all-gather.4.cloned.1.call-update) | async-done | bytes 2097168 | tf_op jit(solution)/shard_map/all_gather | solution.py:146
  61.7 188.5 %all_to_all.15 = bf16[8,64,2,2,16,128]{5,4,3,2,1,0:T(8,128)(2,1)} all-to-all(bf16[8,64,2,2,16,128]{5,4,3,2,1,0:T(8,128)(2,1)} %bitcast.105), channel_id=1, replica_groups=mesh['dp'=8,'mp'=4] {'dp'}, dimensions={0} | all-to-all | bytes 16777216 | tf_op jit(solution)/shard_map/all_to_all | solution.py:148
  252.6 2.6 fusion.54
  255.9 1.2 copy.41
  257.0 1.4 slice_bitcast_fusion.1
  259.8 18.7 %shard_map.100 = bf16[2,2048,128]{2,1,0:T(8,128)(2,1)} custom-call(s32[256]{0:T(256)} %get-tuple-element.27.refs_0_, bf16[512,2,2,16,128]{4,3,2,1,0:T(8,128)(2,1)} %bitcast.103, bf16[2,2048,128]{2,1,0:T(8,128)(2,1)} %bitcast.106, bf16[2,2,256,128]{3,2,1,0:T(8,128)(2,1)} %bitcast.110, s32[16,1,384]{2,1,0:T(1,128)} %copy.43.refs_4_), custom_call_target="tpu_custom_call" | custom-call | tf_op jit(solution)/shard_map/pallas_call | solution.py:93
  278.5 1.4 copy.44
  280.4 16.5 %fusion.4 = bf16[64,4,8192]{2,0,1:T(8,128)(2,1)} fusion(bf16[64,4,2048]{2,0,1:T(8,128)(2,1)S(1)} %dot_general.25, bf16[2048,8192]{1,0:T(8,128)(2,1)} %param.17), kind=kOutput, calls=%fused_computation.6 | convolution fusion | flops 8592031744 | bytes 38797312 | tf_op jit(solution)/shard_map/dot_general | solution.py:167
  298.5 1.2 copy.45
  300.5 18.7 %shard_map.101 = bf16[2,2048,128]{2,1,0:T(8,128)(2,1)} custom-call(s32[256]{0:T(256)} %get-tuple-element.28.refs_0_, bf16[512,2,2,16,128]{4,3,2,1,0:T(8,128)(2,1)} %bitcast.104, bf16[2,2048,128]{2,1,0:T(8,128)(2,1)} %bitcast.107, bf16[2,2,256,128]{3,2,1,0:T(8,128)(2,1)} %bitcast.111, s32[16,1,384]{2,1,0:T(1,128)} %reshape.274.refs_4_), custom_call_target="tpu_custom_call" | custom-call | tf_op jit(solution)/shard_map/pallas_call | solution.py:93
  319.2 1.4 copy.47
  321.1 16.4 %fusion.7 = bf16[64,4,8192]{2,0,1:T(8,128)(2,1)} fusion(bf16[64,4,2048]{2,0,1:T(8,128)(2,1)S(1)} %dot_general.27, bf16[2048,8192]{1,0:T(8,128)(2,1)} %param.17), kind=kOutput, calls=%fused_computation.7 | convolution fusion | flops 8592031744 | bytes 38797312 | tf_op jit(solution)/shard_map/dot_general | solution.py:167
  338.5 2.9 fusion.36
  341.4 2.9 fusion.33
  344.3 12.4 %all-reduce.1 = bf16[128,4,64]{0,2,1:T(8,128)(2,1)S(1)} all-reduce(f32[128,4,64]{0,2,1:T(8,128)S(1)} %add.112), channel_id=1, replica_groups=mesh['dp'=8,'mp'=4] {'mp'}, use_global_device_ids=true, to_apply=%region_6.7 | all-reduce | flops 32768 | bytes 196608 | tf_op jit(solution)/shard_map/psum | solution.py:192
  356.7 15.7 %all-gather.8.cloned.1.call-done = bf16[16,64,2048]{2,1,0:T(8,128)(2,1)} async-done(((bf16[2,64,2048]{2,1,0:T(8,128)(2,1)}), bf16[16,64,2048]{2,1,0:T(8,128)(2,1)}) %all-gather.8.cloned.1.call-update) | async-done | bytes 4194320 | tf_op jit(solution)/shard_map/all_gather | solution.py:193
  372.4 45.2 %reduce-scatter.3.cloned.1.call-done = bf16[64,4,2048]{2,0,1:T(8,128)(2,1)} async-done(((bf16[64,4,8192]{2,0,1:T(8,128)(2,1)}), bf16[64,4,2048]{2,0,1:T(8,128)(2,1)}) %reduce-scatter.3.cloned.1.call-update) | async-done | bytes 1048592 | tf_op jit(solution)/shard_map/reduce_scatter | solution.py:173
  417.6 47.1 %reduce-scatter.5.cloned.1.call-done = bf16[64,4,2048]{2,0,1:T(8,128)(2,1)} async-done(((bf16[64,4,8192]{2,0,1:T(8,128)(2,1)}), bf16[64,4,2048]{2,0,1:T(8,128)(2,1)}) %reduce-scatter.5.cloned.1.call-update) | async-done | bytes 1048592 | tf_op jit(solution)/shard_map/reduce_scatter | solution.py:173
  464.7 5.3 %add_convert_fusion = bf16[128,4,2048]{2,0,1:T(8,128)(2,1)S(1)} fusion(bf16[16,64,2048]{2,1,0:T(8,128)(2,1)} %all-gather.8.cloned.1.call-done, bf16[64,4,2048]{2,0,1:T(8,128)(2,1)} %reduce-scatter.5.cloned.1.call-done, bf16[64,4,2048]{2,0,1:T(8,128)(2,1)} %reduce-scatter.3.cloned.1.call-done, bf16[128,16]{0,1:T(8,128)(2,1)S(1)} %fusion.49, ...), kind=kOutput, calls=%fused_computation.12 | convolution fusion | flops 2157445120 | bytes 8458240 | tf_op jit(solution)/shard_map/utja,jam->utm/dot_general | solution.py:197
  470.0 2.9 copy.48
  (67 shorter events, 12.1 us)
Async XLA Ops:
  6.5 3.0 copy-start
  6.5 55.2 %all-gather.4.cloned.1.call-start = ((), (), s32[]{:S(2)}) async-start(), calls=%async_computation.4 | async-start | bytes 2359296 | tf_op jit(solution)/shard_map/all_gather | solution.py:146
  8.4 333.0 %all-gather.6.cloned.1.call-start = ((), (), s32[]{:S(2)}) async-start(), calls=%async_computation.7 | async-start | bytes 2359296 | tf_op jit(solution)/shard_map/all_gather | solution.py:181
  61.7 189.5 %copy-start.2 = (s32[128]{0:T(128)S(1)}, s32[128]{0:T(128)}, u32[]{:S(2)}) copy-start(s32[128]{0:T(128)} %param.15) | copy-start | bytes 1540
  61.7 190.2 %copy-start.4 = (s32[128]{0:T(128)S(1)}, s32[128]{0:T(128)}, u32[]{:S(2)}) copy-start(s32[128]{0:T(128)} %constant.110.clone.1) | copy-start | bytes 1540
  250.2 122.2 %all-gather.8.cloned.1.call-start = ((), (), s32[]{:S(2)}) async-start(), calls=%async_computation.8 | async-start | bytes 4718592 | tf_op jit(solution)/shard_map/all_gather | solution.py:193
  251.0 166.7 %reduce-scatter.3.cloned.1.call-start = ((), (), s32[]{:S(2)}) async-start(), calls=%async_computation.5 | async-start | bytes 5242880 | tf_op jit(solution)/shard_map/reduce_scatter | solution.py:173
  296.9 167.8 %reduce-scatter.5.cloned.1.call-start = ((), (), s32[]{:S(2)}) async-start(), calls=%async_computation.6 | async-start | bytes 5242880 | tf_op jit(solution)/shard_map/reduce_scatter | solution.py:173
  337.5 0.7 copy-start.3
  464.7 8.3 %copy-start.1 = (s32[4096]{0:T(1024)S(1)}, s32[4096]{0:T(1024)}, u32[]{:S(2)}) copy-start(s32[4096]{0:T(1024)} %param.13) | copy-start | bytes 49156
Sparse Core Ops, SparseCore 0:
  9.5 52.1 all-gather.3
  250.4 47.8 all-gather.5
  300.4 71.9 all-gather.7
  374.8 42.7 reduce-scatter.2
  420.2 44.4 reduce-scatter.4

commit v9 on v3

--- a/solution.py
+++ b/solution.py
@@ -140,7 +140,7 @@
         jnp.where(key[:, None] == table_ids[None, :], local_slot[:, None], 0), axis=0
     ).reshape(owners, capacity)
     wanted = lax.all_to_all(wish_table, "dp", split_axis=0, concat_axis=0, tiled=True)
-    served = jnp.take(key_value_pool, wanted.reshape(-1), axis=0).reshape(
+    served = jnp.take(key_value_pool, wanted.reshape(-1), axis=0, mode="clip").reshape(
         (owners, capacity) + key_value_pool.shape[1:]
     )
     fetched = lax.all_to_all(served, "dp", split_axis=0, concat_axis=0, tiled=True)

time: 405 us -> 403 us (level)
  other arithmetic: 6.97 us -> 2.43 us
    select_n x2 -> x0, other arithmetic: 4.53 us -> none  [shards(): jnp.take(key_value_pool, wanted.reshape(-1), axis=0)]
where the time goes in v9:
time: 403 us; the launch traced here: 401 us
  blocking collectives  213 us (53%)
  waiting for transfers between devices  55.6 us (14%)
  local copies, waits for them, and re-layouts  44.7 us (11%)
  matrix products  37.4 us (9%)
  Pallas kernels  32.7 us (8%)
  between operations  15 us (4%)
    all_to_all x1, blocking collectives, shards(): lax.all_to_all(served, 'dp', split_axis=0, concat_axis=0, tiled=True)  188 us
    all_gather x1, waiting for transfers between devices, shards(): single_panel = lax.all_gather(adapter_up_panels, 'dp', axis=0, tiled=True)  54.8 us
    pallas_call x1, Pallas kernels, attend(): pl.pallas_call(body, grid_spec=grid_spec, out_shape=jax.ShapeDtypeStruct(...  32.7 us
    dot_general x1, matrix products, shards(): jnp.dot(attended.reshape(req_dev * step_count, query_width), output_weigh...  26.1 us
    gather x1, local copies, waits for them, and re-layouts, shards(): jnp.take(key_value_pool, wanted.reshape(-1), axis=0, mode='clip')  22.9 us
    all_to_all x1, blocking collectives, shards(): lax.all_to_all(wish_table, 'dp', split_axis=0, concat_axis=0, tiled=True)  13.5 us
    psum x1, blocking collectives, shards(): rank_sum = lax.psum(rank_part, 'mp').astype(jnp.bfloat16)  12.1 us
  transfers between devices with their start and end apart: 3, of which 1 were waited for; matrix products, arithmetic and copies ran while one was open for 11% of the time, Pallas kernels for 8%

profile of v9, /device:TPU:0, one launch (start us, length us, event | category | flops | bytes accessed | tf_op | source)
XLA Modules:
  0.0 401.3 jit_solution(12722250962965821263)
XLA Ops:
  7.4 0.8 copy.27
  8.4 3.1 gather_fusion
  12.5 0.6 add_select_fusion.2
  13.4 13.5 %all_to_all.14 = s32[8,1,64]{2,1,0:T(1,128)S(1)} all-to-all(s32[8,1,64]{2,1,0:T(1,128)S(1)} %all_to_all.9), channel_id=1, replica_groups=mesh['dp'=8,'mp'=4] {'dp'}, dimensions={0} | all-to-all | bytes 4096 | tf_op jit(solution)/shard_map/all_to_all | solution.py:142
  26.9 0.5 broadcast.265
  27.4 0.7 reduce.5
  28.2 22.9 %gather_fusion.1 = bf16[512,2,2,16,128]{4,3,2,1,0:T(8,128)(2,1)} fusion(bf16[512,2,2,16,128]{4,3,2,1,0:T(8,128)(2,1)} %param.12, s32[1024]{0:T(1024)S(1)} %pad_clamp_fusion), kind=kCustom, calls=%fused_computation.1 | custom fusion | bytes 16779264 | tf_op jit(solution)/shard_map/jit(_take)/gather | solution.py:143
  51.1 187.6 %all_to_all.15 = bf16[8,64,2,2,16,128]{5,4,3,2,1,0:T(8,128)(2,1)} all-to-all(bf16[8,64,2,2,16,128]{5,4,3,2,1,0:T(8,128)(2,1)} %bitcast.53), channel_id=1, replica_groups=mesh['dp'=8,'mp'=4] {'dp'}, dimensions={0} | all-to-all | bytes 16777216 | tf_op jit(solution)/shard_map/all_to_all | solution.py:146
  238.8 0.7 all-gather.5.cloned.1.call-update
  239.7 3.2 reshape.224
  242.9 1.7 copy.29
  244.6 1.0 copy.30
  246.0 0.6 reshape.227.refs_4_
  246.7 32.7 %shard_map.100 = bf16[2,4096,128]{2,1,0:T(8,128)(2,1)} custom-call(s32[512]{0:T(512)} %get-tuple-element.14.refs_0_, bf16[512,2,2,16,128]{4,3,2,1,0:T(8,128)(2,1)} %bitcast.52, bf16[2,4096,128]{2,1,0:T(8,128)(2,1)} %bitcast.54, bf16[2,2,512,128]{3,2,1,0:T(8,128)(2,1)} %bitcast.56, s32[32,1,384]{2,1,0:T(1,128)} %reshape.227.refs_4_), custom_call_target="tpu_custom_call" | custom-call | tf_op jit(solution)/shard_map/pallas_call | solution.py:93
  279.4 2.0 copy.31
  281.4 2.3 dot_general.14
  283.7 26.1 %fusion.2 = bf16[128,4,8192]{2,0,1:T(8,128)(2,1)} fusion(bf16[128,4,2048]{2,0,1:T(8,128)(2,1)} %dot_general.14, bf16[2048,8192]{1,0:T(8,128)(2,1)} %param.17), kind=kOutput, calls=%fused_computation.4 | convolution fusion | flops 17184063488 | bytes 44040192 | tf_op jit(solution)/shard_map/dot_general | solution.py:153
  309.8 0.6 copy-done.4
  310.4 2.3 reshape.247
  312.7 5.9 %multiply_reduce_fusion = f32[128,4,64]{0,2,1:T(8,128)S(1)} fusion(bf16[16,64,2048]{2,1,0:T(8,128)(2,1)} %all-gather.3.cloned.1.call-done, bf16[128,4,2048,1]{2,0,1,3:T(8,128)(2,1)} %reshape.247, f32[128,16]{0,1:T(8,128)S(1)} %get-tuple-element.15), kind=kOutput, calls=%fused_computation.13 | convolution fusion | flops 2148499456 | bytes 6430720 | tf_op jit(solution)/shard_map/qsf,nrf->qsnr/dot_general | solution.py:163
  318.6 12.1 %all-reduce.1 = bf16[128,4,64]{0,2,1:T(8,128)(2,1)S(1)} all-reduce(f32[128,4,64]{0,2,1:T(8,128)S(1)} %multiply_reduce_fusion), channel_id=1, replica_groups=mesh['dp'=8,'mp'=4] {'mp'}, use_global_device_ids=true, to_apply=%region_5.6 | all-reduce | flops 32768 | bytes 196608 | tf_op jit(solution)/shard_map/psum | solution.py:167
  330.7 54.8 %all-gather.5.cloned.1.call-done = bf16[16,64,2048]{2,1,0:T(8,128)(2,1)} async-done(((bf16[2,64,2048]{2,1,0:T(8,128)(2,1)}), bf16[16,64,2048]{2,1,0:T(8,128)(2,1)}) %all-gather.5.cloned.1.call-update) | async-done | bytes 4194320 | tf_op jit(solution)/shard_map/all_gather | solution.py:168
  385.6 5.4 %add_convert_fusion = bf16[128,4,2048]{2,0,1:T(8,128)(2,1)S(1)} fusion(bf16[128,4,2048]{2,0,1:T(8,128)(2,1)} %reduce-scatter.2.cloned.1.call-done, bf16[16,64,2048]{2,1,0:T(8,128)(2,1)} %all-gather.5.cloned.1.call-done, bf16[128,16]{0,1:T(8,128)(2,1)S(1)} %get-tuple-element.16, bf16[128,4,64]{0,2,1:T(8,128)(2,1)S(1)} %all-reduce.1), kind=kOutput, calls=%fused_computation.11 | convolution fusion | flops 2154299392 | bytes 8458240 | tf_op jit(solution)/shard_map/utja,jam->utm/dot_general | solution.py:172
  391.0 2.9 copy.32
  (41 shorter events, 2.3 us)
Async XLA Ops:
  7.4 1.0 copy-start
  7.4 305.3 %all-gather.3.cloned.1.call-start = ((), (), s32[]{:S(2)}) async-start(), calls=%async_computation.4 | async-start | bytes 4718592 | tf_op jit(solution)/shard_map/all_gather | solution.py:160
  238.7 146.8 %all-gather.5.cloned.1.call-start = ((), (), s32[]{:S(2)}) async-start(), calls=%async_computation.5 | async-start | bytes 4718592 | tf_op jit(solution)/shard_map/all_gather | solution.py:168
  239.5 5.1 %copy-start.2 = (bf16[128,4,2,2,128]{4,3,2,1,0:T(2,128)(2,1)S(1)}, bf16[128,4,2,2,128]{4,3,2,1,0:T(2,128)(2,1)}, u32[]{:S(2)}) copy-start(bf16[128,4,2,2,128]{4,3,2,1,0:T(2,128)(2,1)} %param.11) | copy-start | bytes 1572868
  239.5 6.1 %copy-start.3 = (s32[128]{0:T(128)S(1)}, s32[128]{0:T(128)}, u32[]{:S(2)}) copy-start(s32[128]{0:T(128)} %param.15) | copy-start | bytes 1540
  239.5 6.5 %copy-start.5 = (s32[128]{0:T(128)S(1)}, s32[128]{0:T(128)}, u32[]{:S(2)}) copy-start(s32[128]{0:T(128)} %constant.52.clone.1) | copy-start | bytes 1540
  239.5 146.0 %reduce-scatter.2.cloned.1.call-start = ((), (), s32[]{:S(2)}) async-start(), calls=%async_computation.3 | async-start | bytes 10485760 | tf_op jit(solution)/shard_map/reduce_scatter | solution.py:176
  309.8 0.7 copy-start.4
  385.6 8.3 %copy-start.1 = (s32[4096]{0:T(1024)S(1)}, s32[4096]{0:T(1024)}, u32[]{:S(2)}) copy-start(s32[4096]{0:T(1024)} %param.13) | copy-start | bytes 49156
Sparse Core Ops, SparseCore 0:
  238.8 72.7 all-gather.2
  314.0 71.5 all-gather.4
Sparse Core Ops, SparseCore 1:
  309.9 71.0 reduce-scatter.1

commit v10 on v9

--- a/solution.py
+++ b/solution.py
@@ -139,7 +139,15 @@
     wish_table = jnp.sum(
         jnp.where(key[:, None] == table_ids[None, :], local_slot[:, None], 0), axis=0
     ).reshape(owners, capacity)
-    wanted = lax.all_to_all(wish_table, "dp", split_axis=0, concat_axis=0, tiled=True)
+    me = lax.axis_index("dp")
+    arrived = [wish_table[me]]
+    for shift in range(1, owners):
+        outgoing = jnp.take(wish_table, (me + shift) % owners, axis=0)
+        arrived.append(
+            lax.ppermute(outgoing, "dp", [(i, (i + shift) % owners) for i in range(owners)])
+        )
+    by_shift = jnp.stack(arrived)
+    wanted = jnp.take(by_shift, (me - jnp.arange(owners)) % owners, axis=0)
     served = jnp.take(key_value_pool, wanted.reshape(-1), axis=0, mode="clip").reshape(
         (owners, capacity) + key_value_pool.shape[1:]
     )

time: 403 us -> 404 us (level)
  blocking collectives: 213 us -> 198 us
  starting transfers between devices: 0.27 us -> 14.1 us
    ppermute x0 -> x7, starting transfers between devices: none -> 13.8 us  [shards(): lax.ppermute(outgoing, 'dp', [(i, (i + shift) % owners) for i in range(ow...]
    all_to_all x1 -> x0, blocking collectives: 13.5 us -> none  [shards(): lax.all_to_all(wish_table, 'dp', split_axis=0, concat_axis=0, tiled=True)]
  transfers between devices with their start and end apart: 3 -> 10, of which waited for: 1 -> 3; matrix products, arithmetic and copies ran while one was open for 11% -> 11% of each run, Pallas kernels for 8% -> 8%
where the time goes in v10:
time: 404 us; the launch traced here: 402 us
  blocking collectives  198 us (49%)
  waiting for transfers between devices  58.4 us (14%)
  local copies, waits for them, and re-layouts  44.8 us (11%)
  matrix products  37.1 us (9%)
  Pallas kernels  32.7 us (8%)
  between operations  15.2 us (4%)
  starting transfers between devices  14.1 us (3%)
    all_to_all x1, blocking collectives, shards(): lax.all_to_all(served, 'dp', split_axis=0, concat_axis=0, tiled=True)  186 us
    all_gather x1, waiting for transfers between devices, shards(): single_panel = lax.all_gather(adapter_up_panels, 'dp', axis=0, tiled=True)  55.5 us
    pallas_call x1, Pallas kernels, attend(): pl.pallas_call(body, grid_spec=grid_spec, out_shape=jax.ShapeDtypeStruct(...  32.7 us
    dot_general x1, matrix products, shards(): jnp.dot(attended.reshape(req_dev * step_count, query_width), output_weigh...  26 us
    gather x1, local copies, waits for them, and re-layouts, shards(): jnp.take(key_value_pool, wanted.reshape(-1), axis=0, mode='clip')  22.9 us
    ppermute x7, starting transfers between devices, shards(): lax.ppermute(outgoing, 'dp', [(i, (i + shift) % owners) for i in range(ow...  13.8 us
    psum x1, blocking collectives, shards(): rank_sum = lax.psum(rank_part, 'mp').astype(jnp.bfloat16)  12.2 us
  transfers between devices with their start and end apart: 10, of which 3 were waited for; matrix products, arithmetic and copies ran while one was open for 11% of the time, Pallas kernels for 8%

profile of v10, /device:TPU:0, one launch (start us, length us, event | category | flops | bytes accessed | tf_op | source)
XLA Modules:
  0.0 402.5 jit_solution(2887781001107974672)
XLA Ops:
  8.4 3.1 gather_fusion
  13.6 3.0 collective-permute-start
  16.6 1.6 collective-permute-start.1
  18.1 2.6 collective-permute-start.2
  20.7 1.2 collective-permute-start.3
  21.9 2.6 collective-permute-start.4
  24.6 1.4 collective-permute-start.5
  26.0 1.4 collective-permute-start.6
  28.2 1.4 collective-permute-done.6
  30.3 22.9 %gather_fusion.2 = bf16[512,2,2,16,128]{4,3,2,1,0:T(8,128)(2,1)} fusion(bf16[512,2,2,16,128]{4,3,2,1,0:T(8,128)(2,1)} %param.14, s32[1024]{0:T(1024)S(1)} %pad_clamp_fusion), kind=kCustom, calls=%fused_computation.2 | custom fusion | bytes 16779264 | tf_op jit(solution)/shard_map/jit(_take)/gather | solution.py:151
  53.2 186.2 %all_to_all.5 = bf16[8,64,2,2,16,128]{5,4,3,2,1,0:T(8,128)(2,1)} all-to-all(bf16[8,64,2,2,16,128]{5,4,3,2,1,0:T(8,128)(2,1)} %bitcast.76), channel_id=1, replica_groups=mesh['dp'=8,'mp'=4] {'dp'}, dimensions={0} | all-to-all | bytes 16777216 | tf_op jit(solution)/shard_map/all_to_all | solution.py:154
  240.4 3.2 reshape.299
  243.6 1.7 copy.29
  245.3 1.0 copy.30
  247.4 32.7 %shard_map.100 = bf16[2,4096,128]{2,1,0:T(8,128)(2,1)} custom-call(s32[512]{0:T(512)} %get-tuple-element.34.refs_0_, bf16[512,2,2,16,128]{4,3,2,1,0:T(8,128)(2,1)} %bitcast.75, bf16[2,4096,128]{2,1,0:T(8,128)(2,1)} %bitcast.77, bf16[2,2,512,128]{3,2,1,0:T(8,128)(2,1)} %bitcast.79, s32[32,1,384]{2,1,0:T(1,128)} %reshape.302.refs_4_), custom_call_target="tpu_custom_call" | custom-call | tf_op jit(solution)/shard_map/pallas_call | solution.py:93
  280.1 2.0 copy.31
  282.1 2.3 dot_general.14
  284.4 26.0 %fusion.2 = bf16[128,4,8192]{2,0,1:T(8,128)(2,1)} fusion(bf16[128,4,2048]{2,0,1:T(8,128)(2,1)} %dot_general.14, bf16[2048,8192]{1,0:T(8,128)(2,1)} %param.19), kind=kOutput, calls=%fused_computation.5 | convolution fusion | flops 17184063488 | bytes 44040192 | tf_op jit(solution)/shard_map/dot_general | solution.py:161
  311.1 2.3 reshape.445
  313.3 5.7 %multiply_reduce_fusion = f32[128,4,64]{0,2,1:T(8,128)S(1)} fusion(bf16[16,64,2048]{2,1,0:T(8,128)(2,1)} %all-gather.3.cloned.1.call-done, bf16[128,4,2048,1]{2,0,1,3:T(8,128)(2,1)} %reshape.445, f32[128,16]{0,1:T(8,128)S(1)} %get-tuple-element.35), kind=kOutput, calls=%fused_computation.14 | convolution fusion | flops 2148499456 | bytes 6430720 | tf_op jit(solution)/shard_map/qsf,nrf->qsnr/dot_general | solution.py:171
  319.0 12.2 %all-reduce.1 = bf16[128,4,64]{0,2,1:T(8,128)(2,1)S(1)} all-reduce(f32[128,4,64]{0,2,1:T(8,128)S(1)} %multiply_reduce_fusion), channel_id=1, replica_groups=mesh['dp'=8,'mp'=4] {'mp'}, use_global_device_ids=true, to_apply=%region_5.7 | all-reduce | flops 32768 | bytes 196608 | tf_op jit(solution)/shard_map/psum | solution.py:175
  331.2 55.5 %all-gather.5.cloned.1.call-done = bf16[16,64,2048]{2,1,0:T(8,128)(2,1)} async-done(((bf16[2,64,2048]{2,1,0:T(8,128)(2,1)}), bf16[16,64,2048]{2,1,0:T(8,128)(2,1)}) %all-gather.5.cloned.1.call-update) | async-done | bytes 4194320 | tf_op jit(solution)/shard_map/all_gather | solution.py:176
  386.7 5.4 %add_convert_fusion = bf16[128,4,2048]{2,0,1:T(8,128)(2,1)S(1)} fusion(bf16[128,4,2048]{2,0,1:T(8,128)(2,1)} %reduce-scatter.2.cloned.1.call-done, bf16[16,64,2048]{2,1,0:T(8,128)(2,1)} %all-gather.5.cloned.1.call-done, bf16[128,16]{0,1:T(8,128)(2,1)S(1)} %get-tuple-element.36, bf16[128,4,64]{0,2,1:T(8,128)(2,1)S(1)} %all-reduce.1), kind=kOutput, calls=%fused_computation.12 | convolution fusion | flops 2154299392 | bytes 8458240 | tf_op jit(solution)/shard_map/utja,jam->utm/dot_general | solution.py:180
  392.1 2.9 copy.32
  (59 shorter events, 7.1 us)
Async XLA Ops:
  7.4 1.0 copy-start
  7.4 306.0 %all-gather.3.cloned.1.call-start = ((), (), s32[]{:S(2)}) async-start(), calls=%async_computation.3 | async-start | bytes 4718592 | tf_op jit(solution)/shard_map/all_gather | solution.py:168
  13.6 11.0 %collective-permute-start = (s32[64]{0:T(128)S(1)}, s32[64]{0:T(128)S(1)}, u32[]{:S(2)}, u32[]{:S(2)}) collective-permute-start(s32[64]{0:T(128)S(1)} %get-tuple-element.31), channel_id=1, source_target_pairs={{0,4},{4,8},{8,12},{12,16},{16,20},{20,24},{24,28},{28,0},{1,5},{5... | collective-permute-start | bytes 776 | tf_op jit(solution)/shard_map/ppermute | solution.py:147
  16.6 9.4 %collective-permute-start.1 = (s32[64]{0:T(128)S(1)}, s32[64]{0:T(128)S(1)}, u32[]{:S(2)}, u32[]{:S(2)}) collective-permute-start(s32[64]{0:T(128)S(1)} %get-tuple-element.30), channel_id=1, source_target_pairs={{0,8},{4,12},{8,16},{12,20},{16,24},{20,28},{24,0},{28,4},{1,9},{5... | collective-permute-start | bytes 776 | tf_op jit(solution)/shard_map/ppermute | solution.py:147
  18.1 9.3 %collective-permute-start.2 = (s32[64]{0:T(128)S(1)}, s32[64]{0:T(128)S(1)}, u32[]{:S(2)}, u32[]{:S(2)}) collective-permute-start(s32[64]{0:T(128)S(1)} %get-tuple-element.29), channel_id=1, source_target_pairs={{0,12},{4,16},{8,20},{12,24},{16,28},{20,0},{24,4},{28,8},{1,13},{... | collective-permute-start | bytes 776 | tf_op jit(solution)/shard_map/ppermute | solution.py:147
  20.7 6.8 %collective-permute-start.3 = (s32[64]{0:T(128)S(1)}, s32[64]{0:T(128)S(1)}, u32[]{:S(2)}, u32[]{:S(2)}) collective-permute-start(s32[64]{0:T(128)S(1)} %get-tuple-element.28), channel_id=1, source_target_pairs={{0,16},{4,20},{8,24},{12,28},{16,0},{20,4},{24,8},{28,12},{1,17},{... | collective-permute-start | bytes 776 | tf_op jit(solution)/shard_map/ppermute | solution.py:147
  21.9 5.5 %collective-permute-start.4 = (s32[64]{0:T(128)S(1)}, s32[64]{0:T(128)S(1)}, u32[]{:S(2)}, u32[]{:S(2)}) collective-permute-start(s32[64]{0:T(128)S(1)} %get-tuple-element.27), channel_id=1, source_target_pairs={{0,20},{4,24},{8,28},{12,0},{16,4},{20,8},{24,12},{28,16},{1,21},{... | collective-permute-start | bytes 776 | tf_op jit(solution)/shard_map/ppermute | solution.py:147
  24.6 3.6 collective-permute-start.5
  26.0 3.5 collective-permute-start.6
  239.4 147.3 %all-gather.5.cloned.1.call-start = ((), (), s32[]{:S(2)}) async-start(), calls=%async_computation.4 | async-start | bytes 4718592 | tf_op jit(solution)/shard_map/all_gather | solution.py:176
  240.2 5.1 %copy-start.2 = (bf16[128,4,2,2,128]{4,3,2,1,0:T(2,128)(2,1)S(1)}, bf16[128,4,2,2,128]{4,3,2,1,0:T(2,128)(2,1)}, u32[]{:S(2)}) copy-start(bf16[128,4,2,2,128]{4,3,2,1,0:T(2,128)(2,1)} %param.13) | copy-start | bytes 1572868
  240.2 6.1 %copy-start.3 = (s32[128]{0:T(128)S(1)}, s32[128]{0:T(128)}, u32[]{:S(2)}) copy-start(s32[128]{0:T(128)} %param.17) | copy-start | bytes 1540
  240.2 6.5 %copy-start.5 = (s32[128]{0:T(128)S(1)}, s32[128]{0:T(128)}, u32[]{:S(2)}) copy-start(s32[128]{0:T(128)} %constant.139.clone.1) | copy-start | bytes 1540
  240.2 146.5 %reduce-scatter.2.cloned.1.call-start = ((), (), s32[]{:S(2)}) async-start(), calls=%async_computation.2 | async-start | bytes 10485760 | tf_op jit(solution)/shard_map/reduce_scatter | solution.py:184
  310.4 0.7 copy-start.4
  386.7 8.3 %copy-start.1 = (s32[4096]{0:T(1024)S(1)}, s32[4096]{0:T(1024)}, u32[]{:S(2)}) copy-start(s32[4096]{0:T(1024)} %param.15) | copy-start | bytes 49156
Sparse Core Ops, SparseCore 0:
  239.5 72.9 all-gather.2
  314.8 71.8 all-gather.4
Sparse Core Ops, SparseCore 1:
  310.5 71.5 reduce-scatter.1

commit v11 on v4

--- a/solution.py
+++ b/solution.py
@@ -140,13 +140,15 @@
         jnp.where(key[:, None] == table_ids[None, :], local_slot[:, None], 0), axis=0
     ).reshape(owners, capacity)
     wanted = lax.all_to_all(wish_table, "dp", split_axis=0, concat_axis=0, tiled=True)
-    served = jnp.take(key_value_pool, wanted.reshape(-1), axis=0, mode="clip").reshape(
-        (owners, capacity) + key_value_pool.shape[1:]
-    )
-    fetched = lax.all_to_all(served, "dp", split_axis=0, concat_axis=0, tiled=True)
-    fetched, adapter_up_panels = lax.optimization_barrier((fetched, adapter_up_panels))
-    flat_rows = fetched.reshape((owners * capacity,) + key_value_pool.shape[1:])
-    row_index = jnp.clip(target * capacity + slot_index, 0, owners * capacity - 1)
+    me = lax.axis_index("dp")
+    arrived = [jnp.take(key_value_pool, wanted[me], axis=0, mode="clip")]
+    for shift in range(1, owners):
+        outgoing = jnp.take(key_value_pool, wanted[(me + shift) % owners], axis=0, mode="clip")
+        arrived.append(
+            lax.ppermute(outgoing, "dp", [(i, (i + shift) % owners) for i in range(owners)])
+        )
+    flat_rows = jnp.concatenate(arrived, axis=0)
+    row_index = jnp.clip(((me - target) % owners) * capacity + slot_index, 0, owners * capacity - 1)
     attended = attend(row_index, flat_rows, queries, fresh_key_value, live_prefix_length, blocks_per)
     base_product = jnp.dot(
         attended.reshape(req_dev * step_count, query_width),

time: 448 us -> 466 us (1.040)
  waiting for transfers between devices: 283 us -> 234 us
  starting transfers between devices: 5.28 us -> 53.4 us
  local copies, waits for them, and re-layouts: 44.7 us -> 78.3 us
  blocking collectives: 25.2 us -> 11.7 us
    all_to_all x1, waiting for transfers between devices: 232 us -> 6.28 us  [shards(): lax.all_to_all(wish_table, 'dp', split_axis=0, concat_axis=0, tiled=True)]
    reduce_scatter x1, waiting for transfers between devices: 50.6 us -> 141 us  [shards(): lax.psum_scatter(base_product.astype(jnp.bfloat16), 'mp', scatter_dimensi...]
    ppermute x0 -> x7, waiting for transfers between devices: none -> 85.8 us  [shards(): lax.ppermute(outgoing, 'dp', [(i, (i + shift) % owners) for i in range(ow...]
    ppermute x0 -> x7, starting transfers between devices: none -> 46 us  [shards(): lax.ppermute(outgoing, 'dp', [(i, (i + shift) % owners) for i in range(ow...]
    unnamed x13 -> x14, local copies, waits for them, and re-layouts: 1.46 us -> 16.6 us
    gather x1 -> x8, local copies, waits for them, and re-layouts: 22.9 us -> 37.8 us  [the longest x7 33.7 us: shards(): jnp.take(key_value_pool, wanted[(me + shift) % owners], axis=0, mode='clip')]
    all_to_all x1 -> x0, blocking collectives: 13.5 us -> none  [shards(): lax.all_to_all(wish_table, 'dp', split_axis=0, concat_axis=0, tiled=True)]
  transfers between devices with their start and end apart: 4 -> 11, of which waited for: 2 -> 5; matrix products, arithmetic and copies ran while one was open for 10% -> 23% of each run, Pallas kernels for 7% -> 7%
where the time goes in v11:
time: 466 us; the launch traced here: 464 us
  waiting for transfers between devices  234 us (50%)
  local copies, waits for them, and re-layouts  78.3 us (17%)
  starting transfers between devices  53.4 us (11%)
  matrix products  36.7 us (8%)
  Pallas kernels  32.7 us (7%)
  between operations  15.1 us (3%)
  blocking collectives  11.7 us (3%)
    reduce_scatter x1, waiting for transfers between devices, shards(): lax.psum_scatter(base_product.astype(jnp.bfloat16), 'mp', scatter_dimensi...  141 us
    ppermute x7, waiting for transfers between devices, shards(): lax.ppermute(outgoing, 'dp', [(i, (i + shift) % owners) for i in range(ow...  85.8 us
    ppermute x7, starting transfers between devices, shards(): lax.ppermute(outgoing, 'dp', [(i, (i + shift) % owners) for i in range(ow...  46 us
    gather x7, local copies, waits for them, and re-layouts, shards(): jnp.take(key_value_pool, wanted[(me + shift) % owners], axis=0, mode='clip')  33.7 us
    pallas_call x1, Pallas kernels, attend(): pl.pallas_call(body, grid_spec=grid_spec, out_shape=jax.ShapeDtypeStruct(...  32.7 us
    dot_general x1, matrix products, shards(): jnp.dot(attended.reshape(req_dev * step_count, query_width), output_weigh...  26.2 us
    unnamed x14, local copies, waits for them, and re-layouts  16.6 us
    psum x1, blocking collectives, shards(): rank_sum = lax.psum(rank_part, 'mp').astype(jnp.bfloat16)  11.7 us
  transfers between devices with their start and end apart: 11, of which 5 were waited for; matrix products, arithmetic and copies ran while one was open for 23% of the time, Pallas kernels for 7%

profile of v11, /device:TPU:0, one launch (start us, length us, event | category | flops | bytes accessed | tf_op | source)
XLA Modules:
  0.0 464.3 jit_solution(1048760082760370112)
XLA Ops:
  9.9 3.1 gather_fusion
  15.5 7.3 %all-to-all-start = ((s32[8,1,64]{2,1,0:T(1,128)}), s32[8,1,64]{2,1,0:T(1,128)S(1)}, u32[]{:S(2)}, u32[]{:S(2)}) async-start(s32[8,1,64]{2,1,0:T(1,128)} %all_to_all.6), calls=%async_computation | async-start | bytes 8192 | tf_op jit(solution)/shard_map/all_to_all | solution.py:142
  22.9 6.3 %all-to-all-done = s32[8,1,64]{2,1,0:T(1,128)S(1)} async-done(((s32[8,1,64]{2,1,0:T(1,128)}), s32[8,1,64]{2,1,0:T(1,128)S(1)}, u32[]{:S(2)}, u32[]{:S(2)}) %all-to-all-start) | async-done | bytes 2080 | tf_op jit(solution)/shard_map/all_to_all | solution.py:142
  29.2 5.1 %gather_fusion.2 = bf16[64,2,2,16,128]{4,3,2,1,0:T(8,128)(2,1)} fusion(bf16[512,2,2,16,128]{4,3,2,1,0:T(8,128)(2,1)} %param.12, s32[1024]{0:T(1024)S(1)} %pad_clamp_fusion.6), kind=kCustom, calls=%fused_computation.2 | custom fusion | bytes 2097408 | tf_op jit(solution)/shard_map/jit(_take)/gather | solution.py:146
  34.8 4.2 gather_fusion.3
  41.4 5.1 %gather_fusion.4 = bf16[64,2,2,16,128]{4,3,2,1,0:T(8,128)(2,1)} fusion(bf16[512,2,2,16,128]{4,3,2,1,0:T(8,128)(2,1)} %param.12, s32[1024]{0:T(1024)S(1)} %pad_clamp_fusion.4), kind=kCustom, calls=%fused_computation.4 | custom fusion | bytes 2097408 | tf_op jit(solution)/shard_map/jit(_take)/gather | solution.py:146
  48.0 5.1 %gather_fusion.5 = bf16[64,2,2,16,128]{4,3,2,1,0:T(8,128)(2,1)} fusion(bf16[512,2,2,16,128]{4,3,2,1,0:T(8,128)(2,1)} %param.12, s32[1024]{0:T(1024)S(1)} %pad_clamp_fusion.3), kind=kCustom, calls=%fused_computation.5 | custom fusion | bytes 2097408 | tf_op jit(solution)/shard_map/jit(_take)/gather | solution.py:146
  53.0 3.1 collective-permute-start.3
  56.2 5.1 %gather_fusion.6 = bf16[64,2,2,16,128]{4,3,2,1,0:T(8,128)(2,1)} fusion(bf16[512,2,2,16,128]{4,3,2,1,0:T(8,128)(2,1)} %param.12, s32[1024]{0:T(1024)S(1)} %pad_clamp_fusion.2), kind=kCustom, calls=%fused_computation.6 | custom fusion | bytes 2097408 | tf_op jit(solution)/shard_map/jit(_take)/gather | solution.py:146
  61.3 3.2 reshape.237
  68.8 4.1 gather_fusion.7
  73.0 4.8 %collective-permute-done = bf16[64,2,2,16,128]{4,3,2,1,0:T(8,128)(2,1)} collective-permute-done((bf16[64,2,2,16,128]{4,3,2,1,0:T(8,128)(2,1)}, bf16[64,2,2,16,128]{4,3,2,1,0:T(8,128)(2,1)}, u32[]{:S(2)}, u32[]{:S(2)}) %collective-permute-start) | collective-permute-done | bytes 1048608 | tf_op jit(solution)/shard_map/ppermute | solution.py:148
  77.7 11.0 %collective-permute-start.5 = (bf16[64,2,2,16,128]{4,3,2,1,0:T(8,128)(2,1)S(1)}, bf16[64,2,2,16,128]{4,3,2,1,0:T(8,128)(2,1)}, u32[]{:S(2)}, u32[]{:S(2)}) collective-permute-start(bf16[64,2,2,16,128]{4,3,2,1,0:T(8,128)(2,1)S(1)} %gather_fusion.7), channel_id=1, source_target_pairs={{0,24},{4,28},{8,0},{12,4},{16,8},{20,12},{24,16},{28,20},{1,25},{... | collective-permute-start | bytes 3145736 | tf_op jit(solution)/shard_map/ppermute | solution.py:148
  88.7 5.1 %gather_fusion.8 = bf16[64,2,2,16,128]{4,3,2,1,0:T(8,128)(2,1)} fusion(bf16[512,2,2,16,128]{4,3,2,1,0:T(8,128)(2,1)} %param.12, s32[1024]{0:T(1024)S(1)} %pad_clamp_fusion), kind=kCustom, calls=%fused_computation.8 | custom fusion | bytes 2097408 | tf_op jit(solution)/shard_map/jit(_take)/gather | solution.py:146
  93.8 29.2 %collective-permute-start.6 = (bf16[64,2,2,16,128]{4,3,2,1,0:T(8,128)(2,1)}, bf16[64,2,2,16,128]{4,3,2,1,0:T(8,128)(2,1)S(1)}, u32[]{:S(2)}, u32[]{:S(2)}) collective-permute-start(bf16[64,2,2,16,128]{4,3,2,1,0:T(8,128)(2,1)} %gather_fusion.8), channel_id=1, source_target_pairs={{0,28},{4,0},{8,4},{12,8},{16,12},{20,16},{24,20},{28,24},{1,29},{... | collective-permute-start | bytes 3145736 | tf_op jit(solution)/shard_map/ppermute | solution.py:148
  123.0 4.2 gather_fusion.1
  133.0 57.2 %collective-permute-done.2 = bf16[64,2,2,16,128]{4,3,2,1,0:T(8,128)(2,1)} collective-permute-done((bf16[64,2,2,16,128]{4,3,2,1,0:T(8,128)(2,1)}, bf16[64,2,2,16,128]{4,3,2,1,0:T(8,128)(2,1)}, u32[]{:S(2)}, u32[]{:S(2)}) %collective-permute-start.2) | collective-permute-done | bytes 1048608 | tf_op jit(solution)/shard_map/ppermute | solution.py:148
  199.6 23.9 %collective-permute-done.6 = bf16[64,2,2,16,128]{4,3,2,1,0:T(8,128)(2,1)S(1)} collective-permute-done((bf16[64,2,2,16,128]{4,3,2,1,0:T(8,128)(2,1)}, bf16[64,2,2,16,128]{4,3,2,1,0:T(8,128)(2,1)S(1)}, u32[]{:S(2)}, u32[]{:S(2)}) %collective-permute-start.6) | collective-permute-done | bytes 1048608 | tf_op jit(solution)/shard_map/ppermute | solution.py:148
  224.6 32.7 %shard_map.100 = bf16[2,4096,128]{2,1,0:T(8,128)(2,1)} custom-call(s32[512]{0:T(512)} %get-tuple-element.16.refs_0_, bf16[512,2,2,16,128]{4,3,2,1,0:T(8,128)(2,1)} %constant_dynamic-update-slice_fusion.refs_1_, bf16[2,4096,128]{2,1,0:T(8,128)(2,1)} %bitcast.66, bf16[2,2,512,128]{3,2,1,0:T(8,128)(2,1)} %bitcast.68, s32[32,1,384]{2,1,0:T(1,128)} %reshape.240.refs_4_), custom_call_target="tpu_custom_call" | custom-call | tf_op jit(solution)/shard_map/pallas_call | solution.py:93
  261.6 26.2 %fusion.2 = bf16[128,4,8192]{2,0,1:T(8,128)(2,1)} fusion(bf16[128,4,2048]{2,0,1:T(8,128)(2,1)} %dot_general.14, bf16[2048,8192]{1,0:T(8,128)(2,1)} %param.17), kind=kOutput, calls=%fused_computation.11 | convolution fusion | flops 17184063488 | bytes 44040192 | tf_op jit(solution)/shard_map/dot_general | solution.py:153
  290.7 5.2 %multiply_reduce_fusion = f32[128,4,64]{0,2,1:T(8,128)S(1)} fusion(bf16[16,64,2048]{2,1,0:T(8,128)(2,1)} %all-gather.3.cloned.1.call-done, bf16[128,4,2048,1]{2,0,1,3:T(8,128)(2,1)} %reshape.323, f32[128,16]{0,1:T(8,128)S(1)} %get-tuple-element.17), kind=kOutput, calls=%fused_computation.20 | convolution fusion | flops 2148499456 | bytes 6430720 | tf_op jit(solution)/shard_map/qsf,nrf->qsnr/dot_general | solution.py:163
  295.9 11.7 %all-reduce.1 = bf16[128,4,64]{0,2,1:T(8,128)(2,1)S(1)} all-reduce(f32[128,4,64]{0,2,1:T(8,128)S(1)} %multiply_reduce_fusion), channel_id=1, replica_groups=mesh['dp'=8,'mp'=4] {'mp'}, use_global_device_ids=true, to_apply=%region_5.6 | all-reduce | flops 32768 | bytes 196608 | tf_op jit(solution)/shard_map/psum | solution.py:167
  307.6 140.9 %reduce-scatter.2.cloned.1.call-done = bf16[128,4,2048]{2,0,1:T(8,128)(2,1)} async-done(((bf16[128,4,8192]{2,0,1:T(8,128)(2,1)}), bf16[128,4,2048]{2,0,1:T(8,128)(2,1)}) %reduce-scatter.2.cloned.1.call-update) | async-done | bytes 2097168 | tf_op jit(solution)/shard_map/reduce_scatter | solution.py:176
  448.5 5.4 %add_convert_fusion = bf16[128,4,2048]{2,0,1:T(8,128)(2,1)S(1)} fusion(bf16[128,4,2048]{2,0,1:T(8,128)(2,1)} %reduce-scatter.2.cloned.1.call-done, bf16[16,64,2048]{2,1,0:T(8,128)(2,1)} %all-gather.5.cloned.1.call-done, bf16[128,16]{0,1:T(8,128)(2,1)S(1)} %get-tuple-element.18, bf16[128,4,64]{0,2,1:T(8,128)(2,1)S(1)} %all-reduce.1), kind=kOutput, calls=%fused_computation.18 | convolution fusion | flops 2154299392 | bytes 8458240 | tf_op jit(solution)/shard_map/utja,jam->utm/dot_general | solution.py:172
  (69 shorter events, 40.3 us)
Async XLA Ops:
  7.4 2.5 copy-start
  7.4 283.3 %all-gather.3.cloned.1.call-start = ((), (), s32[]{:S(2)}) async-start(), calls=%async_computation.3 | async-start | bytes 4718592 | tf_op jit(solution)/shard_map/all_gather | solution.py:160
  8.1 299.5 %all-gather.5.cloned.1.call-start = ((), (), s32[]{:S(2)}) async-start(), calls=%async_computation.4 | async-start | bytes 4718592 | tf_op jit(solution)/shard_map/all_gather | solution.py:168
  15.5 13.7 %all-to-all-start = ((s32[8,1,64]{2,1,0:T(1,128)}), s32[8,1,64]{2,1,0:T(1,128)S(1)}, u32[]{:S(2)}, u32[]{:S(2)}) async-start(s32[8,1,64]{2,1,0:T(1,128)} %all_to_all.6), calls=%async_computation | async-start | bytes 8192 | tf_op jit(solution)/shard_map/all_to_all | solution.py:142
  22.7 425.8 %reduce-scatter.2.cloned.1.call-start = ((), (), s32[]{:S(2)}) async-start(), calls=%async_computation.2 | async-start | bytes 10485760 | tf_op jit(solution)/shard_map/reduce_scatter | solution.py:176
  34.3 43.4 %collective-permute-start = (bf16[64,2,2,16,128]{4,3,2,1,0:T(8,128)(2,1)}, bf16[64,2,2,16,128]{4,3,2,1,0:T(8,128)(2,1)}, u32[]{:S(2)}, u32[]{:S(2)}) collective-permute-start(bf16[64,2,2,16,128]{4,3,2,1,0:T(8,128)(2,1)} %gather_fusion.2), channel_id=1, source_target_pairs={{0,4},{4,8},{8,12},{12,16},{16,20},{20,24},{24,28},{28,0},{1,5},{5... | collective-permute-start | bytes 3145736 | tf_op jit(solution)/shard_map/ppermute | solution.py:148
  39.0 54.8 %collective-permute-start.1 = (bf16[64,2,2,16,128]{4,3,2,1,0:T(8,128)(2,1)S(1)}, bf16[64,2,2,16,128]{4,3,2,1,0:T(8,128)(2,1)}, u32[]{:S(2)}, u32[]{:S(2)}) collective-permute-start(bf16[64,2,2,16,128]{4,3,2,1,0:T(8,128)(2,1)S(1)} %gather_fusion.3), channel_id=1, source_target_pairs={{0,8},{4,12},{8,16},{12,20},{16,24},{20,28},{24,0},{28,4},{1,9},{5... | collective-permute-start | bytes 3145736 | tf_op jit(solution)/shard_map/ppermute | solution.py:148
  46.5 143.7 %collective-permute-start.2 = (bf16[64,2,2,16,128]{4,3,2,1,0:T(8,128)(2,1)}, bf16[64,2,2,16,128]{4,3,2,1,0:T(8,128)(2,1)}, u32[]{:S(2)}, u32[]{:S(2)}) collective-permute-start(bf16[64,2,2,16,128]{4,3,2,1,0:T(8,128)(2,1)} %gather_fusion.4), channel_id=1, source_target_pairs={{0,12},{4,16},{8,20},{12,24},{16,28},{20,0},{24,4},{28,8},{1,13},{... | collective-permute-start | bytes 3145736 | tf_op jit(solution)/shard_map/ppermute | solution.py:148
  53.0 139.5 %collective-permute-start.3 = (bf16[64,2,2,16,128]{4,3,2,1,0:T(8,128)(2,1)}, bf16[64,2,2,16,128]{4,3,2,1,0:T(8,128)(2,1)}, u32[]{:S(2)}, u32[]{:S(2)}) collective-permute-start(bf16[64,2,2,16,128]{4,3,2,1,0:T(8,128)(2,1)} %gather_fusion.5), channel_id=1, source_target_pairs={{0,16},{4,20},{8,24},{12,28},{16,0},{20,4},{24,8},{28,12},{1,17},{... | collective-permute-start | bytes 3145736 | tf_op jit(solution)/shard_map/ppermute | solution.py:148
  61.3 133.6 %collective-permute-start.4 = (bf16[64,2,2,16,128]{4,3,2,1,0:T(8,128)(2,1)}, bf16[64,2,2,16,128]{4,3,2,1,0:T(8,128)(2,1)}, u32[]{:S(2)}, u32[]{:S(2)}) collective-permute-start(bf16[64,2,2,16,128]{4,3,2,1,0:T(8,128)(2,1)} %gather_fusion.6), channel_id=1, source_target_pairs={{0,20},{4,24},{8,28},{12,0},{16,4},{20,8},{24,12},{28,16},{1,21},{... | collective-permute-start | bytes 3145736 | tf_op jit(solution)/shard_map/ppermute | solution.py:148
  77.7 119.5 %collective-permute-start.5 = (bf16[64,2,2,16,128]{4,3,2,1,0:T(8,128)(2,1)S(1)}, bf16[64,2,2,16,128]{4,3,2,1,0:T(8,128)(2,1)}, u32[]{:S(2)}, u32[]{:S(2)}) collective-permute-start(bf16[64,2,2,16,128]{4,3,2,1,0:T(8,128)(2,1)S(1)} %gather_fusion.7), channel_id=1, source_target_pairs={{0,24},{4,28},{8,0},{12,4},{16,8},{20,12},{24,16},{28,20},{1,25},{... | collective-permute-start | bytes 3145736 | tf_op jit(solution)/shard_map/ppermute | solution.py:148
  93.8 129.6 %collective-permute-start.6 = (bf16[64,2,2,16,128]{4,3,2,1,0:T(8,128)(2,1)}, bf16[64,2,2,16,128]{4,3,2,1,0:T(8,128)(2,1)S(1)}, u32[]{:S(2)}, u32[]{:S(2)}) collective-permute-start(bf16[64,2,2,16,128]{4,3,2,1,0:T(8,128)(2,1)} %gather_fusion.8), channel_id=1, source_target_pairs={{0,28},{4,0},{8,4},{12,8},{16,12},{20,16},{24,20},{28,24},{1,29},{... | collective-permute-start | bytes 3145736 | tf_op jit(solution)/shard_map/ppermute | solution.py:148
  287.7 0.7 copy-start.2
  290.7 166.2 %copy-start.1 = (s32[4096]{0:T(1024)S(1)}, s32[4096]{0:T(1024)}, u32[]{:S(2)}) copy-start(s32[4096]{0:T(1024)} %param.13) | copy-start | bytes 49156
Sparse Core Ops, SparseCore 0:
  10.5 173.4 all-gather.2
  186.4 108.6 all-gather.4
Sparse Core Ops, SparseCore 1:
  287.8 160.6 reduce-scatter.1

commit v12 on v9

--- a/solution.py
+++ b/solution.py
@@ -165,13 +165,21 @@
     )
     rank_part = jnp.einsum("qsnr,qn->qsr", every_rank, hit_mask)
     rank_sum = lax.psum(rank_part, "mp").astype(jnp.bfloat16)
-    single_panel = lax.all_gather(adapter_up_panels, "dp", axis=0, tiled=True)
-    panel_count = single_panel.shape[0]
-    hit_mask = (adapter[:, None] == jnp.arange(panel_count)[None, :]).astype(jnp.bfloat16)
-    selected_panel = rank_sum[:, :, None, :] * hit_mask[:, None, :, None]
-    adapter_sum = jnp.einsum(
-        "utja,jam->utm", selected_panel, single_panel, preferred_element_type=jnp.float32
-    )
+    local_adapters = adapter_up_panels.shape[0]
+    adapter_sum = 0.0
+    for low, width in ((0, 1), (1, local_adapters - 1)):
+        if width == 0:
+            continue
+        panel = lax.all_gather(adapter_up_panels[low:low + width], "dp", axis=0, tiled=True)
+        panel_ids = jnp.arange(panel.shape[0])
+        hit_mask = (
+            (adapter[:, None] // local_adapters == (panel_ids // width)[None, :])
+            & (adapter[:, None] % local_adapters == (low + panel_ids % width)[None, :])
+        ).astype(jnp.bfloat16)
+        selected_panel = rank_sum[:, :, None, :] * hit_mask[:, None, :, None]
+        adapter_sum = adapter_sum + jnp.einsum(
+            "utja,jam->utm", selected_panel, panel, preferred_element_type=jnp.float32
+        )
     adapter_output = (adapter_sum * ADAPTER_SCALE).astype(jnp.bfloat16)
     summed_output = lax.psum_scatter(
         base_product.astype(jnp.bfloat16), "mp", scatter_dimension=2, tiled=True

time: 403 us -> 428 us (1.062)
  waiting for transfers between devices: 55.6 us -> 75.1 us
  matrix products: 37.4 us -> 41.7 us
    all_gather x1 -> x2, waiting for transfers between devices: 54.8 us -> 75 us  [shards(): lax.all_gather(adapter_up_panels[low:low + width], 'dp', axis=0, tiled=True)]
    dot_general x1 -> x2, matrix products: 5.38 us -> 9.79 us  [shards(): jnp.einsum('utja,jam->utm', selected_panel, panel, preferred_element_type...]
  transfers between devices with their start and end apart: 3 -> 4, of which waited for: 1 -> 2; matrix products, arithmetic and copies ran while one was open for 11% -> 12% of each run, Pallas kernels for 8% -> 8%
where the time goes in v12:
time: 428 us; the launch traced here: 427 us
  blocking collectives  214 us (50%)
  waiting for transfers between devices  75.1 us (18%)
  local copies, waits for them, and re-layouts  45.6 us (11%)
  matrix products  41.7 us (10%)
  Pallas kernels  32.8 us (8%)
  between operations  14.8 us (3%)
    all_to_all x1, blocking collectives, shards(): lax.all_to_all(served, 'dp', split_axis=0, concat_axis=0, tiled=True)  188 us
    all_gather x2, waiting for transfers between devices, shards(): lax.all_gather(adapter_up_panels[low:low + width], 'dp', axis=0, tiled=True)  75 us
    pallas_call x1, Pallas kernels, attend(): pl.pallas_call(body, grid_spec=grid_spec, out_shape=jax.ShapeDtypeStruct(...  32.8 us
    dot_general x1, matrix products, shards(): jnp.dot(attended.reshape(req_dev * step_count, query_width), output_weigh...  26.1 us
    gather x1, local copies, waits for them, and re-layouts, shards(): jnp.take(key_value_pool, wanted.reshape(-1), axis=0, mode='clip')  22.9 us
    all_to_all x1, blocking collectives, shards(): lax.all_to_all(wish_table, 'dp', split_axis=0, concat_axis=0, tiled=True)  13.5 us
    psum x1, blocking collectives, shards(): rank_sum = lax.psum(rank_part, 'mp').astype(jnp.bfloat16)  12.6 us
    dot_general x2, matrix products, shards(): jnp.einsum('utja,jam->utm', selected_panel, panel, preferred_element_type...  9.79 us
  transfers between devices with their start and end apart: 4, of which 2 were waited for; matrix products, arithmetic and copies ran while one was open for 12% of the time, Pallas kernels for 8%

profile of v12, /device:TPU:0, one launch (start us, length us, event | category | flops | bytes accessed | tf_op | source)
XLA Modules:
  0.0 426.8 jit_solution(15777495433223835797)
XLA Ops:
  7.4 0.8 copy.27
  8.4 3.1 gather_fusion
  13.4 13.5 %all_to_all.14 = s32[8,1,64]{2,1,0:T(1,128)S(1)} all-to-all(s32[8,1,64]{2,1,0:T(1,128)S(1)} %all_to_all.9), channel_id=1, replica_groups=mesh['dp'=8,'mp'=4] {'dp'}, dimensions={0} | all-to-all | bytes 4096 | tf_op jit(solution)/shard_map/all_to_all | solution.py:142
  27.4 0.7 reduce.5
  28.2 22.9 %gather_fusion.1 = bf16[512,2,2,16,128]{4,3,2,1,0:T(8,128)(2,1)} fusion(bf16[512,2,2,16,128]{4,3,2,1,0:T(8,128)(2,1)} %param.12, s32[1024]{0:T(1024)S(1)} %pad_clamp_fusion), kind=kCustom, calls=%fused_computation.1 | custom fusion | bytes 16779264 | tf_op jit(solution)/shard_map/jit(_take)/gather | solution.py:143
  51.1 187.8 %all_to_all.15 = bf16[8,64,2,2,16,128]{5,4,3,2,1,0:T(8,128)(2,1)} all-to-all(bf16[8,64,2,2,16,128]{5,4,3,2,1,0:T(8,128)(2,1)} %bitcast.65), channel_id=1, replica_groups=mesh['dp'=8,'mp'=4] {'dp'}, dimensions={0} | all-to-all | bytes 16777216 | tf_op jit(solution)/shard_map/all_to_all | solution.py:146
  238.9 0.8 fusion.33
  239.8 3.2 reshape.295
  243.0 1.7 copy.29
  244.7 1.0 copy.30
  246.2 0.6 reshape.298.refs_4_
  246.8 32.8 %shard_map.100 = bf16[2,4096,128]{2,1,0:T(8,128)(2,1)} custom-call(s32[512]{0:T(512)} %get-tuple-element.18.refs_0_, bf16[512,2,2,16,128]{4,3,2,1,0:T(8,128)(2,1)} %bitcast.64, bf16[2,4096,128]{2,1,0:T(8,128)(2,1)} %bitcast.66, bf16[2,2,512,128]{3,2,1,0:T(8,128)(2,1)} %bitcast.68, s32[32,1,384]{2,1,0:T(1,128)} %reshape.298.refs_4_), custom_call_target="tpu_custom_call" | custom-call | tf_op jit(solution)/shard_map/pallas_call | solution.py:93
  279.6 2.0 copy.31
  281.5 2.3 dot_general.17
  284.1 26.1 %fusion.2 = bf16[128,4,8192]{2,0,1:T(8,128)(2,1)} fusion(bf16[128,4,2048]{2,0,1:T(8,128)(2,1)} %dot_general.17, bf16[2048,8192]{1,0:T(8,128)(2,1)} %param.17), kind=kOutput, calls=%fused_computation.4 | convolution fusion | flops 17184063488 | bytes 44040192 | tf_op jit(solution)/shard_map/dot_general | solution.py:153
  310.2 0.6 copy-done.4
  311.0 2.3 reshape.318
  313.3 5.9 %multiply_reduce_fusion = f32[128,4,64]{0,2,1:T(8,128)S(1)} fusion(bf16[16,64,2048]{2,1,0:T(8,128)(2,1)} %all-gather.4.cloned.1.call-done, bf16[128,4,2048,1]{2,0,1,3:T(8,128)(2,1)} %reshape.318, f32[128,16]{0,1:T(8,128)S(1)} %copy.42), kind=kOutput, calls=%fused_computation.15 | convolution fusion | flops 2148499456 | bytes 6430720 | tf_op jit(solution)/shard_map/qsf,nrf->qsnr/dot_general | solution.py:163
  319.2 12.6 %all-reduce.1 = bf16[128,4,64]{0,2,1:T(8,128)(2,1)S(1)} all-reduce(f32[128,4,64]{0,2,1:T(8,128)S(1)} %multiply_reduce_fusion), channel_id=1, replica_groups=mesh['dp'=8,'mp'=4] {'mp'}, use_global_device_ids=true, to_apply=%region_5.6 | all-reduce | flops 32768 | bytes 196608 | tf_op jit(solution)/shard_map/psum | solution.py:167
  331.8 29.7 %all-gather.6.cloned.1.call-done = bf16[8,64,2048]{2,1,0:T(8,128)(2,1)} async-done(((bf16[1,64,2048]{2,1,0:T(8,128)(2,1)}), bf16[8,64,2048]{2,1,0:T(8,128)(2,1)}) %all-gather.6.cloned.1.call-update) | async-done | bytes 2097168 | tf_op jit(solution)/shard_map/all_gather | solution.py:173
  361.6 4.8 %fusion.10 = f32[128,4,2048,1]{2,0,3,1:T(8,128)} fusion(bf16[8,64,2048]{2,1,0:T(8,128)(2,1)} %all-gather.6.cloned.1.call-done, bf16[128,8]{0,1:T(8,128)(2,1)S(1)} %get-tuple-element.20, bf16[128,4,64]{0,2,1:T(8,128)(2,1)S(1)} %all-reduce.1), kind=kOutput, calls=%fused_computation.12 | convolution fusion | flops 1074003968 | bytes 6359040 | tf_op jit(solution)/shard_map/utja,jam->utm/dot_general | solution.py:180
  366.4 45.3 %all-gather.8.cloned.1.call-done = bf16[8,64,2048]{2,1,0:T(8,128)(2,1)} async-done(((bf16[1,64,2048]{2,1,0:T(8,128)(2,1)}), bf16[8,64,2048]{2,1,0:T(8,128)(2,1)}) %all-gather.8.cloned.1.call-update) | async-done | bytes 2097168 | tf_op jit(solution)/shard_map/all_gather | solution.py:173
  411.7 4.9 %add_convert_fusion = bf16[128,4,2048]{2,0,1:T(8,128)(2,1)S(1)} fusion(bf16[128,4,2048]{2,0,1:T(8,128)(2,1)} %reduce-scatter.2.cloned.1.call-done, f32[128,4,2048,1]{2,0,3,1:T(8,128)} %fusion.10, bf16[8,64,2048]{2,1,0:T(8,128)(2,1)} %all-gather.8.cloned.1.call-done, bf16[128,8]{0,1:T(8,128)(2,1)S(1)} %get-tuple-element.19, ...), kind=kOutput, calls=%fused_computation.10 | convolution fusion | flops 1081344000 | bytes 10553344 | tf_op jit(solution)/shard_map/utja,jam->utm/dot_general | solution.py:180
  416.7 2.9 copy.32
  (53 shorter events, 3.6 us)
Async XLA Ops:
  7.4 1.0 copy-start
  7.4 305.9 %all-gather.4.cloned.1.call-start = ((), (), s32[]{:S(2)}) async-start(), calls=%async_computation.4 | async-start | bytes 4718592 | tf_op jit(solution)/shard_map/all_gather | solution.py:160
  51.1 187.9 %copy-start.2 = (bf16[2,64,2048]{2,1,0:T(8,128)(2,1)S(1)}, bf16[2,64,2048]{2,1,0:T(8,128)(2,1)}, u32[]{:S(2)}) copy-start(bf16[2,64,2048]{2,1,0:T(8,128)(2,1)} %param.19) | copy-start | bytes 1572868
  238.9 122.7 %all-gather.6.cloned.1.call-start = ((), (), s32[]{:S(2)}) async-start(), calls=%async_computation.5 | async-start | bytes 2359296 | tf_op jit(solution)/shard_map/all_gather | solution.py:173
  239.8 171.9 %all-gather.8.cloned.1.call-start = ((), (), s32[]{:S(2)}) async-start(), calls=%async_computation.6 | async-start | bytes 2359296 | tf_op jit(solution)/shard_map/all_gather | solution.py:173
  243.0 1.7 copy-start.3
  243.0 2.7 copy-start.5
  243.0 3.1 copy-start.6
  283.9 127.9 %reduce-scatter.2.cloned.1.call-start = ((), (), s32[]{:S(2)}) async-start(), calls=%async_computation.3 | async-start | bytes 10485760 | tf_op jit(solution)/shard_map/reduce_scatter | solution.py:184
  310.1 0.7 copy-start.4
  411.7 7.9 %copy-start.1 = (s32[4096]{0:T(1024)S(1)}, s32[4096]{0:T(1024)}, u32[]{:S(2)}) copy-start(s32[4096]{0:T(1024)} %param.13) | copy-start | bytes 49156
Sparse Core Ops, SparseCore 0:
  239.0 72.6 all-gather.3
  314.1 47.4 all-gather.5
  363.9 47.7 all-gather.7
Sparse Core Ops, SparseCore 1:
  310.3 71.0 reduce-scatter.1

commit v13 on v9

--- a/solution.py
+++ b/solution.py
@@ -139,7 +139,8 @@
     wish_table = jnp.sum(
         jnp.where(key[:, None] == table_ids[None, :], local_slot[:, None], 0), axis=0
     ).reshape(owners, capacity)
-    wanted = lax.all_to_all(wish_table, "dp", split_axis=0, concat_axis=0, tiled=True)
+    every_wish = lax.all_gather(wish_table, "dp", axis=0)
+    wanted = jnp.take(every_wish, lax.axis_index("dp"), axis=1)
     served = jnp.take(key_value_pool, wanted.reshape(-1), axis=0, mode="clip").reshape(
         (owners, capacity) + key_value_pool.shape[1:]
     )

time: 403 us -> 416 us (1.032)
  blocking collectives: 213 us -> 227 us
    all_gather x0 -> x1, blocking collectives: none -> 32.2 us  [shards(): every_wish = lax.all_gather(wish_table, 'dp', axis=0)]
    all_to_all x1 -> x0, blocking collectives: 13.5 us -> none  [shards(): lax.all_to_all(wish_table, 'dp', split_axis=0, concat_axis=0, tiled=True)]
    all_to_all x1, blocking collectives: 188 us -> 183 us  [shards(): lax.all_to_all(served, 'dp', split_axis=0, concat_axis=0, tiled=True)]
where the time goes in v13:
time: 416 us; the launch traced here: 414 us
  blocking collectives  227 us (55%)
  waiting for transfers between devices  55.7 us (13%)
  local copies, waits for them, and re-layouts  44.2 us (11%)
  matrix products  37.4 us (9%)
  Pallas kernels  32.7 us (8%)
  between operations  15 us (4%)
    all_to_all x1, blocking collectives, shards(): lax.all_to_all(served, 'dp', split_axis=0, concat_axis=0, tiled=True)  183 us
    all_gather x1, waiting for transfers between devices, shards(): single_panel = lax.all_gather(adapter_up_panels, 'dp', axis=0, tiled=True)  55 us
    pallas_call x1, Pallas kernels, attend(): pl.pallas_call(body, grid_spec=grid_spec, out_shape=jax.ShapeDtypeStruct(...  32.7 us
    all_gather x1, blocking collectives, shards(): every_wish = lax.all_gather(wish_table, 'dp', axis=0)  32.2 us
    dot_general x1, matrix products, shards(): jnp.dot(attended.reshape(req_dev * step_count, query_width), output_weigh...  26.1 us
    gather x1, local copies, waits for them, and re-layouts, shards(): jnp.take(key_value_pool, wanted.reshape(-1), axis=0, mode='clip')  22.9 us
    psum x1, blocking collectives, shards(): rank_sum = lax.psum(rank_part, 'mp').astype(jnp.bfloat16)  12.1 us
  transfers between devices with their start and end apart: 3, of which 1 were waited for; matrix products, arithmetic and copies ran while one was open for 11% of the time, Pallas kernels for 8%

profile of v13, /device:TPU:0, one launch (start us, length us, event | category | flops | bytes accessed | tf_op | source)
XLA Modules:
  0.0 414.1 jit_solution(10719050263069694052)
XLA Ops:
  7.4 0.8 copy.27
  8.4 3.1 gather_fusion
  11.9 0.3 convert_reduce_fusion
  12.1 0.4 select_reduce_fusion.1
  12.5 0.6 add_select_fusion.2
  13.4 32.2 %all_gather.9 = s32[8,8,64]{2,1,0:T(8,128)S(1)} all-gather(s32[1,8,64]{2,1,0:T(8,128)S(1)} %all_gather_reshape.3), channel_id=1, replica_groups=mesh['dp'=8,'mp'=4] {'dp'}, dimensions={0}, use_global_device_ids=true | all-gather | bytes 18432 | tf_op jit(solution)/shard_map/all_gather | solution.py:142
  45.7 22.9 %gather_fusion.1 = bf16[512,2,2,16,128]{4,3,2,1,0:T(8,128)(2,1)} fusion(bf16[512,2,2,16,128]{4,3,2,1,0:T(8,128)(2,1)} %param.12, s32[1024]{0:T(1024)S(1)} %pad_clamp_fusion), kind=kCustom, calls=%fused_computation.1 | custom fusion | bytes 16779264 | tf_op jit(solution)/shard_map/jit(_take)/gather | solution.py:144
  68.6 182.7 %all_to_all.5 = bf16[8,64,2,2,16,128]{5,4,3,2,1,0:T(8,128)(2,1)} all-to-all(bf16[8,64,2,2,16,128]{5,4,3,2,1,0:T(8,128)(2,1)} %bitcast.53), channel_id=1, replica_groups=mesh['dp'=8,'mp'=4] {'dp'}, dimensions={0} | all-to-all | bytes 16777216 | tf_op jit(solution)/shard_map/all_to_all | solution.py:147
  251.4 0.7 all-gather.5.cloned.1.call-update
  252.3 3.2 reshape.233
  255.5 1.7 copy.29
  257.2 1.0 copy.30
  258.6 0.6 reshape.236.refs_4_
  259.3 32.7 %shard_map.100 = bf16[2,4096,128]{2,1,0:T(8,128)(2,1)} custom-call(s32[512]{0:T(512)} %get-tuple-element.25.refs_0_, bf16[512,2,2,16,128]{4,3,2,1,0:T(8,128)(2,1)} %bitcast.52, bf16[2,4096,128]{2,1,0:T(8,128)(2,1)} %bitcast.54, bf16[2,2,512,128]{3,2,1,0:T(8,128)(2,1)} %bitcast.56, s32[32,1,384]{2,1,0:T(1,128)} %reshape.236.refs_4_), custom_call_target="tpu_custom_call" | custom-call | tf_op jit(solution)/shard_map/pallas_call | solution.py:93
  292.0 2.0 copy.31
  294.0 2.3 dot_general.14
  296.3 26.1 %fusion.2 = bf16[128,4,8192]{2,0,1:T(8,128)(2,1)} fusion(bf16[128,4,2048]{2,0,1:T(8,128)(2,1)} %dot_general.14, bf16[2048,8192]{1,0:T(8,128)(2,1)} %param.17), kind=kOutput, calls=%fused_computation.4 | convolution fusion | flops 17184063488 | bytes 44040192 | tf_op jit(solution)/shard_map/dot_general | solution.py:154
  322.4 0.6 copy-done.4
  323.0 2.3 reshape.294
  325.3 5.9 %multiply_reduce_fusion = f32[128,4,64]{0,2,1:T(8,128)S(1)} fusion(bf16[16,64,2048]{2,1,0:T(8,128)(2,1)} %all-gather.3.cloned.1.call-done, bf16[128,4,2048,1]{2,0,1,3:T(8,128)(2,1)} %reshape.294, f32[128,16]{0,1:T(8,128)S(1)} %get-tuple-element.26), kind=kOutput, calls=%fused_computation.13 | convolution fusion | flops 2148499456 | bytes 6430720 | tf_op jit(solution)/shard_map/qsf,nrf->qsnr/dot_general | solution.py:164
  331.2 12.1 %all-reduce.1 = bf16[128,4,64]{0,2,1:T(8,128)(2,1)S(1)} all-reduce(f32[128,4,64]{0,2,1:T(8,128)S(1)} %multiply_reduce_fusion), channel_id=1, replica_groups=mesh['dp'=8,'mp'=4] {'mp'}, use_global_device_ids=true, to_apply=%region_5.6 | all-reduce | flops 32768 | bytes 196608 | tf_op jit(solution)/shard_map/psum | solution.py:168
  343.3 55.0 %all-gather.5.cloned.1.call-done = bf16[16,64,2048]{2,1,0:T(8,128)(2,1)} async-done(((bf16[2,64,2048]{2,1,0:T(8,128)(2,1)}), bf16[16,64,2048]{2,1,0:T(8,128)(2,1)}) %all-gather.5.cloned.1.call-update) | async-done | bytes 4194320 | tf_op jit(solution)/shard_map/all_gather | solution.py:169
  398.3 5.4 %add_convert_fusion = bf16[128,4,2048]{2,0,1:T(8,128)(2,1)S(1)} fusion(bf16[128,4,2048]{2,0,1:T(8,128)(2,1)} %reduce-scatter.2.cloned.1.call-done, bf16[16,64,2048]{2,1,0:T(8,128)(2,1)} %all-gather.5.cloned.1.call-done, bf16[128,16]{0,1:T(8,128)(2,1)S(1)} %get-tuple-element.27, bf16[128,4,64]{0,2,1:T(8,128)(2,1)S(1)} %all-reduce.1), kind=kOutput, calls=%fused_computation.11 | convolution fusion | flops 2154299392 | bytes 8458240 | tf_op jit(solution)/shard_map/utja,jam->utm/dot_general | solution.py:173
  403.7 2.9 copy.32
  (40 shorter events, 1.6 us)
Async XLA Ops:
  7.4 1.0 copy-start
  7.4 317.9 %all-gather.3.cloned.1.call-start = ((), (), s32[]{:S(2)}) async-start(), calls=%async_computation.3 | async-start | bytes 4718592 | tf_op jit(solution)/shard_map/all_gather | solution.py:161
  251.3 147.0 %all-gather.5.cloned.1.call-start = ((), (), s32[]{:S(2)}) async-start(), calls=%async_computation.4 | async-start | bytes 4718592 | tf_op jit(solution)/shard_map/all_gather | solution.py:169
  252.1 5.1 %copy-start.2 = (bf16[128,4,2,2,128]{4,3,2,1,0:T(2,128)(2,1)S(1)}, bf16[128,4,2,2,128]{4,3,2,1,0:T(2,128)(2,1)}, u32[]{:S(2)}) copy-start(bf16[128,4,2,2,128]{4,3,2,1,0:T(2,128)(2,1)} %param.11) | copy-start | bytes 1572868
  252.1 6.1 %copy-start.3 = (s32[128]{0:T(128)S(1)}, s32[128]{0:T(128)}, u32[]{:S(2)}) copy-start(s32[128]{0:T(128)} %param.15) | copy-start | bytes 1540
  252.1 6.5 %copy-start.5 = (s32[128]{0:T(128)S(1)}, s32[128]{0:T(128)}, u32[]{:S(2)}) copy-start(s32[128]{0:T(128)} %constant.73.clone.1) | copy-start | bytes 1540
  252.1 146.2 %reduce-scatter.2.cloned.1.call-start = ((), (), s32[]{:S(2)}) async-start(), calls=%async_computation.2 | async-start | bytes 10485760 | tf_op jit(solution)/shard_map/reduce_scatter | solution.py:177
  322.4 0.7 copy-start.4
  398.3 8.3 %copy-start.1 = (s32[4096]{0:T(1024)S(1)}, s32[4096]{0:T(1024)}, u32[]{:S(2)}) copy-start(s32[4096]{0:T(1024)} %param.13) | copy-start | bytes 49156
Sparse Core Ops, SparseCore 0:
  251.4 72.8 all-gather.2
  326.6 71.5 all-gather.4
Sparse Core Ops, SparseCore 1:
  322.5 71.0 reduce-scatter.1
